TPU v7x, 128 devices: a whole 4x4x4 slice. The times are simulated.
128 devices in a mesh: section: 2 (over core), seq: 64 (over z, x, y).
Axes of the slice: x: 4, y: 4, z: 4, core: 2. Of those that a mesh axis runs over, the one named last changes fastest.
Arguments:
- patches: bfloat16 [32768, 1408], P('seq'), may hold values from -42 to 42
- image_grid: int32 [256, 2], P('seq'), may hold values from 2 to 52, as said below
- image_offsets: int32 [256], P('seq'), may hold values from 0 to 32736, as said below
- dest_positions: int32 [8192], replicated, may hold values from 0 to 16383, as said below
- text_embeds: bfloat16 [256, 64, 1408], P(None, 'seq'), may hold values from -42 to 42
- segment_ids: int32 [256, 64], replicated, may hold values from 0 to 3, as said below
- vision_qkv: bfloat16 [1408, 3, 1408], P(None, None, 'section'), may hold values from -0.15625 to 0.15625
- vision_out: bfloat16 [1408, 1408], P('section'), may hold values from -0.875 to 0.875
- projector: bfloat16 [4, 1408, 1408], P('section'), may hold values from -0.078125 to 0.078125
- decoder_q: bfloat16 [1408, 1408], P(None, 'section'), may hold values from -0.15625 to 0.15625
- decoder_kv: bfloat16 [1408, 2, 176], P(None, None, 'section'), may hold values from -0.15625 to 0.15625
- decoder_out: bfloat16 [1408, 1408], P('section'), may hold values from -0.875 to 0.875
Outputs:
- decoded: bfloat16 [256, 64, 1408], P(None, 'seq')
Inputs may be any that keep to these rules, and one draw needn't show every extreme that they name: `image_grid`: patch rows and columns are even, columns are 8 or 16; the images of one index of seq lie back to back and cover exactly its 512 patches. `image_offsets`: each image's first patch; images are in order, back to back, the first of an index of seq at its first patch. `dest_positions`: the 128 merged rows of one index of seq go, in order, to 128 consecutive prompt positions; the ranges of different indices do not meet. `segment_ids`: never falls along prompt positions; every document number is used.
All inputs are finite; a program needn't handle non-finite values.
Results may differ from a plain program's by a relative error of at most 0.025.
Values may be sent and summed in bfloat16 or wider, within the bound.
No kernel may reach another device: no remote copies, remote signals or barrier semaphores. Data moves between devices by JAX's collectives and lax.ppermute only.
A program may use at most 128 MiB of HBM per device.

v0:
```python
import math

import jax
import jax.numpy as jnp
from jax import lax
from jax.sharding import PartitionSpec as P

D = 1408
HEAD = 88


def layer_norm(values):
    values = values.astype(jnp.float32)
    centred = values - jnp.mean(values, -1, keepdims=True)
    return centred * lax.rsqrt(jnp.mean(centred * centred, -1, keepdims=True) + 1e-06)


def root_norm(values):
    values = values.astype(jnp.float32)
    return values * lax.rsqrt(jnp.mean(values * values, -1, keepdims=True) + 1e-06)


def merge_rows(grid, offsets, count):
    heights = grid[:, 0]
    widths = grid[:, 1]
    group_start = offsets // 4
    group_count = heights * widths // 4
    merged_ids = jnp.arange(count, dtype=jnp.int32)
    inside = (
        (merged_ids[:, None] >= group_start[None, :])
        & (merged_ids[:, None] < (group_start + group_count)[None, :])
    ).astype(jnp.int32)
    first_group = jnp.sum(inside * group_start[None, :], 1)
    first_patch = jnp.sum(inside * offsets[None, :], 1)
    row_width = jnp.sum(inside * widths[None, :], 1)
    within = merged_ids - first_group
    groups_across = row_width // 2
    group_row = within // groups_across
    group_col = within % groups_across
    corner = first_patch + 2 * group_row * row_width + 2 * group_col
    return jnp.stack([corner, corner + 1, corner + row_width, corner + row_width + 1], 1)


def body(
    patches,
    image_grid,
    image_offsets,
    dest_positions,
    text_embeds,
    segment_ids,
    vision_qkv,
    vision_out,
    projector,
    decoder_q,
    decoder_kv,
    decoder_out,
):
    section_index = lax.axis_index("section")
    seq_index = lax.axis_index("seq")
    seq_count = lax.axis_size("seq")
    scale = 3.0 / math.sqrt(HEAD)
    patch_count = patches.shape[0]
    local_heads = vision_out.shape[0] // HEAD
    merged_count = patch_count // 4
    normed = layer_norm(patches).astype(jnp.bfloat16)
    mixed = jnp.dot(normed, vision_qkv.reshape(D, -1), preferred_element_type=jnp.float32).reshape(
        patch_count, 3, local_heads, HEAD
    )
    queries = root_norm(mixed[:, 0]).astype(jnp.bfloat16)
    keys = root_norm(mixed[:, 1]).astype(jnp.bfloat16)
    values = mixed[:, 2].astype(jnp.bfloat16)
    offsets = image_offsets - seq_index * patch_count
    image_of = jnp.sum(
        (jnp.arange(patch_count, dtype=jnp.int32)[:, None] >= offsets[None, :]).astype(jnp.int32), 1
    )
    query_block = math.gcd(patch_count, 512)

    def vision_block(first):
        scores = (
            jnp.einsum("qhd,khd->hqk", queries, keys, preferred_element_type=jnp.float32) * scale
        )
        same = (image_of[:, None] == image_of[None, :])[None]
        weights = jnp.where(same, jnp.exp(scores), jnp.zeros_like(scores))
        totals = jnp.sum(weights, -1)
        mixed_values = jnp.einsum(
            "hqk,khd->qhd", weights.astype(jnp.bfloat16), values, preferred_element_type=jnp.float32
        )
        return (
            (mixed_values / jnp.transpose(totals)[:, :, None])
            .astype(jnp.bfloat16)
            .reshape(query_block, local_heads * HEAD)
        )

    attended = lax.map(
        vision_block, jnp.arange(patch_count // query_block, dtype=jnp.int32) * query_block
    )
    attended = attended.reshape(patch_count, local_heads * HEAD)
    picks = merge_rows(image_grid, offsets, merged_count)
    own_picks = lax.dynamic_slice_in_dim(picks, 2 * section_index, 2, 1).reshape(-1)
    head_terms = jnp.dot(attended, vision_out, preferred_element_type=jnp.float32)
    vision = (patches.astype(jnp.float32) + lax.psum(head_terms, "section")).astype(jnp.bfloat16)
    kept = vision[own_picks]
    merge_terms = jnp.dot(
        kept.reshape(merged_count, 2 * D),
        projector.reshape(2 * D, D),
        preferred_element_type=jnp.float32,
    )
    per_peer = merged_count // seq_count
    run_starts = dest_positions.reshape(seq_count, merged_count)[:, 0]
    own_start = run_starts[seq_index]
    image_rows = lax.psum(merge_terms, "section").astype(jnp.bfloat16)
    received = lax.all_to_all(
        jnp.roll(image_rows.reshape(per_peer, seq_count, image_rows.shape[1]), own_start, axis=1),
        "seq",
        split_axis=1,
        concat_axis=1,
        tiled=True,
    )
    slot_base = jnp.arange(per_peer, dtype=jnp.int32)[:, None] * seq_count
    landing = (
        run_starts[None, :] + slot_base + (seq_index - run_starts[None, :]) % seq_count
    ) // seq_count
    text_rows = text_embeds.shape[0]
    prompt = text_embeds.reshape(text_rows, D).at[landing.reshape(-1)].set(received.reshape(-1, D))
    text_normed = root_norm(prompt).astype(jnp.bfloat16)
    kv_local = decoder_kv.shape[2] // HEAD
    group = local_heads // kv_local
    text_queries = root_norm(
        jnp.dot(text_normed, decoder_q, preferred_element_type=jnp.float32).reshape(
            text_rows, local_heads, HEAD
        )
    )
    text_queries = text_queries.astype(jnp.bfloat16).reshape(text_rows, kv_local, group, HEAD)
    paired = jnp.dot(
        text_normed, decoder_kv.reshape(D, -1), preferred_element_type=jnp.float32
    ).reshape(text_rows, 2, kv_local, HEAD)
    key_rows = root_norm(paired[:, 0]).astype(jnp.bfloat16)
    value_rows = paired[:, 1].astype(jnp.bfloat16)
    shared = jnp.stack([key_rows, value_rows], 1)[None]
    query_places = jnp.arange(text_rows, dtype=jnp.int32) * seq_count + seq_index
    query_segments = lax.dynamic_slice_in_dim(segment_ids, seq_index, 1, 1)[:, 0]
    start_state = (
        jnp.zeros((text_rows, kv_local, group, HEAD), jnp.float32),
        jnp.zeros((text_rows, kv_local, group), jnp.float32),
    )
    piece = lax.all_gather(shared, "seq", axis=0, tiled=True)
    shards = piece.shape[0]
    stride = math.gcd(shards, 8)
    blocks = shards // stride
    key_segments = jnp.transpose(segment_ids).reshape(blocks, stride * text_rows)
    shard_ids = jnp.arange(shards, dtype=jnp.int32)
    key_places = (
        jnp.arange(text_rows, dtype=jnp.int32)[None, :] * seq_count + shard_ids[:, None]
    ).reshape(blocks, stride * text_rows)
    grouped = piece.reshape(blocks, stride * text_rows, 2, kv_local, HEAD)

    def one_block(state, inputs):
        block_pair, block_places, block_segments = inputs
        scores = (
            jnp.einsum(
                "qkgd,lkd->qkgl", text_queries, block_pair[:, 0], preferred_element_type=jnp.float32
            )
            * scale
        )
        allowed = (block_places[None, :] <= query_places[:, None]) & (
            block_segments[None, :] == query_segments[:, None]
        )
        weights = jnp.where(allowed[:, None, None, :], jnp.exp(scores), jnp.zeros_like(scores))
        totals = state[1] + jnp.sum(weights, -1)
        sums = state[0] + jnp.einsum(
            "qkgl,lkd->qkgd",
            weights.astype(jnp.bfloat16),
            block_pair[:, 1],
            preferred_element_type=jnp.float32,
        )
        return ((sums, totals), None)

    result, unused = lax.scan(one_block, start_state, (grouped, key_places, key_segments))
    sums, totals = result
    attended_text = (
        (sums / totals[..., None]).astype(jnp.bfloat16).reshape(text_rows, local_heads * HEAD)
    )
    output_terms = jnp.dot(attended_text, decoder_out, preferred_element_type=jnp.float32)
    decoded = (prompt.astype(jnp.float32) + lax.psum(output_terms, "section")).astype(jnp.bfloat16)
    return decoded.reshape(text_rows, 1, D)


def solution(mesh):
    placed = (
        P("seq", None),
        P("seq", None),
        P("seq"),
        P(),
        P(None, "seq", None),
        P(),
        P(None, None, "section"),
        P("section", None),
        P("section", None, None),
        P(None, "section"),
        P(None, None, "section"),
        P("section", None),
    )
    return jax.shard_map(
        body, mesh=mesh, in_specs=placed, out_specs=P(None, "seq", None), check_vma=False
    )
```

profile of v0, /device:TPU:1, one launch (start us, length us, event | category | flops | bytes accessed | tf_op | source)
XLA Modules:
  0.0 298.4 jit_solution(1817690820470734248)
XLA Ops:
  7.5 1.7 convert_reduce_fusion
  9.9 6.0 %fusion.37 = f32[512,3,8,88]{0,3,2,1:T(8,128)S(1)} fusion(bf16[3,8,88,1408]{3,2,1,0:T(8,128)(2,1)} %bitcast.211, bf16[512,1408]{1,0:T(8,128)(2,1)S(1)} %copy-done.3, f32[512]{0:T(512)S(1)} %add_rsqrt_fusion.3, f32[512]{0:T(512)S(1)} %broadcast_multiply_fusion), kind=kOutput, calls=%fused_computation.47 | convolution fusion | flops 3047948288 | bytes 11718656 | tf_op jit(solution)/shard_map/dot_general | solution.py:66
  16.4 2.5 fusion.18
  18.9 1.8 divide_convert_fusion
  20.7 3.1 %fusion.66 = f32[512,1408]{1,0:T(8,128)} fusion(bf16[512,704]{0,1:T(8,128)(2,1)S(1)} %bitcast.203, bf16[704,1408]{1,0:T(8,128)(2,1)S(1)} %copy-done), kind=kOutput, calls=%fused_computation.146 | convolution fusion | flops 1015021568 | bytes 5586944 | tf_op jit(solution)/shard_map/dot_general | solution.py:100
  27.0 28.8 %all-reduce.4.cloned.1.call-done = f32[512,1408]{1,0:T(8,128)} async-done(((f32[512,1408]{1,0:T(8,128)}), f32[512,1408]{1,0:T(8,128)}) %all-reduce.4.cloned.1.call-update) | async-done | bytes 2883600 | tf_op jit(solution)/shard_map/psum | solution.py:101
  55.8 2.1 fusion.29
  57.9 1.3 gather_fusion
  59.5 4.5 %fusion.67 = f32[128,1408]{1,0:T(8,128)S(1)} fusion(bf16[128,2816]{1,0:T(8,128)(2,1)S(1)} %reshape.607, bf16[2816,1408]{1,0:T(8,128)(2,1)} %bitcast.193), kind=kOutput, calls=%fused_computation.147 | convolution fusion | flops 1015021568 | bytes 9371648 | tf_op jit(solution)/shard_map/dot_general | solution.py:103
  64.0 5.7 %all-reduce.7 = bf16[128,1408]{1,0:T(8,128)(2,1)S(1)} all-reduce(f32[128,1408]{1,0:T(8,128)S(1)} %fusion.67), channel_id=1, replica_groups=mesh['section'=2,'seq'=64] {'section'}, use_global_device_ids=true, to_apply=%region_10.11 | all-reduce | flops 180224 | bytes 1081344 | tf_op jit(solution)/shard_map/psum | solution.py:111
  70.1 1.7 fusion.51
  71.8 10.1 %all-to-all-start = ((bf16[2,64,1408]{2,0,1:T(2,128)(2,1)}), bf16[2,64,1408]{2,0,1:T(2,128)(2,1)S(1)}, u32[]{:S(2)}, u32[]{:S(2)}) async-start(bf16[2,64,1408]{2,0,1:T(2,128)(2,1)} %fusion.51), calls=%async_computation | async-start | bytes 720896 | tf_op jit(solution)/shard_map/all_to_all | solution.py:112
  82.1 10.5 %all-to-all-done = bf16[2,64,1408]{2,0,1:T(2,128)(2,1)S(1)} async-done(((bf16[2,64,1408]{2,0,1:T(2,128)(2,1)}), bf16[2,64,1408]{2,0,1:T(2,128)(2,1)S(1)}, u32[]{:S(2)}, u32[]{:S(2)}) %all-to-all-start) | async-done | bytes 360480 | tf_op jit(solution)/shard_map/all_to_all | solution.py:112
  92.7 1.6 scatter_fusion
  96.0 2.4 fusion.65
  98.5 76.8 %all-gather.3.cloned.1.call-done = bf16[16384,2,1,88]{0,3,1,2:T(8,128)(2,1)} async-done(((bf16[256,2,1,88]{0,3,1,2:T(8,128)(2,1)}), bf16[16384,2,1,88]{0,3,1,2:T(8,128)(2,1)}) %all-gather.3.cloned.1.call-update) | async-done | bytes 5767184 | tf_op jit(solution)/shard_map/all_gather | solution.py:146
  175.3 6.1 %copy.44 = bf16[1,2,11,8,8,2048]{5,4,2,1,0,3:T(8,128)(2,1)} copy(bf16[1,2,11,8,8,2048]{5,4,3,2,1,0:T(8,128)(2,1)} %bitcast.195) | data formatting | bytes 11534336 | tf_op jit(solution)/shard_map/reshape | solution.py:155
  181.4 76.3 %while.4 = (s32[]{:T(128)}, f32[256,1,8,88]{0,3,2,1:T(8,128)S(1)}, f32[256,1,8]{0,2,1:T(8,128)S(1)}, bf16[8,2048,2,1,88]{1,4,2,3,0:T(8,128)(2,1)}, s32[8,2048]{1...) while((s32[]{:T(128)}, f32[256,1,8,88]{0,3,2,1:T(8,128)S(1)}, ...), condition=%wide.region_17.18_spmd.clone, body=%wide.region_15.17_spmd.clone.sunk | while | flops 1503496704 | bytes 39177352 | solution.py:178
  181.5 1.4 compare_and_fusion.2
  184.1 3.9 %fusion.81 = (f32[256,8]{0,1:T(8,128)S(1)}, f32[2048,256,8]{1,0,2:T(8,128)S(1)}) fusion(pred[256,2048]{0,1:T(8,128)(4,1)S(1)} %compare_and_fusion.2, bf16[256,1,8,88]{0,3,2,1:T(8,128)(2,1)S(1)} %get-tuple-element.285, bf16[2048,2,1,88]{0,3,2,1:T(8,128)(2,1)S(1)} %dynamic-slice_bitcast_fusion.2), kind=kOutput, calls=%fused_computation.4.clone.1 | convolution fusion | flops 750778368 | bytes 18030592 | tf_op jit(solution)/shard_map/while/body/eval_jaxpr/qkgd,lkd->qkgl/dot_general | solution.py:160
  188.0 2.9 fusion.82
  191.0 1.4 compare_and_fusion.2
  193.7 3.9 %fusion.81 = (f32[256,8]{0,1:T(8,128)S(1)}, f32[2048,256,8]{1,0,2:T(8,128)S(1)}) fusion(pred[256,2048]{0,1:T(8,128)(4,1)S(1)} %compare_and_fusion.2, bf16[256,1,8,88]{0,3,2,1:T(8,128)(2,1)S(1)} %get-tuple-element.285, bf16[2048,2,1,88]{0,3,2,1:T(8,128)(2,1)S(1)} %dynamic-slice_bitcast_fusion.2), kind=kOutput, calls=%fused_computation.4.clone.1 | convolution fusion | flops 750778368 | bytes 18030592 | tf_op jit(solution)/shard_map/while/body/eval_jaxpr/qkgd,lkd->qkgl/dot_general | solution.py:160
  197.6 2.9 fusion.82
  200.6 1.4 compare_and_fusion.2
  203.2 3.9 %fusion.81 = (f32[256,8]{0,1:T(8,128)S(1)}, f32[2048,256,8]{1,0,2:T(8,128)S(1)}) fusion(pred[256,2048]{0,1:T(8,128)(4,1)S(1)} %compare_and_fusion.2, bf16[256,1,8,88]{0,3,2,1:T(8,128)(2,1)S(1)} %get-tuple-element.285, bf16[2048,2,1,88]{0,3,2,1:T(8,128)(2,1)S(1)} %dynamic-slice_bitcast_fusion.2), kind=kOutput, calls=%fused_computation.4.clone.1 | convolution fusion | flops 750778368 | bytes 18030592 | tf_op jit(solution)/shard_map/while/body/eval_jaxpr/qkgd,lkd->qkgl/dot_general | solution.py:160
  207.1 2.9 fusion.82
  210.1 1.4 compare_and_fusion.2
  211.6 1.2 dynamic-slice_bitcast_fusion.2
  212.8 3.9 %fusion.81 = (f32[256,8]{0,1:T(8,128)S(1)}, f32[2048,256,8]{1,0,2:T(8,128)S(1)}) fusion(pred[256,2048]{0,1:T(8,128)(4,1)S(1)} %compare_and_fusion.2, bf16[256,1,8,88]{0,3,2,1:T(8,128)(2,1)S(1)} %get-tuple-element.285, bf16[2048,2,1,88]{0,3,2,1:T(8,128)(2,1)S(1)} %dynamic-slice_bitcast_fusion.2), kind=kOutput, calls=%fused_computation.4.clone.1 | convolution fusion | flops 750778368 | bytes 18030592 | tf_op jit(solution)/shard_map/while/body/eval_jaxpr/qkgd,lkd->qkgl/dot_general | solution.py:160
  216.6 2.9 fusion.82
  219.6 1.4 compare_and_fusion.2
  221.1 1.2 dynamic-slice_bitcast_fusion.2
  222.3 3.9 %fusion.81 = (f32[256,8]{0,1:T(8,128)S(1)}, f32[2048,256,8]{1,0,2:T(8,128)S(1)}) fusion(pred[256,2048]{0,1:T(8,128)(4,1)S(1)} %compare_and_fusion.2, bf16[256,1,8,88]{0,3,2,1:T(8,128)(2,1)S(1)} %get-tuple-element.285, bf16[2048,2,1,88]{0,3,2,1:T(8,128)(2,1)S(1)} %dynamic-slice_bitcast_fusion.2), kind=kOutput, calls=%fused_computation.4.clone.1 | convolution fusion | flops 750778368 | bytes 18030592 | tf_op jit(solution)/shard_map/while/body/eval_jaxpr/qkgd,lkd->qkgl/dot_general | solution.py:160
  226.2 2.9 fusion.82
  229.2 1.4 compare_and_fusion.2
  230.7 1.2 dynamic-slice_bitcast_fusion.2
  231.9 3.9 %fusion.81 = (f32[256,8]{0,1:T(8,128)S(1)}, f32[2048,256,8]{1,0,2:T(8,128)S(1)}) fusion(pred[256,2048]{0,1:T(8,128)(4,1)S(1)} %compare_and_fusion.2, bf16[256,1,8,88]{0,3,2,1:T(8,128)(2,1)S(1)} %get-tuple-element.285, bf16[2048,2,1,88]{0,3,2,1:T(8,128)(2,1)S(1)} %dynamic-slice_bitcast_fusion.2), kind=kOutput, calls=%fused_computation.4.clone.1 | convolution fusion | flops 750778368 | bytes 18030592 | tf_op jit(solution)/shard_map/while/body/eval_jaxpr/qkgd,lkd->qkgl/dot_general | solution.py:160
  235.7 2.9 fusion.82
  238.7 1.4 compare_and_fusion.2
  241.4 3.9 %fusion.81 = (f32[256,8]{0,1:T(8,128)S(1)}, f32[2048,256,8]{1,0,2:T(8,128)S(1)}) fusion(pred[256,2048]{0,1:T(8,128)(4,1)S(1)} %compare_and_fusion.2, bf16[256,1,8,88]{0,3,2,1:T(8,128)(2,1)S(1)} %get-tuple-element.285, bf16[2048,2,1,88]{0,3,2,1:T(8,128)(2,1)S(1)} %dynamic-slice_bitcast_fusion.2), kind=kOutput, calls=%fused_computation.4.clone.1 | convolution fusion | flops 750778368 | bytes 18030592 | tf_op jit(solution)/shard_map/while/body/eval_jaxpr/qkgd,lkd->qkgl/dot_general | solution.py:160
  245.3 2.9 fusion.82
  248.3 1.4 compare_and_fusion.2
  251.0 3.9 %fusion.81 = (f32[256,8]{0,1:T(8,128)S(1)}, f32[2048,256,8]{1,0,2:T(8,128)S(1)}) fusion(pred[256,2048]{0,1:T(8,128)(4,1)S(1)} %compare_and_fusion.2, bf16[256,1,8,88]{0,3,2,1:T(8,128)(2,1)S(1)} %get-tuple-element.285, bf16[2048,2,1,88]{0,3,2,1:T(8,128)(2,1)S(1)} %dynamic-slice_bitcast_fusion.2), kind=kOutput, calls=%fused_computation.4.clone.1 | convolution fusion | flops 750778368 | bytes 18030592 | tf_op jit(solution)/shard_map/while/body/eval_jaxpr/qkgd,lkd->qkgl/dot_general | solution.py:160
  254.8 2.9 fusion.82
  257.9 3.6 %fusion.68 = f32[256,1408]{1,0:T(8,128)} fusion(bf16[256,704]{0,1:T(8,128)(2,1)S(1)} %bitcast.200, bf16[704,1408]{1,0:T(8,128)(2,1)} %param.25), kind=kOutput, calls=%fused_computation.148 | convolution fusion | flops 507510784 | bytes 3784704 | tf_op jit(solution)/shard_map/dot_general | solution.py:183
  261.5 28.1 %all-reduce.6.cloned.1.call-done = f32[256,1408]{1,0:T(8,128)} async-done(((f32[256,1408]{1,0:T(8,128)}), f32[256,1408]{1,0:T(8,128)}) %all-reduce.6.cloned.1.call-update) | async-done | bytes 1441808 | tf_op jit(solution)/shard_map/psum | solution.py:184
  289.6 2.3 fusion.46
  (101 shorter events, 12.2 us)
Async XLA Ops:
  6.5 14.2 %copy-start = (bf16[704,1408]{1,0:T(8,128)(2,1)S(1)}, bf16[704,1408]{1,0:T(8,128)(2,1)}, u32[]{:S(2)}) copy-start(bf16[704,1408]{1,0:T(8,128)(2,1)} %param.21) | copy-start | bytes 5947396
  6.5 2.6 copy-start.3
  6.5 49.3 %all-reduce.4.cloned.1.call-start = ((), (), s32[]{:S(2)}) async-start(), calls=%async_computation.1 | async-start | bytes 5767168 | tf_op jit(solution)/shard_map/psum | solution.py:101
  20.7 3.1 %copy-start.5 = (s32[8192]{0:T(1024)S(1)}, s32[8192]{0:T(1024)}, u32[]{:S(2)}) copy-start(s32[8192]{0:T(1024)} %param.17) | copy-start | bytes 98308
  23.8 2.6 copy-start.6
  64.0 28.6 %copy-start.2 = (bf16[256,1,1408]{2,0,1:T(8,128)(2,1)S(1)}, bf16[256,1,1408]{2,0,1:T(8,128)(2,1)}, u32[]{:S(2)}) copy-start(bf16[256,1,1408]{2,0,1:T(8,128)(2,1)} %param.18) | copy-start | bytes 2162692
  71.8 20.8 %all-to-all-start = ((bf16[2,64,1408]{2,0,1:T(2,128)(2,1)}), bf16[2,64,1408]{2,0,1:T(2,128)(2,1)S(1)}, u32[]{:S(2)}, u32[]{:S(2)}) async-start(bf16[2,64,1408]{2,0,1:T(2,128)(2,1)} %fusion.51), calls=%async_computation | async-start | bytes 720896 | tf_op jit(solution)/shard_map/all_to_all | solution.py:112
  81.9 93.4 %all-gather.3.cloned.1.call-start = ((), (), s32[]{:S(2)}) async-start(), calls=%async_computation.3 | async-start | bytes 5857280 | tf_op jit(solution)/shard_map/all_gather | solution.py:146
  92.6 1.8 copy-start.7
  94.2 1.6 copy-start.4
  95.7 193.8 %all-reduce.6.cloned.1.call-start = ((), (), s32[]{:S(2)}) async-start(), calls=%async_computation.2 | async-start | bytes 2883584 | tf_op jit(solution)/shard_map/psum | solution.py:184
  257.9 34.0 %copy-start.1 = (bf16[704,1408]{1,0:T(8,128)(2,1)S(1)}, bf16[704,1408]{1,0:T(8,128)(2,1)}, u32[]{:S(2)}) copy-start(bf16[704,1408]{1,0:T(8,128)(2,1)} %param.21) | copy-start | bytes 5947396
Sparse Core Ops, SparseCore 0:
  23.9 31.8 all-reduce.3
  95.8 79.4 all-gather.2
  261.6 27.8 all-reduce.5
where the time goes:
time: 299 us; the launch traced here: 298 us
  waiting for transfers between devices  144 us (48%)
  matrix products  79 us (26%)
  other arithmetic  23 us (8%)
  local copies, waits for them, and re-layouts  20.3 us (7%)
  between operations  15.5 us (5%)
  starting transfers between devices  10.2 us (3%)
  blocking collectives  5.69 us (2%)
    all_gather x1, waiting for transfers between devices, body(): piece = lax.all_gather(shared, 'seq', axis=0, tiled=True)  76.8 us
    dot_general x8, matrix products, one_block(): jnp.einsum('qkgd,lkd->qkgl', text_queries, block_pair[:, 0], preferred_el...  31.2 us
    psum x1, waiting for transfers between devices, body(): lax.psum(head_terms, 'section')  28.8 us
    psum x1, waiting for transfers between devices, body(): lax.psum(output_terms, 'section')  28.1 us
    dot_general x8, matrix products, one_block(): jnp.einsum('qkgl,lkd->qkgd', weights.astype(jnp.bfloat16), block_pair[:,...  23.4 us
    and x8, other arithmetic, one_block(): (block_places[None, :] <= query_places[:, None]) & (block_segments[None,...  11.6 us
    all_to_all x1, waiting for transfers between devices, body(): lax.all_to_all(jnp.roll(image_rows.reshape(per_peer, seq_count, image_row...  10.5 us
    all_to_all x1, starting transfers between devices, body(): lax.all_to_all(jnp.roll(image_rows.reshape(per_peer, seq_count, image_row...  10.1 us
  transfers between devices with their start and end apart: 4, of which 4 were waited for; matrix products, arithmetic and copies ran while one was open for 1% of the time, Pallas kernels for 0%

commit v1 on v0

v1 whole, which is shorter than its diff:
```python
import math

import jax
import jax.numpy as jnp
from jax import lax
from jax.sharding import PartitionSpec as P

D = 1408
HEAD = 88
CHUNKS = 4


def layer_norm(values):
    values = values.astype(jnp.float32)
    centred = values - jnp.mean(values, -1, keepdims=True)
    return centred * lax.rsqrt(jnp.mean(centred * centred, -1, keepdims=True) + 1e-06)


def root_norm(values):
    values = values.astype(jnp.float32)
    return values * lax.rsqrt(jnp.mean(values * values, -1, keepdims=True) + 1e-06)


def merge_rows(grid, offsets, count):
    heights = grid[:, 0]
    widths = grid[:, 1]
    group_start = offsets // 4
    group_count = heights * widths // 4
    merged_ids = jnp.arange(count, dtype=jnp.int32)
    inside = (
        (merged_ids[:, None] >= group_start[None, :])
        & (merged_ids[:, None] < (group_start + group_count)[None, :])
    ).astype(jnp.int32)
    first_group = jnp.sum(inside * group_start[None, :], 1)
    first_patch = jnp.sum(inside * offsets[None, :], 1)
    row_width = jnp.sum(inside * widths[None, :], 1)
    within = merged_ids - first_group
    groups_across = row_width // 2
    group_row = within // groups_across
    group_col = within % groups_across
    corner = first_patch + 2 * group_row * row_width + 2 * group_col
    return jnp.stack([corner, corner + 1, corner + row_width, corner + row_width + 1], 1)


def swap(values):
    return lax.ppermute(values, "section", [(0, 1), (1, 0)])


def in_head_order(first, own, other, axis):
    return jnp.where(
        first, jnp.concatenate([own, other], axis), jnp.concatenate([other, own], axis)
    )


def body(
    patches,
    image_grid,
    image_offsets,
    dest_positions,
    text_embeds,
    segment_ids,
    vision_qkv,
    vision_out,
    projector,
    decoder_q,
    decoder_kv,
    decoder_out,
):
    section_index = lax.axis_index("section")
    seq_index = lax.axis_index("seq")
    seq_count = lax.axis_size("seq")
    first = section_index == 0
    scale = 3.0 / math.sqrt(HEAD)
    patch_count = patches.shape[0]
    local_heads = vision_out.shape[0] // HEAD
    merged_count = patch_count // 4

    vision_out_other = swap(vision_out)
    decoder_out_full = in_head_order(first, decoder_out, swap(decoder_out), 0)

    normed = layer_norm(patches).astype(jnp.bfloat16)
    mixed = jnp.dot(normed, vision_qkv.reshape(D, -1), preferred_element_type=jnp.float32).reshape(
        patch_count, 3, local_heads, HEAD
    )
    queries = root_norm(mixed[:, 0]).astype(jnp.bfloat16)
    keys = root_norm(mixed[:, 1]).astype(jnp.bfloat16)
    values = mixed[:, 2].astype(jnp.bfloat16)
    offsets = image_offsets - seq_index * patch_count
    image_of = jnp.sum(
        (jnp.arange(patch_count, dtype=jnp.int32)[:, None] >= offsets[None, :]).astype(jnp.int32), 1
    )
    scores = jnp.einsum("qhd,khd->hqk", queries, keys, preferred_element_type=jnp.float32) * scale
    same = (image_of[:, None] == image_of[None, :])[None]
    weights = jnp.where(same, jnp.exp(scores), jnp.zeros_like(scores))
    totals = jnp.sum(weights, -1)
    mixed_values = jnp.einsum(
        "hqk,khd->qhd", weights.astype(jnp.bfloat16), values, preferred_element_type=jnp.float32
    )
    attended = (
        (mixed_values / jnp.transpose(totals)[:, :, None])
        .astype(jnp.bfloat16)
        .reshape(patch_count, local_heads * HEAD)
    )
    picks = merge_rows(image_grid, offsets, merged_count)
    own_picks = lax.dynamic_slice_in_dim(picks, 2 * section_index, 2, 1).reshape(-1)
    other_picks = lax.dynamic_slice_in_dim(picks, 2 - 2 * section_index, 2, 1).reshape(-1)
    received_heads = swap(attended[other_picks])
    own_rows = jnp.concatenate([attended[own_picks], received_heads], 1)
    full_out = jnp.concatenate([vision_out, vision_out_other], 0)
    kept = (
        patches[own_picks].astype(jnp.float32)
        + jnp.dot(own_rows, full_out, preferred_element_type=jnp.float32)
    ).astype(jnp.bfloat16)
    merge_terms = jnp.dot(
        kept.reshape(merged_count, 2 * D),
        projector.reshape(2 * D, D),
        preferred_element_type=jnp.float32,
    )
    image_rows = (merge_terms + swap(merge_terms)).astype(jnp.bfloat16)

    per_peer = merged_count // seq_count
    run_starts = dest_positions.reshape(seq_count, merged_count)[:, 0]
    own_start = run_starts[seq_index]
    received = lax.all_to_all(
        jnp.roll(image_rows.reshape(per_peer, seq_count, image_rows.shape[1]), own_start, axis=1),
        "seq",
        split_axis=1,
        concat_axis=1,
        tiled=True,
    )
    slot_base = jnp.arange(per_peer, dtype=jnp.int32)[:, None] * seq_count
    landing = (
        run_starts[None, :] + slot_base + (seq_index - run_starts[None, :]) % seq_count
    ) // seq_count
    text_rows = text_embeds.shape[0]
    prompt = text_embeds.reshape(text_rows, D).at[landing.reshape(-1)].set(received.reshape(-1, D))
    text_normed = root_norm(prompt).astype(jnp.bfloat16)
    text_queries = root_norm(
        jnp.dot(text_normed, decoder_q, preferred_element_type=jnp.float32).reshape(
            text_rows, local_heads, HEAD
        )
    ).astype(jnp.bfloat16)
    paired = jnp.dot(
        text_normed, decoder_kv.reshape(D, -1), preferred_element_type=jnp.float32
    ).reshape(text_rows, 2, HEAD)
    key_rows = root_norm(paired[:, 0]).astype(jnp.bfloat16)
    value_rows = paired[:, 1].astype(jnp.bfloat16)
    shared = jnp.stack([key_rows, value_rows], 1)

    query_places = jnp.arange(text_rows, dtype=jnp.int32) * seq_count + seq_index
    query_segments = lax.dynamic_slice_in_dim(segment_ids, seq_index, 1, 1)[:, 0]
    step = text_rows // CHUNKS
    sums = jnp.zeros((text_rows, local_heads, HEAD), jnp.float32)
    totals = jnp.zeros((text_rows, local_heads), jnp.float32)
    for chunk in range(CHUNKS):
        low = chunk * step
        piece = lax.all_gather(shared[None, low : low + step], "seq", axis=0, tiled=True)
        piece = piece.reshape(seq_count * step, 2, HEAD)
        key_places = (
            jnp.arange(seq_count, dtype=jnp.int32)[:, None]
            + (low + jnp.arange(step, dtype=jnp.int32))[None, :] * seq_count
        ).reshape(-1)
        key_segments = jnp.transpose(segment_ids[low : low + step]).reshape(-1)
        chunk_queries = text_queries[low:]
        scores = (
            jnp.einsum("qgd,ld->qgl", chunk_queries, piece[:, 0], preferred_element_type=jnp.float32)
            * scale
        )
        allowed = (key_places[None, :] <= query_places[low:, None]) & (
            key_segments[None, :] == query_segments[low:, None]
        )
        weights = jnp.where(allowed[:, None, :], jnp.exp(scores), jnp.zeros_like(scores))
        totals = totals.at[low:].add(jnp.sum(weights, -1))
        sums = sums.at[low:].add(
            jnp.einsum(
                "qgl,ld->qgd",
                weights.astype(jnp.bfloat16),
                piece[:, 1],
                preferred_element_type=jnp.float32,
            )
        )
    attended_text = (sums / totals[..., None]).astype(jnp.bfloat16).reshape(text_rows, -1)
    all_heads = in_head_order(first, attended_text, swap(attended_text), 1)
    output_terms = jnp.dot(all_heads, decoder_out_full, preferred_element_type=jnp.float32)
    decoded = (prompt.astype(jnp.float32) + output_terms).astype(jnp.bfloat16)
    return decoded.reshape(text_rows, 1, D)


def solution(mesh):
    placed = (
        P("seq", None),
        P("seq", None),
        P("seq"),
        P(),
        P(None, "seq", None),
        P(),
        P(None, None, "section"),
        P("section", None),
        P("section", None, None),
        P(None, "section"),
        P(None, None, "section"),
        P("section", None),
    )
    return jax.shard_map(
        body, mesh=mesh, in_specs=placed, out_specs=P(None, "seq", None), check_vma=False
    )
```

time: 299 us -> 401 us (1.34); the launches traced: 298 us -> 394 us
  local copies, waits for them, and re-layouts: 20.3 us -> 102 us
  matrix products: 79 us -> 98 us
  other arithmetic: 23 us -> 15.7 us
  starting transfers between devices: 10.2 us -> 17 us
  blocking collectives: 5.69 us -> 0 us
    psum x2 -> x0, waiting for transfers between devices: 56.9 us -> none  [the longest x1 28.8 us: body(): lax.psum(head_terms, 'section')]
    all_gather x1 -> x4, waiting for transfers between devices: 76.8 us -> 133 us  [body(): lax.all_gather(shared[None, low:low + step], 'seq', axis=0, tiled=True)]
    unnamed x18 -> x44, local copies, waits for them, and re-layouts: 0.05 us -> 43.9 us
    slice x0 -> x14, local copies, waits for them, and re-layouts: none -> 31 us  [the longest x4 27.8 us: body(): piece[:, 1]]
    dot_general x20 -> x12, matrix products: 65.6 us -> 85.1 us  [the longest x4 38.2 us: body(): jnp.einsum('qgd,ld->qgl', chunk_queries, piece[:, 0], preferred_element_t...]
    scatter-add x0 -> x4, local copies, waits for them, and re-layouts: none -> 12.5 us  [the longest x2 12.1 us: body(): sums.at[low:]]
    squeeze x8 -> x0, local copies, waits for them, and re-layouts: 9.42 us -> none  [body(): lax.scan(one_block, start_state, (grouped, key_places, key_segments))]
    gather x1 -> x3, local copies, waits for them, and re-layouts: 1.3 us -> 7.4 us  [the longest x1 4.27 us: body(): patches[own_picks].astype(jnp.float32)]
  transfers between devices with their start and end apart: 4 -> 10, of which waited for: 4 -> 5; matrix products, arithmetic and copies ran while one was open for 1% -> 48% of each run, Pallas kernels for 0% -> 0%
where the time goes in v1:
time: 401 us; the launch traced here: 394 us
  waiting for transfers between devices  145 us (36%)
  local copies, waits for them, and re-layouts  102 us (25%)
  matrix products  98 us (24%)
  starting transfers between devices  17 us (4%)
  between operations  15.9 us (4%)
  other arithmetic  15.7 us (4%)
    all_gather x4, waiting for transfers between devices, body(): lax.all_gather(shared[None, low:low + step], 'seq', axis=0, tiled=True)  133 us
    unnamed x44, local copies, waits for them, and re-layouts  43.9 us
    dot_general x4, matrix products, body(): jnp.einsum('qgd,ld->qgl', chunk_queries, piece[:, 0], preferred_element_t...  38.2 us
    dot_general x4, matrix products, body(): jnp.einsum('qgl,ld->qgd', weights.astype(jnp.bfloat16), piece[:, 1], pref...  29.7 us
    slice x4, local copies, waits for them, and re-layouts, body(): piece[:, 1]  27.8 us
    scatter-add x2, local copies, waits for them, and re-layouts, body(): sums.at[low:]  12.1 us
    all_to_all x1, starting transfers between devices, body(): lax.all_to_all(jnp.roll(image_rows.reshape(per_peer, seq_count, image_row...  11.2 us
    all_to_all x1, waiting for transfers between devices, body(): lax.all_to_all(jnp.roll(image_rows.reshape(per_peer, seq_count, image_row...  10.6 us
  transfers between devices with their start and end apart: 10, of which 5 were waited for; matrix products, arithmetic and copies ran while one was open for 48% of the time, Pallas kernels for 0%

profile of v1, /device:TPU:1, one launch (start us, length us, event | category | flops | bytes accessed | tf_op | source)
XLA Modules:
  0.0 394.0 jit_solution(17752541069491407956)
XLA Ops:
  6.5 1.4 collective-permute-start.1
  10.7 1.6 convert_reduce_fusion
  12.8 6.0 %fusion.57 = f32[512,3,8,88]{0,3,2,1:T(8,128)S(1)} fusion(bf16[3,8,88,1408]{3,2,1,0:T(8,128)(2,1)} %bitcast.178, bf16[512,1408]{1,0:T(8,128)(2,1)S(1)} %copy-done.2, f32[512]{0:T(512)S(1)} %add_rsqrt_fusion.3, f32[512]{0:T(512)S(1)} %broadcast_multiply_fusion), kind=kOutput, calls=%fused_computation.63 | convolution fusion | flops 3047948288 | bytes 11718656 | tf_op jit(solution)/shard_map/dot_general | solution.py:82
  18.8 2.0 copy-done.4
  21.8 4.2 %fusion.15 = (f32[8,512]{1,0:T(8,128)S(1)}, f32[8,512,512]{1,2,0:T(8,128)S(1)}) fusion(pred[512,512]{0,1:T(8,128)(4,1)} %broadcast_compare_fusion, f32[512,3,8,88]{0,3,2,1:T(8,128)} %copy-done.4, f32[512,8]{0,1:T(8,128)S(1)} %get-tuple-element.165, f32[512,8]{0,1:T(8,128)S(1)} %get-tuple-element.166), kind=kOutput, calls=%fused_computation.21 | convolution fusion | flops 376827904 | bytes 11583488 | tf_op jit(solution)/shard_map/qhd,khd->hqk/dot_general | solution.py:92
  26.1 3.1 divide_convert_fusion
  29.5 1.2 gather_fusion.2
  31.1 4.3 %gather_fusion = bf16[256,1408]{1,0:T(8,128)(2,1)} fusion(bf16[512,1408]{1,0:T(8,128)(2,1)} %param.32, s32[1024]{0:T(1024)S(1)} %pad_clamp_fusion.1), kind=kCustom, calls=%fused_computation | custom fusion | bytes 1442816 | tf_op jit(solution)/shard_map/gather | solution.py:111
  35.4 1.9 gather_fusion.1
  37.3 4.0 %fusion.46 = bf16[256,1408]{1,0:T(8,128)(2,1)S(1)} fusion(bf16[704,1408]{1,0:T(8,128)(2,1)} %collective-permute-done.1, bf16[704,1408]{1,0:T(8,128)(2,1)} %param.39, bf16[256,1408]{1,0:T(8,128)(2,1)} %gather_fusion, bf16[256,704]{1,0:T(8,128)(2,1)} %collective-permute-done, bf16[256,704]{1,0:T(8,128)(2,1)} %gather_fusion.1), kind=kOutput, calls=%fused_computation.53 | convolution fusion | flops 1025474560 | bytes 6127616 | tf_op jit(solution)/shard_map/dot_general | solution.py:112
  41.6 4.5 %fusion.128 = f32[128,1408]{1,0:T(8,128)S(1)} fusion(bf16[128,2816]{1,0:T(8,128)(2,1)S(1)} %reshape.1031, bf16[2816,1408]{1,0:T(8,128)(2,1)} %bitcast.163), kind=kOutput, calls=%fused_computation.233 | convolution fusion | flops 1015021568 | bytes 9371648 | tf_op jit(solution)/shard_map/dot_general | solution.py:114
  50.7 1.7 fusion.96
  52.4 11.2 %all-to-all-start = ((bf16[2,64,1408]{2,0,1:T(2,128)(2,1)}), bf16[2,64,1408]{2,0,1:T(2,128)(2,1)S(1)}, u32[]{:S(2)}, u32[]{:S(2)}) async-start(bf16[2,64,1408]{2,0,1:T(2,128)(2,1)} %fusion.96), calls=%async_computation | async-start | bytes 720896 | tf_op jit(solution)/shard_map/all_to_all | solution.py:124
  63.9 10.6 %all-to-all-done = bf16[2,64,1408]{2,0,1:T(2,128)(2,1)S(1)} async-done(((bf16[2,64,1408]{2,0,1:T(2,128)(2,1)}), bf16[2,64,1408]{2,0,1:T(2,128)(2,1)S(1)}, u32[]{:S(2)}, u32[]{:S(2)}) %all-to-all-start) | async-done | bytes 360480 | tf_op jit(solution)/shard_map/all_to_all | solution.py:124
  74.5 1.6 scatter_fusion
  76.3 1.5 fusion.89
  78.8 1.8 collective-permute-start.4
  83.0 1.3 compare_and_fusion.2
  85.5 1.6 compare_and_fusion.1
  87.2 1.9 compare_and_fusion
  92.6 48.0 %all-gather.9.cloned.1.call-done = bf16[4096,2,88]{2,1,0:T(2,128)(2,1)} async-done(((bf16[64,2,88]{2,1,0:T(2,128)(2,1)}), bf16[4096,2,88]{2,1,0:T(2,128)(2,1)}) %all-gather.9.cloned.1.call-update) | async-done | bytes 1441808 | tf_op jit(solution)/shard_map/all_gather | solution.py:157
  140.6 7.2 %fusion.126 = (bf16[4096,1,88]{2,1,0:T(2,128)(2,1)}, bf16[4096,1,88]{2,1,0:T(2,128)(2,1)}) fusion(bf16[4096,2,88]{2,1,0:T(2,128)(2,1)} %all-gather.9.cloned.1.call-done), kind=kLoop, calls=%fused_computation.231 | loop fusion | bytes 2883584 | tf_op jit(solution)/shard_map/slice | solution.py:178
  147.8 5.3 %copy.126 = bf16[4096,1,88]{0,2,1:T(8,128)(2,1)} copy(bf16[4096,1,88]{2,1,0:T(2,128)(2,1)} %get-tuple-element.138) | data formatting | bytes 1441792
  153.0 5.3 %copy.127 = bf16[4096,1,88]{0,2,1:T(8,128)(2,1)} copy(bf16[4096,1,88]{2,1,0:T(2,128)(2,1)} %get-tuple-element.137) | data formatting | bytes 1441792
  158.3 48.3 %all-gather.11.cloned.1.call-done = bf16[4096,2,88]{2,1,0:T(2,128)(2,1)} async-done(((bf16[64,2,88]{2,1,0:T(2,128)(2,1)}), bf16[4096,2,88]{2,1,0:T(2,128)(2,1)}) %all-gather.11.cloned.1.call-update) | async-done | bytes 1441808 | tf_op jit(solution)/shard_map/all_gather | solution.py:157
  206.6 6.9 %fusion.125 = (bf16[4096,1,88]{2,1,0:T(2,128)(2,1)}, bf16[4096,1,88]{2,1,0:T(2,128)(2,1)}) fusion(bf16[4096,2,88]{2,1,0:T(2,128)(2,1)} %all-gather.11.cloned.1.call-done), kind=kLoop, calls=%fused_computation.230 | loop fusion | bytes 2883584 | tf_op jit(solution)/shard_map/slice | solution.py:178
  213.5 4.7 %copy.128 = bf16[4096,1,88]{0,2,1:T(8,128)(2,1)S(1)} copy(bf16[4096,1,88]{2,1,0:T(2,128)(2,1)} %get-tuple-element.136) | data formatting | bytes 1441792
  218.2 5.3 %copy.129 = bf16[4096,1,88]{0,2,1:T(8,128)(2,1)} copy(bf16[4096,1,88]{2,1,0:T(2,128)(2,1)} %get-tuple-element.135) | data formatting | bytes 1441792
  223.5 12.1 %fusion.2 = (f32[192,8]{1,0:T(8,128)}, f32[192,8,4096]{2,1,0:T(8,128)}) fusion(pred[192,4096]{1,0:T(8,128)(4,1)S(1)} %copy-done.7, bf16[256,8,88]{2,1,0:T(8,128)(2,1)S(1)} %multiply_convert_fusion.2, bf16[4096,1,88]{0,2,1:T(8,128)(2,1)S(1)} %copy.128), kind=kOutput, calls=%fused_computation.8 | convolution fusion | flops 1126169088 | bytes 27039744 | tf_op jit(solution)/shard_map/qgd,ld->qgl/dot_general | solution.py:166
  235.6 10.5 %fusion.9 = f32[192,8,88]{2,1,0:T(8,128)S(1)} fusion(f32[192,8,4096]{2,1,0:T(8,128)} %get-tuple-element.158, pred[192,4096]{1,0:T(8,128)(4,1)S(1)} %copy-done.7, bf16[4096,1,88]{0,2,1:T(8,128)(2,1)} %copy.129), kind=kOutput, calls=%fused_computation.15 | convolution fusion | flops 1126170624 | bytes 27213824 | tf_op jit(solution)/shard_map/qgl,ld->qgd/dot_general | solution.py:175
  246.5 16.5 %fusion = (f32[256,8]{0,1:T(8,128)S(1)}, f32[256,8,4096]{2,0,1:T(8,128)}) fusion(pred[256,4096]{1,0:T(8,128)(4,1)} %compare_and_fusion, bf16[256,8,88]{0,2,1:T(8,128)(2,1)} %bitcast.170, bf16[4096,1,88]{0,2,1:T(8,128)(2,1)} %copy.126), kind=kOutput, calls=%fused_computation.5 | convolution fusion | flops 1501558784 | bytes 35692544 | tf_op jit(solution)/shard_map/qgd,ld->qgl/dot_general | solution.py:166
  263.0 13.8 %fusion.4 = f32[256,8,88]{0,2,1:T(8,128)S(1)} fusion(f32[256,8,4096]{2,0,1:T(8,128)} %get-tuple-element.156, pred[256,4096]{1,0:T(8,128)(4,1)S(1)} %copy-done.6, bf16[4096,1,88]{0,2,1:T(8,128)(2,1)S(1)} %copy-done.9), kind=kOutput, calls=%fused_computation.11 | convolution fusion | flops 1501560832 | bytes 36044800 | tf_op jit(solution)/shard_map/qgl,ld->qgd/dot_general | solution.py:175
  277.1 7.1 %scatter-add.20 = f32[256,8,88]{0,2,1:T(8,128)S(1)} dynamic-update-slice(f32[256,8,88]{0,2,1:T(8,128)S(1)} %fusion.4, f32[192,8,88]{0,2,1:T(8,128)S(1)} %slice_add_fusion, s32[]{:T(128)} %constant.358.clone.1, s32[]{:T(128)} %constant.360.clone.1, s32[]{:T(128)} %constant.360.clone.1) | dynamic-update-slice | bytes 1081348 | tf_op jit(solution)/shard_map/scatter-add | solution.py:174
  284.2 7.0 %fusion.124 = (bf16[4096,1,88]{2,1,0:T(2,128)(2,1)}, bf16[4096,1,88]{2,1,0:T(2,128)(2,1)}) fusion(bf16[4096,2,88]{2,1,0:T(2,128)(2,1)} %all-gather.13.cloned.1.call-done), kind=kLoop, calls=%fused_computation.229 | loop fusion | bytes 2883584 | tf_op jit(solution)/shard_map/slice | solution.py:178
  291.2 5.3 %copy.131 = bf16[4096,1,88]{0,2,1:T(8,128)(2,1)} copy(bf16[4096,1,88]{2,1,0:T(2,128)(2,1)} %get-tuple-element.133) | data formatting | bytes 1441792
  296.4 5.3 %copy.130 = bf16[4096,1,88]{0,2,1:T(8,128)(2,1)} copy(bf16[4096,1,88]{2,1,0:T(2,128)(2,1)} %get-tuple-element.134) | data formatting | bytes 1441792
  301.8 36.9 %all-gather.15.cloned.1.call-done = bf16[4096,2,88]{2,1,0:T(2,128)(2,1)} async-done(((bf16[64,2,88]{2,1,0:T(2,128)(2,1)}), bf16[4096,2,88]{2,1,0:T(2,128)(2,1)}) %all-gather.15.cloned.1.call-update) | async-done | bytes 1441808 | tf_op jit(solution)/shard_map/all_gather | solution.py:157
  338.7 6.8 %fusion.123 = (bf16[4096,1,88]{2,1,0:T(2,128)(2,1)}, bf16[4096,1,88]{2,1,0:T(2,128)(2,1)}) fusion(bf16[4096,2,88]{2,1,0:T(2,128)(2,1)} %all-gather.15.cloned.1.call-done), kind=kLoop, calls=%fused_computation.228 | loop fusion | bytes 2883584 | tf_op jit(solution)/shard_map/slice | solution.py:178
  345.5 4.6 %copy.132 = bf16[4096,1,88]{0,2,1:T(8,128)(2,1)S(1)} copy(bf16[4096,1,88]{2,1,0:T(2,128)(2,1)} %get-tuple-element.132) | data formatting | bytes 1441792
  350.1 5.3 %copy.133 = bf16[4096,1,88]{0,2,1:T(8,128)(2,1)} copy(bf16[4096,1,88]{2,1,0:T(2,128)(2,1)} %get-tuple-element.131) | data formatting | bytes 1441792
  355.4 3.9 fusion.17
  359.4 2.5 fusion.23
  363.4 5.7 %fusion.7 = (f32[128,8]{0,1:T(8,128)S(1)}, f32[128,8,4096]{2,0,1:T(8,128)S(1)}) fusion(pred[128,4096]{1,0:T(8,128)(4,1)S(1)} %copy-done.11, bf16[4096,1,88]{0,2,1:T(8,128)(2,1)} %copy.130, bf16[128,8,88]{2,1,0:T(8,128)(2,1)S(1)} %slice-done), kind=kOutput, calls=%fused_computation.13 | convolution fusion | flops 750779392 | bytes 18206720 | tf_op jit(solution)/shard_map/qgd,ld->qgl/dot_general | solution.py:166
  369.2 2.8 constant_dynamic-update-slice_fusion.1
  372.2 5.0 %scatter-add.24 = f32[256,8,88]{0,2,1:T(8,128)S(1)} dynamic-update-slice(f32[256,8,88]{0,2,1:T(8,128)S(1)} %get-tuple-element.153, f32[64,8,88]{0,2,1:T(8,128)S(1)} %slice_add_fusion.1, s32[]{:T(128)} %constant.377.clone.1, s32[]{:T(128)} %constant.360.clone.1, s32[]{:T(128)} %constant.360.clone.1) | dynamic-update-slice | bytes 360452 | tf_op jit(solution)/shard_map/scatter-add | solution.py:174
  378.3 1.6 collective-permute-start.3
  380.0 1.3 collective-permute-done.3
  381.3 6.0 %fusion.50 = bf16[256,1,1408]{2,0,1:T(8,128)(2,1)} fusion(bf16[704,1408]{1,0:T(8,128)(2,1)} %collective-permute-done.4, bf16[704,1408]{1,0:T(8,128)(2,1)} %param.43, pred[]{:T(512)S(6)} %eq.136, bf16[256,1408]{1,0:T(8,128)(2,1)S(1)} %scatter_fusion, bf16[256,704]{0,1:T(8,128)(2,1)S(1)} %collective-permute-done.3, bf16[256,704]{0,1:T(8,128)(2,1)} %bitcast.172), kind=kOutput, calls=%fused_computation.55 | convolution fusion | flops 1037189120 | bytes 6127617 | tf_op jit(solution)/shard_map/dot_general | solution.py:184
  (141 shorter events, 19.7 us)
Async XLA Ops:
  6.5 82.6 %copy-start = (bf16[1408,704]{0,1:T(8,128)(2,1)S(1)}, bf16[1408,704]{0,1:T(8,128)(2,1)}, u32[]{:S(2)}) copy-start(bf16[1408,704]{0,1:T(8,128)(2,1)} %param.41) | copy-start | bytes 5947396
  6.5 5.8 %copy-start.2 = (bf16[512,1408]{1,0:T(8,128)(2,1)S(1)}, bf16[512,1408]{1,0:T(8,128)(2,1)}, u32[]{:S(2)}) copy-start(bf16[512,1408]{1,0:T(8,128)(2,1)} %param.32) | copy-start | bytes 4325380
  6.5 30.8 %collective-permute-start.1 = (bf16[704,1408]{1,0:T(8,128)(2,1)}, bf16[704,1408]{1,0:T(8,128)(2,1)}, u32[]{:S(2)}, u32[]{:S(2)}) collective-permute-start(bf16[704,1408]{1,0:T(8,128)(2,1)} %param.39), channel_id=1, source_target_pairs={{0,64},{64,0},{1,65},{65,1},{2,66},{66,2},{3,67},{67,3},{4,68},{68... | collective-permute-start | bytes 5947400 | tf_op jit(solution)/shard_map/ppermute | solution.py:46
  18.8 2.0 copy-start.4
  21.8 4.2 %copy-start.15 = (pred[512,512]{0,1:T(8,128)(4,1)S(1)}, pred[512,512]{0,1:T(8,128)(4,1)}, u32[]{:S(2)}) copy-start(pred[512,512]{0,1:T(8,128)(4,1)} %broadcast_compare_fusion) | copy-start | bytes 786436
  30.7 6.6 %collective-permute-start = (bf16[256,704]{1,0:T(8,128)(2,1)S(1)}, bf16[256,704]{1,0:T(8,128)(2,1)}, u32[]{:S(2)}, u32[]{:S(2)}) collective-permute-start(bf16[256,704]{1,0:T(8,128)(2,1)S(1)} %gather_fusion.2), channel_id=1, source_target_pairs={{0,64},{64,0},{1,65},{65,1},{2,66},{66,2},{3,67},{67,3},{4,68},{68... | collective-permute-start | bytes 1081352 | tf_op jit(solution)/shard_map/ppermute | solution.py:46
  41.5 5.0 %copy-start.17 = (s32[8192]{0:T(1024)S(1)}, s32[8192]{0:T(1024)}, u32[]{:S(2)}) copy-start(s32[8192]{0:T(1024)} %param.35) | copy-start | bytes 98308
  46.1 28.4 %copy-start.3 = (bf16[256,1,1408]{2,0,1:T(8,128)(2,1)S(1)}, bf16[256,1,1408]{2,0,1:T(8,128)(2,1)}, u32[]{:S(2)}) copy-start(bf16[256,1,1408]{2,0,1:T(8,128)(2,1)} %param.36) | copy-start | bytes 2162692
  46.1 3.0 collective-permute-start.2
  52.4 22.1 %all-to-all-start = ((bf16[2,64,1408]{2,0,1:T(2,128)(2,1)}), bf16[2,64,1408]{2,0,1:T(2,128)(2,1)S(1)}, u32[]{:S(2)}, u32[]{:S(2)}) async-start(bf16[2,64,1408]{2,0,1:T(2,128)(2,1)} %fusion.96), calls=%async_computation | async-start | bytes 720896 | tf_op jit(solution)/shard_map/all_to_all | solution.py:124
  63.6 76.9 %all-gather.9.cloned.1.call-start = ((), (), s32[]{:S(2)}) async-start(), calls=%async_computation.1 | async-start | bytes 2129920 | tf_op jit(solution)/shard_map/all_gather | solution.py:157
  74.5 6.1 %copy-start.13 = (s32[256,64]{0,1:T(8,128)S(1)}, s32[256,64]{0,1:T(8,128)}, u32[]{:S(2)}) copy-start(s32[256,64]{0,1:T(8,128)} %param.37) | copy-start | bytes 196612
  78.8 127.9 %all-gather.11.cloned.1.call-start = ((), (), s32[]{:S(2)}) async-start(), calls=%async_computation.2 | async-start | bytes 2129920 | tf_op jit(solution)/shard_map/all_gather | solution.py:157
  78.8 301.1 %collective-permute-start.4 = (bf16[704,1408]{1,0:T(8,128)(2,1)}, bf16[704,1408]{1,0:T(8,128)(2,1)}, u32[]{:S(2)}, u32[]{:S(2)}) collective-permute-start(bf16[704,1408]{1,0:T(8,128)(2,1)} %param.43), channel_id=1, source_target_pairs={{0,64},{64,0},{1,65},{65,1},{2,66},{66,2},{3,67},{67,3},{4,68},{68... | collective-permute-start | bytes 5947400 | tf_op jit(solution)/shard_map/ppermute | solution.py:46
  81.7 202.5 %all-gather.13.cloned.1.call-start = ((), (), s32[]{:S(2)}) async-start(), calls=%async_computation.3 | async-start | bytes 2129920 | tf_op jit(solution)/shard_map/all_gather | solution.py:157
  85.0 253.6 %all-gather.15.cloned.1.call-start = ((), (), s32[]{:S(2)}) async-start(), calls=%async_computation.4 | async-start | bytes 2129920 | tf_op jit(solution)/shard_map/all_gather | solution.py:157
  91.7 263.7 %copy-start.5 = (bf16[256,8,88]{2,1,0:T(8,128)(2,1)}, bf16[256,8,88]{2,1,0:T(8,128)(2,1)S(1)}, u32[]{:S(2)}) copy-start(bf16[256,8,88]{2,1,0:T(8,128)(2,1)S(1)} %multiply_convert_fusion.2) | copy-start | bytes 1081348
  213.5 10.0 %copy-start.7 = (pred[192,4096]{1,0:T(8,128)(4,1)S(1)}, pred[192,4096]{1,0:T(8,128)(4,1)}, u32[]{:S(2)}) copy-start(pred[192,4096]{1,0:T(8,128)(4,1)} %compare_and_fusion.1) | copy-start | bytes 2359300
  246.5 16.5 %copy-start.6 = (pred[256,4096]{1,0:T(8,128)(4,1)S(1)}, pred[256,4096]{1,0:T(8,128)(4,1)}, u32[]{:S(2)}) copy-start(pred[256,4096]{1,0:T(8,128)(4,1)} %compare_and_fusion) | copy-start | bytes 3145732
  246.5 16.5 %copy-start.9 = (bf16[4096,1,88]{0,2,1:T(8,128)(2,1)S(1)}, bf16[4096,1,88]{0,2,1:T(8,128)(2,1)}, u32[]{:S(2)}) copy-start(bf16[4096,1,88]{0,2,1:T(8,128)(2,1)} %copy.127) | copy-start | bytes 2162692
  355.4 3.9 copy-start.10
  355.4 3.9 copy-start.14
  359.3 3.7 copy-start.16
  359.3 4.1 %slice-start = ((bf16[256,8,88]{2,1,0:T(8,128)(2,1)}), bf16[128,8,88]{2,1,0:T(8,128)(2,1)S(1)}, s32[]{:S(2)}) async-start(bf16[256,8,88]{2,1,0:T(8,128)(2,1)} %copy-done.5), calls=%async_computation.5 | async-start | bytes 524288 | tf_op jit(solution)/shard_map/slice | solution.py:164
  359.3 4.1 %copy-start.11 = (pred[128,4096]{1,0:T(8,128)(4,1)S(1)}, pred[128,4096]{1,0:T(8,128)(4,1)}, u32[]{:S(2)}) copy-start(pred[128,4096]{1,0:T(8,128)(4,1)} %compare_and_fusion.2) | copy-start | bytes 1572868
  363.4 5.7 %copy-start.8 = (bf16[4096,1,88]{0,2,1:T(8,128)(2,1)S(1)}, bf16[4096,1,88]{0,2,1:T(8,128)(2,1)}, u32[]{:S(2)}) copy-start(bf16[4096,1,88]{0,2,1:T(8,128)(2,1)} %copy.131) | copy-start | bytes 2162692
  377.6 0.7 copy-start.12
  378.3 2.9 collective-permute-start.3
  381.3 6.0 %copy-start.1 = (bf16[1408,704]{0,1:T(8,128)(2,1)S(1)}, bf16[1408,704]{0,1:T(8,128)(2,1)}, u32[]{:S(2)}) copy-start(bf16[1408,704]{0,1:T(8,128)(2,1)} %param.41) | copy-start | bytes 5947396
Sparse Core Ops, SparseCore 0:
  78.9 61.6 all-gather.8
  143.4 63.1 all-gather.10
  209.5 63.1 all-gather.12
  275.4 63.1 all-gather.14

commit v2 on v1

--- a/solution.py
+++ b/solution.py
@@ -7,7 +7,6 @@
 
 D = 1408
 HEAD = 88
-CHUNKS = 4
 
 
 def layer_norm(values):
@@ -149,36 +148,45 @@
 
     query_places = jnp.arange(text_rows, dtype=jnp.int32) * seq_count + seq_index
     query_segments = lax.dynamic_slice_in_dim(segment_ids, seq_index, 1, 1)[:, 0]
-    step = text_rows // CHUNKS
-    sums = jnp.zeros((text_rows, local_heads, HEAD), jnp.float32)
-    totals = jnp.zeros((text_rows, local_heads), jnp.float32)
-    for chunk in range(CHUNKS):
-        low = chunk * step
-        piece = lax.all_gather(shared[None, low : low + step], "seq", axis=0, tiled=True)
-        piece = piece.reshape(seq_count * step, 2, HEAD)
-        key_places = (
-            jnp.arange(seq_count, dtype=jnp.int32)[:, None]
-            + (low + jnp.arange(step, dtype=jnp.int32))[None, :] * seq_count
-        ).reshape(-1)
-        key_segments = jnp.transpose(segment_ids[low : low + step]).reshape(-1)
-        chunk_queries = text_queries[low:]
+    text_queries = text_queries.reshape(text_rows, 1, local_heads, HEAD)
+    start_state = (
+        jnp.zeros((text_rows, 1, local_heads, HEAD), jnp.float32),
+        jnp.zeros((text_rows, 1, local_heads), jnp.float32),
+    )
+    piece = lax.all_gather(shared.reshape(1, text_rows, 2, 1, HEAD), "seq", axis=0, tiled=True)
+    shards = piece.shape[0]
+    stride = math.gcd(shards, 8)
+    blocks = shards // stride
+    key_segments = jnp.transpose(segment_ids).reshape(blocks, stride * text_rows)
+    shard_ids = jnp.arange(shards, dtype=jnp.int32)
+    key_places = (
+        jnp.arange(text_rows, dtype=jnp.int32)[None, :] * seq_count + shard_ids[:, None]
+    ).reshape(blocks, stride * text_rows)
+    grouped = piece.reshape(blocks, stride * text_rows, 2, 1, HEAD)
+
+    def one_block(state, inputs):
+        block_pair, block_places, block_segments = inputs
         scores = (
-            jnp.einsum("qgd,ld->qgl", chunk_queries, piece[:, 0], preferred_element_type=jnp.float32)
+            jnp.einsum(
+                "qkgd,lkd->qkgl", text_queries, block_pair[:, 0], preferred_element_type=jnp.float32
+            )
             * scale
         )
-        allowed = (key_places[None, :] <= query_places[low:, None]) & (
-            key_segments[None, :] == query_segments[low:, None]
-        )
-        weights = jnp.where(allowed[:, None, :], jnp.exp(scores), jnp.zeros_like(scores))
-        totals = totals.at[low:].add(jnp.sum(weights, -1))
-        sums = sums.at[low:].add(
-            jnp.einsum(
-                "qgl,ld->qgd",
-                weights.astype(jnp.bfloat16),
-                piece[:, 1],
-                preferred_element_type=jnp.float32,
-            )
-        )
+        allowed = (block_places[None, :] <= query_places[:, None]) & (
+            block_segments[None, :] == query_segments[:, None]
+        )
+        weights = jnp.where(allowed[:, None, None, :], jnp.exp(scores), jnp.zeros_like(scores))
+        totals = state[1] + jnp.sum(weights, -1)
+        sums = state[0] + jnp.einsum(
+            "qkgl,lkd->qkgd",
+            weights.astype(jnp.bfloat16),
+            block_pair[:, 1],
+            preferred_element_type=jnp.float32,
+        )
+        return ((sums, totals), None)
+
+    result, unused = lax.scan(one_block, start_state, (grouped, key_places, key_segments))
+    sums, totals = result
     attended_text = (sums / totals[..., None]).astype(jnp.bfloat16).reshape(text_rows, -1)
     all_heads = in_head_order(first, attended_text, swap(attended_text), 1)
     output_terms = jnp.dot(all_heads, decoder_out_full, preferred_element_type=jnp.float32)

time: 401 us -> 333 us (0.83); the launches traced: 394 us -> 332 us
  local copies, waits for them, and re-layouts: 102 us -> 41.5 us
  waiting for transfers between devices: 145 us -> 85 us
  matrix products: 98 us -> 150 us
  other arithmetic: 15.7 us -> 22.1 us
    all_gather x4 -> x1, waiting for transfers between devices: 133 us -> 73 us  [body(): lax.all_gather(shared.reshape(1, text_rows, 2, 1, HEAD), 'seq', axis=0, t...]
    dot_general x8 -> x16, matrix products: 67.9 us -> 119 us  [the longest x8 61.2 us: one_block(): jnp.einsum('qkgd,lkd->qkgl', text_queries, block_pair[:, 0], preferred_el...]
    slice x14 -> x0, local copies, waits for them, and re-layouts: 31 us -> none  [the longest x4 27.8 us: body(): piece[:, 1]]
    unnamed x44 -> x22, local copies, waits for them, and re-layouts: 43.9 us -> 14.2 us
    scatter-add x4 -> x0, local copies, waits for them, and re-layouts: 12.5 us -> none  [the longest x2 12.1 us: body(): sums.at[low:]]
    squeeze x0 -> x8, local copies, waits for them, and re-layouts: none -> 9.31 us  [body(): lax.scan(one_block, start_state, (grouped, key_places, key_segments))]
    dynamic_slice x0 -> x8, local copies, waits for them, and re-layouts: none -> 6.88 us  [body(): lax.scan(one_block, start_state, (grouped, key_places, key_segments))]
    and x4 -> x8, other arithmetic: 5.81 us -> 11.6 us  [one_block(): (block_places[None, :] <= query_places[:, None]) & (block_segments[None,...]
  transfers between devices with their start and end apart: 10 -> 7, of which waited for: 5 -> 3; matrix products, arithmetic and copies ran while one was open for 48% -> 57% of each run, Pallas kernels for 0% -> 0%
where the time goes in v2:
time: 333 us; the launch traced here: 332 us
  matrix products  150 us (45%)
  waiting for transfers between devices  85 us (26%)
  local copies, waits for them, and re-layouts  41.5 us (12%)
  other arithmetic  22.1 us (7%)
  starting transfers between devices  17.2 us (5%)
  between operations  15.7 us (5%)
    all_gather x1, waiting for transfers between devices, body(): lax.all_gather(shared.reshape(1, text_rows, 2, 1, HEAD), 'seq', axis=0, t...  73 us
    dot_general x8, matrix products, one_block(): jnp.einsum('qkgd,lkd->qkgl', text_queries, block_pair[:, 0], preferred_el...  61.2 us
    dot_general x8, matrix products, one_block(): jnp.einsum('qkgl,lkd->qkgd', weights.astype(jnp.bfloat16), block_pair[:,...  57.9 us
    unnamed x22, local copies, waits for them, and re-layouts  14.2 us
    and x8, other arithmetic, one_block(): (block_places[None, :] <= query_places[:, None]) & (block_segments[None,...  11.6 us
    all_to_all x1, starting transfers between devices, body(): lax.all_to_all(jnp.roll(image_rows.reshape(per_peer, seq_count, image_row...  11.2 us
    all_to_all x1, waiting for transfers between devices, body(): lax.all_to_all(jnp.roll(image_rows.reshape(per_peer, seq_count, image_row...  10.6 us
    squeeze x8, local copies, waits for them, and re-layouts, body(): lax.scan(one_block, start_state, (grouped, key_places, key_segments))  9.31 us
  transfers between devices with their start and end apart: 7, of which 3 were waited for; matrix products, arithmetic and copies ran while one was open for 57% of the time, Pallas kernels for 0%

profile of v2, /device:TPU:1, one launch (start us, length us, event | category | flops | bytes accessed | tf_op | source)
XLA Modules:
  0.0 331.5 jit_solution(15955560327595768903)
XLA Ops:
  6.5 1.4 collective-permute-start.1
  9.7 1.6 convert_reduce_fusion
  11.9 6.0 %fusion.55 = f32[512,3,8,88]{0,3,2,1:T(8,128)S(1)} fusion(bf16[3,8,88,1408]{3,2,1,0:T(8,128)(2,1)} %bitcast.209, bf16[512,1408]{1,0:T(8,128)(2,1)S(1)} %copy-done.2, f32[512]{0:T(512)S(1)} %add_rsqrt_fusion.3, f32[512]{0:T(512)S(1)} %broadcast_multiply_fusion), kind=kOutput, calls=%fused_computation.61 | convolution fusion | flops 3047948288 | bytes 11718656 | tf_op jit(solution)/shard_map/dot_general | solution.py:81
  17.9 2.0 copy-done.4
  21.1 4.1 %fusion.18 = (f32[8,512]{1,0:T(8,128)S(1)}, f32[8,512,512]{1,2,0:T(8,128)S(1)}) fusion(pred[512,512]{0,1:T(8,128)(4,1)S(1)} %broadcast_compare_fusion, f32[512,3,8,88]{0,3,2,1:T(8,128)} %copy-done.4, f32[512,8]{0,1:T(8,128)S(1)} %get-tuple-element.177, f32[512,8]{0,1:T(8,128)S(1)} %get-tuple-element.178), kind=kOutput, calls=%fused_computation.26 | convolution fusion | flops 376827904 | bytes 11583488 | tf_op jit(solution)/shard_map/qhd,khd->hqk/dot_general | solution.py:91
  25.2 3.1 divide_convert_fusion
  30.3 1.9 gather_fusion.1
  32.2 3.5 %gather_fusion = bf16[256,1408]{1,0:T(8,128)(2,1)S(1)} fusion(bf16[512,1408]{1,0:T(8,128)(2,1)} %param.14, s32[1024]{0:T(1024)S(1)} %pad_clamp_fusion.1), kind=kCustom, calls=%fused_computation | custom fusion | bytes 1442816 | tf_op jit(solution)/shard_map/gather | solution.py:110
  35.7 3.8 %fusion.44 = bf16[256,1408]{1,0:T(8,128)(2,1)S(1)} fusion(bf16[704,1408]{1,0:T(8,128)(2,1)} %collective-permute-done.1, bf16[704,1408]{1,0:T(8,128)(2,1)} %param.21, bf16[256,1408]{1,0:T(8,128)(2,1)S(1)} %gather_fusion, bf16[256,704]{1,0:T(8,128)(2,1)} %collective-permute-done, bf16[256,704]{1,0:T(8,128)(2,1)} %gather_fusion.1), kind=kOutput, calls=%fused_computation.52 | convolution fusion | flops 1025474560 | bytes 6127616 | tf_op jit(solution)/shard_map/dot_general | solution.py:111
  39.8 4.5 %fusion.95 = f32[128,1408]{1,0:T(8,128)S(1)} fusion(bf16[128,2816]{1,0:T(8,128)(2,1)S(1)} %reshape.611, bf16[2816,1408]{1,0:T(8,128)(2,1)} %bitcast.189), kind=kOutput, calls=%fused_computation.175 | convolution fusion | flops 1015021568 | bytes 9371648 | tf_op jit(solution)/shard_map/dot_general | solution.py:113
  48.9 1.7 fusion.78
  50.6 11.2 %all-to-all-start = ((bf16[2,64,1408]{2,0,1:T(2,128)(2,1)}), bf16[2,64,1408]{2,0,1:T(2,128)(2,1)S(1)}, u32[]{:S(2)}, u32[]{:S(2)}) async-start(bf16[2,64,1408]{2,0,1:T(2,128)(2,1)} %fusion.78), calls=%async_computation | async-start | bytes 720896 | tf_op jit(solution)/shard_map/all_to_all | solution.py:123
  62.1 10.6 %all-to-all-done = bf16[2,64,1408]{2,0,1:T(2,128)(2,1)S(1)} async-done(((bf16[2,64,1408]{2,0,1:T(2,128)(2,1)}), bf16[2,64,1408]{2,0,1:T(2,128)(2,1)S(1)}, u32[]{:S(2)}, u32[]{:S(2)}) %all-to-all-start) | async-done | bytes 360480 | tf_op jit(solution)/shard_map/all_to_all | solution.py:123
  72.7 1.6 scatter_fusion
  74.6 1.5 fusion.72
  76.8 2.0 collective-permute-start.4
  79.6 1.7 fusion.94
  83.3 73.0 %all-gather.3.cloned.1.call-done = bf16[16384,2,88]{0,2,1:T(8,128)(2,1)} async-done(((bf16[256,2,88]{0,2,1:T(8,128)(2,1)}), bf16[16384,2,88]{0,2,1:T(8,128)(2,1)}) %all-gather.3.cloned.1.call-update) | async-done | bytes 5767184 | tf_op jit(solution)/shard_map/all_gather | solution.py:156
  156.3 6.6 %copy.55 = bf16[22,8,8,2048]{3,2,1,0:T(8,128)(2,1)S(1)} copy(bf16[22,8,8,2048]{3,1,2,0:T(8,128)(2,1)} %bitcast.191) | data formatting | bytes 11534336
  162.9 5.6 %copy.51 = bf16[8,2048,2,1,88]{1,4,2,3,0:T(8,128)(2,1)} copy(bf16[8,2048,2,1,88]{1,0,4,2,3:T(8,128)(2,1)S(1)} %bitcast.190) | data formatting | bytes 11534336
  168.5 147.3 %while.13 = (s32[]{:T(128)}, f32[256,1,8,88]{0,3,2,1:T(8,128)S(1)}, f32[256,1,8]{0,2,1:T(8,128)S(1)}, bf16[8,2048,2,1,88]{1,4,2,3,0:T(8,128)(2,1)}, s32[8,2048]{...) while((s32[]{:T(128)}, f32[256,1,8,88]{0,3,2,1:T(8,128)S(1)}, ...), condition=%wide.region_15.16_spmd.clone, body=%wide.region_13.15_spmd.clone.sunk | while | flops 1503496704 | bytes 39177344 | solution.py:188
  169.4 1.4 compare_and_fusion.2
  172.0 7.7 %fusion.104 = (f32[256,8]{0,1:T(8,128)S(1)}, f32[2048,256,8]{1,0,2:T(8,128)}) fusion(pred[256,2048]{0,1:T(8,128)(4,1)S(1)} %compare_and_fusion.2, bf16[256,1,8,88]{0,3,2,1:T(8,128)(2,1)S(1)} %get-tuple-element.271, bf16[2048,2,1,88]{0,3,2,1:T(8,128)(2,1)S(1)} %dynamic-slice_bitcast_fusion.2), kind=kOutput, calls=%fused_computation.6.clone.1 | convolution fusion | flops 750778368 | bytes 18030592 | tf_op jit(solution)/shard_map/while/body/eval_jaxpr/qkgd,lkd->qkgl/dot_general | solution.py:170
  179.6 7.2 %fusion.105 = f32[256,1,8,88]{0,3,2,1:T(8,128)S(1)} fusion(f32[2048,256,8]{1,0,2:T(8,128)} %get-tuple-element.240, pred[256,2048]{0,1:T(8,128)(4,1)S(1)} %compare_and_fusion.2, f32[256,1,8,88]{0,3,2,1:T(8,128)S(1)} %get-tuple-element.254, bf16[2048,2,1,88]{0,3,2,1:T(8,128)(2,1)S(1)} %dynamic-slice_bitcast_fusion.2, pred[]{:T(512)S(6)} %compare.49), kind=kOutput, calls=%fused_computation.13.clone.1 | convolution fusion | flops 751140864 | bytes 19103744 | tf_op jit(solution)/shard_map/while/body/eval_jaxpr/qkgl,lkd->qkgd/dot_general | solution.py:180
  187.8 1.4 compare_and_fusion.2
  190.4 7.7 %fusion.104 = (f32[256,8]{0,1:T(8,128)S(1)}, f32[2048,256,8]{1,0,2:T(8,128)}) fusion(pred[256,2048]{0,1:T(8,128)(4,1)S(1)} %compare_and_fusion.2, bf16[256,1,8,88]{0,3,2,1:T(8,128)(2,1)S(1)} %get-tuple-element.271, bf16[2048,2,1,88]{0,3,2,1:T(8,128)(2,1)S(1)} %dynamic-slice_bitcast_fusion.2), kind=kOutput, calls=%fused_computation.6.clone.1 | convolution fusion | flops 750778368 | bytes 18030592 | tf_op jit(solution)/shard_map/while/body/eval_jaxpr/qkgd,lkd->qkgl/dot_general | solution.py:170
  198.1 7.2 %fusion.105 = f32[256,1,8,88]{0,3,2,1:T(8,128)S(1)} fusion(f32[2048,256,8]{1,0,2:T(8,128)} %get-tuple-element.240, pred[256,2048]{0,1:T(8,128)(4,1)S(1)} %compare_and_fusion.2, f32[256,1,8,88]{0,3,2,1:T(8,128)S(1)} %get-tuple-element.254, bf16[2048,2,1,88]{0,3,2,1:T(8,128)(2,1)S(1)} %dynamic-slice_bitcast_fusion.2, pred[]{:T(512)S(6)} %compare.49), kind=kOutput, calls=%fused_computation.13.clone.1 | convolution fusion | flops 751140864 | bytes 19103744 | tf_op jit(solution)/shard_map/while/body/eval_jaxpr/qkgl,lkd->qkgd/dot_general | solution.py:180
  206.2 1.4 compare_and_fusion.2
  208.8 7.7 %fusion.104 = (f32[256,8]{0,1:T(8,128)S(1)}, f32[2048,256,8]{1,0,2:T(8,128)}) fusion(pred[256,2048]{0,1:T(8,128)(4,1)S(1)} %compare_and_fusion.2, bf16[256,1,8,88]{0,3,2,1:T(8,128)(2,1)S(1)} %get-tuple-element.271, bf16[2048,2,1,88]{0,3,2,1:T(8,128)(2,1)S(1)} %dynamic-slice_bitcast_fusion.2), kind=kOutput, calls=%fused_computation.6.clone.1 | convolution fusion | flops 750778368 | bytes 18030592 | tf_op jit(solution)/shard_map/while/body/eval_jaxpr/qkgd,lkd->qkgl/dot_general | solution.py:170
  216.5 7.2 %fusion.105 = f32[256,1,8,88]{0,3,2,1:T(8,128)S(1)} fusion(f32[2048,256,8]{1,0,2:T(8,128)} %get-tuple-element.240, pred[256,2048]{0,1:T(8,128)(4,1)S(1)} %compare_and_fusion.2, f32[256,1,8,88]{0,3,2,1:T(8,128)S(1)} %get-tuple-element.254, bf16[2048,2,1,88]{0,3,2,1:T(8,128)(2,1)S(1)} %dynamic-slice_bitcast_fusion.2, pred[]{:T(512)S(6)} %compare.49), kind=kOutput, calls=%fused_computation.13.clone.1 | convolution fusion | flops 751140864 | bytes 19103744 | tf_op jit(solution)/shard_map/while/body/eval_jaxpr/qkgl,lkd->qkgd/dot_general | solution.py:180
  224.6 1.4 compare_and_fusion.2
  227.2 7.7 %fusion.104 = (f32[256,8]{0,1:T(8,128)S(1)}, f32[2048,256,8]{1,0,2:T(8,128)}) fusion(pred[256,2048]{0,1:T(8,128)(4,1)S(1)} %compare_and_fusion.2, bf16[256,1,8,88]{0,3,2,1:T(8,128)(2,1)S(1)} %get-tuple-element.271, bf16[2048,2,1,88]{0,3,2,1:T(8,128)(2,1)S(1)} %dynamic-slice_bitcast_fusion.2), kind=kOutput, calls=%fused_computation.6.clone.1 | convolution fusion | flops 750778368 | bytes 18030592 | tf_op jit(solution)/shard_map/while/body/eval_jaxpr/qkgd,lkd->qkgl/dot_general | solution.py:170
  234.9 7.2 %fusion.105 = f32[256,1,8,88]{0,3,2,1:T(8,128)S(1)} fusion(f32[2048,256,8]{1,0,2:T(8,128)} %get-tuple-element.240, pred[256,2048]{0,1:T(8,128)(4,1)S(1)} %compare_and_fusion.2, f32[256,1,8,88]{0,3,2,1:T(8,128)S(1)} %get-tuple-element.254, bf16[2048,2,1,88]{0,3,2,1:T(8,128)(2,1)S(1)} %dynamic-slice_bitcast_fusion.2, pred[]{:T(512)S(6)} %compare.49), kind=kOutput, calls=%fused_computation.13.clone.1 | convolution fusion | flops 751140864 | bytes 19103744 | tf_op jit(solution)/shard_map/while/body/eval_jaxpr/qkgl,lkd->qkgd/dot_general | solution.py:180
  243.0 1.4 compare_and_fusion.2
  245.7 7.7 %fusion.104 = (f32[256,8]{0,1:T(8,128)S(1)}, f32[2048,256,8]{1,0,2:T(8,128)}) fusion(pred[256,2048]{0,1:T(8,128)(4,1)S(1)} %compare_and_fusion.2, bf16[256,1,8,88]{0,3,2,1:T(8,128)(2,1)S(1)} %get-tuple-element.271, bf16[2048,2,1,88]{0,3,2,1:T(8,128)(2,1)S(1)} %dynamic-slice_bitcast_fusion.2), kind=kOutput, calls=%fused_computation.6.clone.1 | convolution fusion | flops 750778368 | bytes 18030592 | tf_op jit(solution)/shard_map/while/body/eval_jaxpr/qkgd,lkd->qkgl/dot_general | solution.py:170
  253.3 7.2 %fusion.105 = f32[256,1,8,88]{0,3,2,1:T(8,128)S(1)} fusion(f32[2048,256,8]{1,0,2:T(8,128)} %get-tuple-element.240, pred[256,2048]{0,1:T(8,128)(4,1)S(1)} %compare_and_fusion.2, f32[256,1,8,88]{0,3,2,1:T(8,128)S(1)} %get-tuple-element.254, bf16[2048,2,1,88]{0,3,2,1:T(8,128)(2,1)S(1)} %dynamic-slice_bitcast_fusion.2, pred[]{:T(512)S(6)} %compare.49), kind=kOutput, calls=%fused_computation.13.clone.1 | convolution fusion | flops 751140864 | bytes 19103744 | tf_op jit(solution)/shard_map/while/body/eval_jaxpr/qkgl,lkd->qkgd/dot_general | solution.py:180
  261.5 1.4 compare_and_fusion.2
  264.1 7.7 %fusion.104 = (f32[256,8]{0,1:T(8,128)S(1)}, f32[2048,256,8]{1,0,2:T(8,128)}) fusion(pred[256,2048]{0,1:T(8,128)(4,1)S(1)} %compare_and_fusion.2, bf16[256,1,8,88]{0,3,2,1:T(8,128)(2,1)S(1)} %get-tuple-element.271, bf16[2048,2,1,88]{0,3,2,1:T(8,128)(2,1)S(1)} %dynamic-slice_bitcast_fusion.2), kind=kOutput, calls=%fused_computation.6.clone.1 | convolution fusion | flops 750778368 | bytes 18030592 | tf_op jit(solution)/shard_map/while/body/eval_jaxpr/qkgd,lkd->qkgl/dot_general | solution.py:170
  271.7 7.2 %fusion.105 = f32[256,1,8,88]{0,3,2,1:T(8,128)S(1)} fusion(f32[2048,256,8]{1,0,2:T(8,128)} %get-tuple-element.240, pred[256,2048]{0,1:T(8,128)(4,1)S(1)} %compare_and_fusion.2, f32[256,1,8,88]{0,3,2,1:T(8,128)S(1)} %get-tuple-element.254, bf16[2048,2,1,88]{0,3,2,1:T(8,128)(2,1)S(1)} %dynamic-slice_bitcast_fusion.2, pred[]{:T(512)S(6)} %compare.49), kind=kOutput, calls=%fused_computation.13.clone.1 | convolution fusion | flops 751140864 | bytes 19103744 | tf_op jit(solution)/shard_map/while/body/eval_jaxpr/qkgl,lkd->qkgd/dot_general | solution.py:180
  279.9 1.4 compare_and_fusion.2
  282.5 7.7 %fusion.104 = (f32[256,8]{0,1:T(8,128)S(1)}, f32[2048,256,8]{1,0,2:T(8,128)}) fusion(pred[256,2048]{0,1:T(8,128)(4,1)S(1)} %compare_and_fusion.2, bf16[256,1,8,88]{0,3,2,1:T(8,128)(2,1)S(1)} %get-tuple-element.271, bf16[2048,2,1,88]{0,3,2,1:T(8,128)(2,1)S(1)} %dynamic-slice_bitcast_fusion.2), kind=kOutput, calls=%fused_computation.6.clone.1 | convolution fusion | flops 750778368 | bytes 18030592 | tf_op jit(solution)/shard_map/while/body/eval_jaxpr/qkgd,lkd->qkgl/dot_general | solution.py:170
  290.1 7.2 %fusion.105 = f32[256,1,8,88]{0,3,2,1:T(8,128)S(1)} fusion(f32[2048,256,8]{1,0,2:T(8,128)} %get-tuple-element.240, pred[256,2048]{0,1:T(8,128)(4,1)S(1)} %compare_and_fusion.2, f32[256,1,8,88]{0,3,2,1:T(8,128)S(1)} %get-tuple-element.254, bf16[2048,2,1,88]{0,3,2,1:T(8,128)(2,1)S(1)} %dynamic-slice_bitcast_fusion.2, pred[]{:T(512)S(6)} %compare.49), kind=kOutput, calls=%fused_computation.13.clone.1 | convolution fusion | flops 751140864 | bytes 19103744 | tf_op jit(solution)/shard_map/while/body/eval_jaxpr/qkgl,lkd->qkgd/dot_general | solution.py:180
  298.3 1.4 compare_and_fusion.2
  300.9 7.7 %fusion.104 = (f32[256,8]{0,1:T(8,128)S(1)}, f32[2048,256,8]{1,0,2:T(8,128)}) fusion(pred[256,2048]{0,1:T(8,128)(4,1)S(1)} %compare_and_fusion.2, bf16[256,1,8,88]{0,3,2,1:T(8,128)(2,1)S(1)} %get-tuple-element.271, bf16[2048,2,1,88]{0,3,2,1:T(8,128)(2,1)S(1)} %dynamic-slice_bitcast_fusion.2), kind=kOutput, calls=%fused_computation.6.clone.1 | convolution fusion | flops 750778368 | bytes 18030592 | tf_op jit(solution)/shard_map/while/body/eval_jaxpr/qkgd,lkd->qkgl/dot_general | solution.py:170
  308.6 7.2 %fusion.105 = f32[256,1,8,88]{0,3,2,1:T(8,128)S(1)} fusion(f32[2048,256,8]{1,0,2:T(8,128)} %get-tuple-element.240, pred[256,2048]{0,1:T(8,128)(4,1)S(1)} %compare_and_fusion.2, f32[256,1,8,88]{0,3,2,1:T(8,128)S(1)} %get-tuple-element.254, bf16[2048,2,1,88]{0,3,2,1:T(8,128)(2,1)S(1)} %dynamic-slice_bitcast_fusion.2, pred[]{:T(512)S(6)} %compare.49), kind=kOutput, calls=%fused_computation.13.clone.1 | convolution fusion | flops 751140864 | bytes 19103744 | tf_op jit(solution)/shard_map/while/body/eval_jaxpr/qkgl,lkd->qkgd/dot_general | solution.py:180
  315.9 1.7 collective-permute-start.3
  317.6 1.3 collective-permute-done.3
  318.9 5.8 %fusion.48 = bf16[256,1,1408]{2,0,1:T(8,128)(2,1)} fusion(bf16[704,1408]{1,0:T(8,128)(2,1)} %collective-permute-done.4, bf16[704,1408]{1,0:T(8,128)(2,1)} %param.25, pred[]{:T(512)S(6)} %eq.73, bf16[256,1408]{1,0:T(8,128)(2,1)S(1)} %scatter_fusion, bf16[256,704]{0,1:T(8,128)(2,1)S(1)} %collective-permute-done.3, bf16[256,704]{0,1:T(8,128)(2,1)S(1)} %bitcast.200), kind=kOutput, calls=%fused_computation.54 | convolution fusion | flops 1037189120 | bytes 6127617 | tf_op jit(solution)/shard_map/dot_general | solution.py:192
  (112 shorter events, 28.5 us)
Async XLA Ops:
  6.5 73.0 %copy-start = (bf16[1408,704]{0,1:T(8,128)(2,1)S(1)}, bf16[1408,704]{0,1:T(8,128)(2,1)}, u32[]{:S(2)}) copy-start(bf16[1408,704]{0,1:T(8,128)(2,1)} %param.23) | copy-start | bytes 5947396
  6.5 4.8 %copy-start.2 = (bf16[512,1408]{1,0:T(8,128)(2,1)S(1)}, bf16[512,1408]{1,0:T(8,128)(2,1)}, u32[]{:S(2)}) copy-start(bf16[512,1408]{1,0:T(8,128)(2,1)} %param.14) | copy-start | bytes 4325380
  6.5 29.1 %collective-permute-start.1 = (bf16[704,1408]{1,0:T(8,128)(2,1)}, bf16[704,1408]{1,0:T(8,128)(2,1)}, u32[]{:S(2)}, u32[]{:S(2)}) collective-permute-start(bf16[704,1408]{1,0:T(8,128)(2,1)} %param.21), channel_id=1, source_target_pairs={{0,64},{64,0},{1,65},{65,1},{2,66},{66,2},{3,67},{67,3},{4,68},{68... | collective-permute-start | bytes 5947400 | tf_op jit(solution)/shard_map/ppermute | solution.py:45
  17.9 2.0 copy-start.4
  29.8 5.8 %collective-permute-start = (bf16[256,704]{1,0:T(8,128)(2,1)S(1)}, bf16[256,704]{1,0:T(8,128)(2,1)}, u32[]{:S(2)}, u32[]{:S(2)}) collective-permute-start(bf16[256,704]{1,0:T(8,128)(2,1)S(1)} %gather_fusion.2), channel_id=1, source_target_pairs={{0,64},{64,0},{1,65},{65,1},{2,66},{66,2},{3,67},{67,3},{4,68},{68... | collective-permute-start | bytes 1081352 | tf_op jit(solution)/shard_map/ppermute | solution.py:45
  39.8 5.0 %copy-start.8 = (s32[8192]{0:T(1024)S(1)}, s32[8192]{0:T(1024)}, u32[]{:S(2)}) copy-start(s32[8192]{0:T(1024)} %param.17) | copy-start | bytes 98308
  44.3 28.4 %copy-start.3 = (bf16[256,1,1408]{2,0,1:T(8,128)(2,1)S(1)}, bf16[256,1,1408]{2,0,1:T(8,128)(2,1)}, u32[]{:S(2)}) copy-start(bf16[256,1,1408]{2,0,1:T(8,128)(2,1)} %param.18) | copy-start | bytes 2162692
  44.3 3.0 collective-permute-start.2
  50.6 22.1 %all-to-all-start = ((bf16[2,64,1408]{2,0,1:T(2,128)(2,1)}), bf16[2,64,1408]{2,0,1:T(2,128)(2,1)S(1)}, u32[]{:S(2)}, u32[]{:S(2)}) async-start(bf16[2,64,1408]{2,0,1:T(2,128)(2,1)} %fusion.78), calls=%async_computation | async-start | bytes 720896 | tf_op jit(solution)/shard_map/all_to_all | solution.py:123
  61.8 94.4 %all-gather.3.cloned.1.call-start = ((), (), s32[]{:S(2)}) async-start(), calls=%async_computation.1 | async-start | bytes 5857280 | tf_op jit(solution)/shard_map/all_gather | solution.py:156
  74.3 4.5 %copy-start.7 = (s32[256,64]{0,1:T(8,128)S(1)}, s32[256,64]{0,1:T(8,128)}, u32[]{:S(2)}) copy-start(s32[256,64]{0,1:T(8,128)} %param.19) | copy-start | bytes 196612
  76.8 240.8 %collective-permute-start.4 = (bf16[704,1408]{1,0:T(8,128)(2,1)}, bf16[704,1408]{1,0:T(8,128)(2,1)}, u32[]{:S(2)}, u32[]{:S(2)}) collective-permute-start(bf16[704,1408]{1,0:T(8,128)(2,1)} %param.25), channel_id=1, source_target_pairs={{0,64},{64,0},{1,65},{65,1},{2,66},{66,2},{3,67},{67,3},{4,68},{68... | collective-permute-start | bytes 5947400 | tf_op jit(solution)/shard_map/ppermute | solution.py:45
  162.8 5.7 %copy-start.5 = (f32[256,1,8,88]{0,3,2,1:T(8,128)S(1)}, f32[256,1,8,88]{0,3,2,1:T(8,128)}, u32[]{:S(2)}) copy-start(f32[256,1,8,88]{0,3,2,1:T(8,128)} %custom-call) | copy-start | bytes 2162692
  162.8 5.7 %copy-start.6 = (bf16[256,1,8,88]{0,3,2,1:T(8,128)(2,1)S(1)}, bf16[256,1,8,88]{0,3,2,1:T(8,128)(2,1)}, u32[]{:S(2)}) copy-start(bf16[256,1,8,88]{0,3,2,1:T(8,128)(2,1)} %multiply_convert_fusion.4) | copy-start | bytes 1081348
  315.9 3.0 collective-permute-start.3
  318.9 5.8 %copy-start.1 = (bf16[1408,704]{0,1:T(8,128)(2,1)S(1)}, bf16[1408,704]{0,1:T(8,128)(2,1)}, u32[]{:S(2)}) copy-start(bf16[1408,704]{0,1:T(8,128)(2,1)} %param.23) | copy-start | bytes 5947396
Sparse Core Ops, SparseCore 0:
  76.9 79.3 all-gather.2

commit v3 on v1

--- a/solution.py
+++ b/solution.py
@@ -4,10 +4,12 @@
 import jax.numpy as jnp
 from jax import lax
 from jax.sharding import PartitionSpec as P
+from jax.experimental import pallas as pl
+from jax.experimental.pallas import tpu as pltpu
+import functools
 
 D = 1408
 HEAD = 88
-CHUNKS = 4
 
 
 def layer_norm(values):
@@ -40,6 +42,55 @@
     group_col = within % groups_across
     corner = first_patch + 2 * group_row * row_width + 2 * group_col
     return jnp.stack([corner, corner + 1, corner + row_width, corner + row_width + 1], 1)
+
+
+def _text_kernel(q_ref, kv_ref, qpos_ref, qseg_ref, kpos_ref, kseg_ref, o_ref, acc_ref, tot_ref, *, scale):
+    qb = pl.program_id(0)
+    kb = pl.program_id(1)
+    heads, rows, head = q_ref.shape
+
+    @pl.when(kb == 0)
+    def _():
+        acc_ref[...] = jnp.zeros_like(acc_ref)
+        tot_ref[...] = jnp.zeros_like(tot_ref)
+
+    @pl.when(kb <= qb)
+    def _():
+        q = q_ref[...].reshape(heads * rows, head)
+        shards, _, krows, _ = kv_ref.shape
+        k = kv_ref[:, 0].reshape(shards * krows, head)
+        v = kv_ref[:, 1].reshape(shards * krows, head)
+        s = lax.dot_general(q, k, (((1,), (1,)), ((), ())), preferred_element_type=jnp.float32) * scale
+        allowed = (kpos_ref[0] <= qpos_ref[0]) & (kseg_ref[0] == qseg_ref[0])
+        w = jnp.where(allowed, jnp.exp(s), 0.0)
+        tot_ref[...] += jnp.sum(w, -1, keepdims=True)
+        acc_ref[...] += jnp.dot(w.astype(jnp.bfloat16), v, preferred_element_type=jnp.float32)
+
+    @pl.when(kb == pl.num_programs(1) - 1)
+    def _():
+        o_ref[...] = (acc_ref[...] / tot_ref[...]).astype(o_ref.dtype).reshape(o_ref.shape)
+
+
+def text_attention(q, kv, qpos, qseg, kpos, kseg, rows, scale):
+    heads, text_rows, head = q.shape
+    shards = kv.shape[0]
+    blocks = text_rows // rows
+    return pl.pallas_call(
+        functools.partial(_text_kernel, scale=scale),
+        grid=(blocks, blocks),
+        in_specs=[
+            pl.BlockSpec((heads, rows, head), lambda i, j: (0, i, 0)),
+            pl.BlockSpec((shards, 2, rows, head), lambda i, j: (0, 0, jnp.minimum(i, j), 0)),
+            pl.BlockSpec((1, heads * rows, 1), lambda i, j: (i, 0, 0)),
+            pl.BlockSpec((1, heads * rows, 1), lambda i, j: (i, 0, 0)),
+            pl.BlockSpec((1, 1, shards * rows), lambda i, j: (jnp.minimum(i, j), 0, 0)),
+            pl.BlockSpec((1, 1, shards * rows), lambda i, j: (jnp.minimum(i, j), 0, 0)),
+        ],
+        out_specs=pl.BlockSpec((heads, rows, head), lambda i, j: (0, i, 0)),
+        out_shape=jax.ShapeDtypeStruct((heads, text_rows, head), jnp.bfloat16),
+        scratch_shapes=[pltpu.VMEM((heads * rows, head), jnp.float32), pltpu.VMEM((heads * rows, 1), jnp.float32)],
+        compiler_params=pltpu.CompilerParams(dimension_semantics=("arbitrary", "arbitrary")),
+    )(q, kv, qpos, qseg, kpos, kseg)
 
 
 def swap(values):
@@ -145,41 +196,38 @@
     ).reshape(text_rows, 2, HEAD)
     key_rows = root_norm(paired[:, 0]).astype(jnp.bfloat16)
     value_rows = paired[:, 1].astype(jnp.bfloat16)
-    shared = jnp.stack([key_rows, value_rows], 1)
-
+
+    shared = jnp.stack([key_rows, value_rows], 0)[None]
+    piece = lax.all_gather(shared, "seq", axis=0, tiled=True)
+    rows = 32
+    blocks = text_rows // rows
     query_places = jnp.arange(text_rows, dtype=jnp.int32) * seq_count + seq_index
     query_segments = lax.dynamic_slice_in_dim(segment_ids, seq_index, 1, 1)[:, 0]
-    step = text_rows // CHUNKS
-    sums = jnp.zeros((text_rows, local_heads, HEAD), jnp.float32)
-    totals = jnp.zeros((text_rows, local_heads), jnp.float32)
-    for chunk in range(CHUNKS):
-        low = chunk * step
-        piece = lax.all_gather(shared[None, low : low + step], "seq", axis=0, tiled=True)
-        piece = piece.reshape(seq_count * step, 2, HEAD)
-        key_places = (
-            jnp.arange(seq_count, dtype=jnp.int32)[:, None]
-            + (low + jnp.arange(step, dtype=jnp.int32))[None, :] * seq_count
-        ).reshape(-1)
-        key_segments = jnp.transpose(segment_ids[low : low + step]).reshape(-1)
-        chunk_queries = text_queries[low:]
-        scores = (
-            jnp.einsum("qgd,ld->qgl", chunk_queries, piece[:, 0], preferred_element_type=jnp.float32)
-            * scale
+
+    def per_query_row(values):
+        spread = jnp.broadcast_to(values.reshape(blocks, 1, rows), (blocks, local_heads, rows))
+        return spread.reshape(blocks, local_heads * rows, 1)
+
+    def per_key(values):
+        return jnp.transpose(values.reshape(seq_count, blocks, rows), (1, 0, 2)).reshape(
+            blocks, 1, seq_count * rows
         )
-        allowed = (key_places[None, :] <= query_places[low:, None]) & (
-            key_segments[None, :] == query_segments[low:, None]
-        )
-        weights = jnp.where(allowed[:, None, :], jnp.exp(scores), jnp.zeros_like(scores))
-        totals = totals.at[low:].add(jnp.sum(weights, -1))
-        sums = sums.at[low:].add(
-            jnp.einsum(
-                "qgl,ld->qgd",
-                weights.astype(jnp.bfloat16),
-                piece[:, 1],
-                preferred_element_type=jnp.float32,
-            )
-        )
-    attended_text = (sums / totals[..., None]).astype(jnp.bfloat16).reshape(text_rows, -1)
+
+    key_places = (
+        jnp.arange(text_rows, dtype=jnp.int32)[None, :] * seq_count
+        + jnp.arange(seq_count, dtype=jnp.int32)[:, None]
+    )
+    head_major = text_attention(
+        jnp.transpose(text_queries, (1, 0, 2)),
+        piece,
+        per_query_row(query_places),
+        per_query_row(query_segments),
+        per_key(key_places),
+        per_key(jnp.transpose(segment_ids)),
+        rows,
+        scale,
+    )
+    attended_text = jnp.transpose(head_major, (1, 0, 2)).reshape(text_rows, -1)
     all_heads = in_head_order(first, attended_text, swap(attended_text), 1)
     output_terms = jnp.dot(all_heads, decoder_out_full, preferred_element_type=jnp.float32)
     decoded = (prompt.astype(jnp.float32) + output_terms).astype(jnp.bfloat16)

time: 401 us -> 228 us (0.57); the launches traced: 394 us -> 227 us
  waiting for transfers between devices: 145 us -> 66.7 us
  local copies, waits for them, and re-layouts: 102 us -> 30.9 us
  matrix products: 98 us -> 29.6 us
  Pallas kernels: 0 us -> 56 us
  other arithmetic: 15.7 us -> 10.9 us
    all_gather x4 -> x1, waiting for transfers between devices: 133 us -> 54.7 us  [body(): piece = lax.all_gather(shared, 'seq', axis=0, tiled=True)]
    dot_general x8 -> x0, matrix products: 67.9 us -> none  [the longest x4 38.2 us: body(): jnp.einsum('qgd,ld->qgl', chunk_queries, piece[:, 0], preferred_element_t...]
    pallas_call x0 -> x1, Pallas kernels: none -> 56 us  [text_attention(): pl.pallas_call(functools.partial(_text_kernel, scale=scale), grid=(blocks...]
    unnamed x44 -> x13, local copies, waits for them, and re-layouts: 43.9 us -> 2.09 us
    slice x15 -> x0, local copies, waits for them, and re-layouts: 31 us -> none  [the longest x4 27.8 us: body(): piece[:, 1]]
    scatter-add x4 -> x0, local copies, waits for them, and re-layouts: 12.5 us -> none  [the longest x2 12.1 us: body(): sums.at[low:]]
    all_gather x0 -> x1, local copies, waits for them, and re-layouts: none -> 9.83 us  [body(): piece = lax.all_gather(shared, 'seq', axis=0, tiled=True)]
    and x4 -> x0, other arithmetic: 5.81 us -> none  [body(): (key_places[None, :] <= query_places[low:, None]) & (key_segments[None, :...]
  transfers between devices with their start and end apart: 10 -> 7, of which waited for: 5 -> 3; matrix products, arithmetic and copies ran while one was open for 48% -> 21% of each run, Pallas kernels for 0% -> 25%
where the time goes in v3:
time: 228 us; the launch traced here: 227 us
  waiting for transfers between devices  66.7 us (29%)
  Pallas kernels  56 us (25%)
  local copies, waits for them, and re-layouts  30.9 us (14%)
  matrix products  29.6 us (13%)
  starting transfers between devices  16.8 us (7%)
  between operations  15.7 us (7%)
  other arithmetic  10.9 us (5%)
    pallas_call x1, Pallas kernels, text_attention(): pl.pallas_call(functools.partial(_text_kernel, scale=scale), grid=(blocks...  56 us
    all_gather x1, waiting for transfers between devices, body(): piece = lax.all_gather(shared, 'seq', axis=0, tiled=True)  54.7 us
    all_to_all x1, starting transfers between devices, body(): lax.all_to_all(jnp.roll(image_rows.reshape(per_peer, seq_count, image_row...  11.2 us
    all_to_all x1, waiting for transfers between devices, body(): lax.all_to_all(jnp.roll(image_rows.reshape(per_peer, seq_count, image_row...  10.6 us
    all_gather x1, local copies, waits for them, and re-layouts, body(): piece = lax.all_gather(shared, 'seq', axis=0, tiled=True)  9.83 us
    dot_general x1, matrix products, body(): jnp.dot(normed, vision_qkv.reshape(D, -1), preferred_element_type=jnp.flo...  5.99 us
    dot_general x1, matrix products, body(): jnp.dot(all_heads, decoder_out_full, preferred_element_type=jnp.float32)  5.62 us
    ppermute x5, starting transfers between devices, swap(): return lax.ppermute(values, 'section', [(0, 1), (1, 0)])  5.59 us
  transfers between devices with their start and end apart: 7, of which 3 were waited for; matrix products, arithmetic and copies ran while one was open for 21% of the time, Pallas kernels for 25%

profile of v3, /device:TPU:1, one launch (start us, length us, event | category | flops | bytes accessed | tf_op | source)
XLA Modules:
  0.0 226.6 jit_solution(2056598850977350990)
XLA Ops:
  6.5 1.4 collective-permute-start.1
  8.0 0.7 slice_bitcast_fusion.2
  8.6 0.8 fusion.73
  9.6 0.1 broadcast_add_fusion.3
  9.7 1.6 convert_reduce_fusion
  11.4 0.5 fusion.20
  11.9 6.0 %fusion.37 = f32[512,3,8,88]{0,3,2,1:T(8,128)S(1)} fusion(bf16[3,8,88,1408]{3,2,1,0:T(8,128)(2,1)} %bitcast.129, bf16[512,1408]{1,0:T(8,128)(2,1)S(1)} %copy-done.1, f32[512]{0:T(512)S(1)} %add_rsqrt_fusion.3, f32[512]{0:T(512)S(1)} %broadcast_multiply_fusion), kind=kOutput, calls=%fused_computation.40 | convolution fusion | flops 3047948288 | bytes 11718656 | tf_op jit(solution)/shard_map/dot_general | solution.py:133
  17.9 2.0 copy-done.3
  19.9 0.4 multiply_reduce_fusion.1
  20.3 0.2 broadcast_compare_fusion
  20.9 0.1 reshape.601
  21.1 4.1 %fusion = (f32[8,512]{1,0:T(8,128)S(1)}, f32[8,512,512]{1,2,0:T(8,128)S(1)}) fusion(pred[512,512]{0,1:T(8,128)(4,1)S(1)} %broadcast_compare_fusion, f32[512,3,8,88]{0,3,2,1:T(8,128)} %copy-done.3, f32[512,8]{0,1:T(8,128)S(1)} %get-tuple-element.25, f32[512,8]{0,1:T(8,128)S(1)} %get-tuple-element.26), kind=kOutput, calls=%fused_computation.5 | convolution fusion | flops 376827904 | bytes 11583488 | tf_op jit(solution)/shard_map/qhd,khd->hqk/dot_general | solution.py:143
  25.2 3.1 %divide_convert_fusion = bf16[512,8,88]{0,2,1:T(8,128)(2,1)S(1)} fusion(f32[8,512,512]{1,2,0:T(8,128)S(1)} %get-tuple-element.22, pred[512,512]{0,1:T(8,128)(4,1)S(1)} %broadcast_compare_fusion, f32[512,3,8,88]{0,3,2,1:T(8,128)} %copy-done.3, f32[512,8]{0,1:T(8,128)S(1)} %bitcast.130), kind=kOutput, calls=%fused_computation.44 | convolution fusion | flops 376111104 | bytes 10108928 | tf_op jit(solution)/shard_map/hqk,khd->qhd/dot_general | solution.py:147
  28.3 0.3 copy.82
  28.7 1.2 gather_fusion.2
  29.8 0.4 collective-permute-start
  30.3 1.9 gather_fusion.1
  32.2 3.5 %gather_fusion = bf16[256,1408]{1,0:T(8,128)(2,1)S(1)} fusion(bf16[512,1408]{1,0:T(8,128)(2,1)} %param.12, s32[1024]{0:T(1024)S(1)} %pad_clamp_fusion.1), kind=kCustom, calls=%fused_computation | custom fusion | bytes 1442816 | tf_op jit(solution)/shard_map/gather | solution.py:162
  35.7 3.8 %fusion.26 = bf16[256,1408]{1,0:T(8,128)(2,1)S(1)} fusion(bf16[704,1408]{1,0:T(8,128)(2,1)} %collective-permute-done.1, bf16[704,1408]{1,0:T(8,128)(2,1)} %param.19, bf16[256,1408]{1,0:T(8,128)(2,1)S(1)} %gather_fusion, bf16[256,704]{1,0:T(8,128)(2,1)} %collective-permute-done, bf16[256,704]{1,0:T(8,128)(2,1)} %gather_fusion.1), kind=kOutput, calls=%fused_computation.31 | convolution fusion | flops 1025474560 | bytes 6127616 | tf_op jit(solution)/shard_map/dot_general | solution.py:163
  39.5 0.2 reshape.602
  39.8 4.5 %fusion.80 = f32[128,1408]{1,0:T(8,128)S(1)} fusion(bf16[128,2816]{1,0:T(8,128)(2,1)S(1)} %reshape.602, bf16[2816,1408]{1,0:T(8,128)(2,1)} %bitcast.115), kind=kOutput, calls=%fused_computation.156 | convolution fusion | flops 1015021568 | bytes 9371648 | tf_op jit(solution)/shard_map/dot_general | solution.py:165
  44.3 0.4 collective-permute-start.2
  44.9 0.5 constant_dynamic-slice_fusion.1
  47.4 1.2 add_convert_fusion
  48.6 0.4 copy.85
  48.9 1.7 fusion.61
  50.6 11.2 %all-to-all-start = ((bf16[2,64,1408]{2,0,1:T(2,128)(2,1)}), bf16[2,64,1408]{2,0,1:T(2,128)(2,1)S(1)}, u32[]{:S(2)}, u32[]{:S(2)}) async-start(bf16[2,64,1408]{2,0,1:T(2,128)(2,1)} %fusion.61), calls=%async_computation | async-start | bytes 720896 | tf_op jit(solution)/shard_map/all_to_all | solution.py:175
  62.1 10.6 %all-to-all-done = bf16[2,64,1408]{2,0,1:T(2,128)(2,1)S(1)} async-done(((bf16[2,64,1408]{2,0,1:T(2,128)(2,1)}), bf16[2,64,1408]{2,0,1:T(2,128)(2,1)S(1)}, u32[]{:S(2)}, u32[]{:S(2)}) %all-to-all-start) | async-done | bytes 360480 | tf_op jit(solution)/shard_map/all_to_all | solution.py:175
  72.7 1.6 scatter_fusion
  74.3 0.2 fusion.34
  74.6 1.5 fusion.54
  76.1 0.7 pad_maximum_fusion
  76.8 2.0 collective-permute-start.4
  79.0 2.1 reshape.650.qseg_ref
  81.1 2.1 reshape.649.qpos_ref
  83.3 0.8 reshape.651.kseg_ref
  84.1 0.2 add.413
  84.4 0.7 broadcast_add_fusion.kpos_ref
  85.1 0.8 fusion.63
  85.9 1.3 copy.88
  87.3 2.4 %fusion.59.q_ref = bf16[8,256,88]{2,1,0:T(8,128)(2,1)} fusion(f32[256,8,88]{2,0,1:T(8,128)} %copy.88, f32[256,8]{0,1:T(8,128)S(1)} %add_rsqrt_fusion.2), kind=kLoop, calls=%fused_computation.72 | loop fusion | flops 360448 | bytes 1089536 | tf_op jit(solution)/shard_map/transpose | solution.py:221
  89.7 54.7 %all-gather.3.cloned.1.call-done = bf16[128,256,88]{1,2,0:T(8,128)(2,1)} async-done(((bf16[2,256,88]{1,2,0:T(8,128)(2,1)}), bf16[128,256,88]{1,2,0:T(8,128)(2,1)}) %all-gather.3.cloned.1.call-update) | async-done | bytes 5767184 | tf_op jit(solution)/shard_map/all_gather | solution.py:201
  144.4 9.8 %copy.89 = bf16[128,256,88]{2,1,0:T(8,128)(2,1)} copy(bf16[128,256,88]{1,2,0:T(8,128)(2,1)} %all-gather.3.cloned.1.call-done) | data formatting | bytes 11534336 | tf_op jit(solution)/shard_map/all_gather | solution.py:201
  154.3 56.0 %shard_map.118 = bf16[8,256,88]{2,1,0:T(8,128)(2,1)} custom-call(bf16[8,256,88]{2,1,0:T(8,128)(2,1)} %fusion.59.q_ref, bf16[64,2,256,88]{3,2,1,0:T(8,128)(2,1)} %bitcast.114, s32[8,256,1]{2,1,0:T(8,128)} %reshape.649.qpos_ref, s32[8,256,1]{2,1,0:T(8,128)} %reshape.650.qseg_ref, s32[8,1,2048]{2,1,0:T(1,128)} %broadcast_add_fusion.kpos_ref, ...), custom_call_target="tpu_custom_call" | custom-call | tf_op jit(solution)/shard_map/pallas_call | solution.py:78
  210.3 1.2 copy.97
  211.5 1.3 collective-permute-start.3
  212.8 1.3 collective-permute-done.3
  214.1 5.6 %fusion.30 = bf16[256,1,1408]{2,0,1:T(8,128)(2,1)} fusion(bf16[704,1408]{1,0:T(8,128)(2,1)} %collective-permute-done.4, bf16[704,1408]{1,0:T(8,128)(2,1)} %param.23, pred[]{:T(512)S(6)} %eq.52, bf16[256,1408]{1,0:T(8,128)(2,1)S(1)} %scatter_fusion, bf16[256,704]{0,1:T(8,128)(2,1)S(1)} %collective-permute-done.3, bf16[256,704]{0,1:T(8,128)(2,1)S(1)} %bitcast.125), kind=kOutput, calls=%fused_computation.33 | convolution fusion | flops 1037189120 | bytes 6127617 | tf_op jit(solution)/shard_map/dot_general | solution.py:232
  (56 shorter events, 1.6 us)
Async XLA Ops:
  6.5 78.5 %copy-start = (bf16[1408,704]{0,1:T(8,128)(2,1)S(1)}, bf16[1408,704]{0,1:T(8,128)(2,1)}, u32[]{:S(2)}) copy-start(bf16[1408,704]{0,1:T(8,128)(2,1)} %param.21) | copy-start | bytes 5947396
  6.5 4.8 %copy-start.1 = (bf16[512,1408]{1,0:T(8,128)(2,1)S(1)}, bf16[512,1408]{1,0:T(8,128)(2,1)}, u32[]{:S(2)}) copy-start(bf16[512,1408]{1,0:T(8,128)(2,1)} %param.12) | copy-start | bytes 4325380
  6.5 29.1 %collective-permute-start.1 = (bf16[704,1408]{1,0:T(8,128)(2,1)}, bf16[704,1408]{1,0:T(8,128)(2,1)}, u32[]{:S(2)}, u32[]{:S(2)}) collective-permute-start(bf16[704,1408]{1,0:T(8,128)(2,1)} %param.19), channel_id=1, source_target_pairs={{0,64},{64,0},{1,65},{65,1},{2,66},{66,2},{3,67},{67,3},{4,68},{68... | collective-permute-start | bytes 5947400 | tf_op jit(solution)/shard_map/ppermute | solution.py:97
  17.9 2.0 copy-start.3
  29.8 5.8 %collective-permute-start = (bf16[256,704]{1,0:T(8,128)(2,1)S(1)}, bf16[256,704]{1,0:T(8,128)(2,1)}, u32[]{:S(2)}, u32[]{:S(2)}) collective-permute-start(bf16[256,704]{1,0:T(8,128)(2,1)S(1)} %gather_fusion.2), channel_id=1, source_target_pairs={{0,64},{64,0},{1,65},{65,1},{2,66},{66,2},{3,67},{67,3},{4,68},{68... | collective-permute-start | bytes 1081352 | tf_op jit(solution)/shard_map/ppermute | solution.py:97
  39.8 5.0 %copy-start.5 = (s32[8192]{0:T(1024)S(1)}, s32[8192]{0:T(1024)}, u32[]{:S(2)}) copy-start(s32[8192]{0:T(1024)} %param.15) | copy-start | bytes 98308
  44.3 28.4 %copy-start.2 = (bf16[256,1,1408]{2,0,1:T(8,128)(2,1)S(1)}, bf16[256,1,1408]{2,0,1:T(8,128)(2,1)}, u32[]{:S(2)}) copy-start(bf16[256,1,1408]{2,0,1:T(8,128)(2,1)} %param.16) | copy-start | bytes 2162692
  44.3 3.0 %collective-permute-start.2 = (f32[128,1408]{1,0:T(8,128)S(1)}, f32[128,1408]{1,0:T(8,128)}, u32[]{:S(2)}, u32[]{:S(2)}) collective-permute-start(f32[128,1408]{1,0:T(8,128)S(1)} %fusion.80), channel_id=1, source_target_pairs={{0,64},{64,0},{1,65},{65,1},{2,66},{66,2},{3,67},{67,3},{4,68},{68... | collective-permute-start | bytes 2162696 | tf_op jit(solution)/shard_map/ppermute | solution.py:97
  50.6 22.1 %all-to-all-start = ((bf16[2,64,1408]{2,0,1:T(2,128)(2,1)}), bf16[2,64,1408]{2,0,1:T(2,128)(2,1)S(1)}, u32[]{:S(2)}, u32[]{:S(2)}) async-start(bf16[2,64,1408]{2,0,1:T(2,128)(2,1)} %fusion.61), calls=%async_computation | async-start | bytes 720896 | tf_op jit(solution)/shard_map/all_to_all | solution.py:175
  61.8 82.6 %all-gather.3.cloned.1.call-start = ((), (), s32[]{:S(2)}) async-start(), calls=%async_computation.1 | async-start | bytes 5857280 | tf_op jit(solution)/shard_map/all_gather | solution.py:201
  74.3 4.5 %copy-start.4 = (s32[256,64]{0,1:T(8,128)S(1)}, s32[256,64]{0,1:T(8,128)}, u32[]{:S(2)}) copy-start(s32[256,64]{0,1:T(8,128)} %param.17) | copy-start | bytes 196612
  76.8 136.0 %collective-permute-start.4 = (bf16[704,1408]{1,0:T(8,128)(2,1)}, bf16[704,1408]{1,0:T(8,128)(2,1)}, u32[]{:S(2)}, u32[]{:S(2)}) collective-permute-start(bf16[704,1408]{1,0:T(8,128)(2,1)} %param.23), channel_id=1, source_target_pairs={{0,64},{64,0},{1,65},{65,1},{2,66},{66,2},{3,67},{67,3},{4,68},{68... | collective-permute-start | bytes 5947400 | tf_op jit(solution)/shard_map/ppermute | solution.py:97
  211.5 2.6 %collective-permute-start.3 = (bf16[256,704]{0,1:T(8,128)(2,1)S(1)}, bf16[256,704]{0,1:T(8,128)(2,1)S(1)}, u32[]{:S(2)}, u32[]{:S(2)}) collective-permute-start(bf16[256,704]{0,1:T(8,128)(2,1)S(1)} %bitcast.124), channel_id=1, source_target_pairs={{0,64},{64,0},{1,65},{65,1},{2,66},{66,2},{3,67},{67,3},{4,68},{68... | collective-permute-start | bytes 1081352 | tf_op jit(solution)/shard_map/ppermute | solution.py:97
Sparse Core Ops, SparseCore 0:
  76.9 67.4 all-gather.2

commit v4 on v3

--- a/solution.py
+++ b/solution.py
@@ -44,53 +44,93 @@
     return jnp.stack([corner, corner + 1, corner + row_width, corner + row_width + 1], 1)
 
 
-def _text_kernel(q_ref, kv_ref, qpos_ref, qseg_ref, kpos_ref, kseg_ref, o_ref, acc_ref, tot_ref, *, scale):
+def _segment_start(info_ref, places):
+    start = jnp.zeros_like(places) + info_ref[0]
+    for doc in range(1, 4):
+        bound = info_ref[doc]
+        start = jnp.where(places >= bound, bound, start)
+    return start
+
+
+def _text_kernel(info_ref, q_ref, kv_ref, o_ref, acc_ref, tot_ref, *, scale):
     qb = pl.program_id(0)
     kb = pl.program_id(1)
     heads, rows, head = q_ref.shape
+    shards = kv_ref.shape[0]
+    span = rows * shards
+    own = info_ref[4]
+    first_query = qb * span + own
+    last_query = first_query + (rows - 1) * shards
+    first_block = _segment_start(info_ref, first_query) // span
+    active = (kb >= first_block) & (kb <= qb)
+    unmasked = (kb < qb) & (kb * span >= _segment_start(info_ref, last_query))
 
     @pl.when(kb == 0)
     def _():
         acc_ref[...] = jnp.zeros_like(acc_ref)
         tot_ref[...] = jnp.zeros_like(tot_ref)
 
-    @pl.when(kb <= qb)
-    def _():
+    def accumulate(masked):
         q = q_ref[...].reshape(heads * rows, head)
-        shards, _, krows, _ = kv_ref.shape
-        k = kv_ref[:, 0].reshape(shards * krows, head)
-        v = kv_ref[:, 1].reshape(shards * krows, head)
-        s = lax.dot_general(q, k, (((1,), (1,)), ((), ())), preferred_element_type=jnp.float32) * scale
-        allowed = (kpos_ref[0] <= qpos_ref[0]) & (kseg_ref[0] == qseg_ref[0])
-        w = jnp.where(allowed, jnp.exp(s), 0.0)
+        k = kv_ref[:, 0].reshape(span, head)
+        v = kv_ref[:, 1].reshape(span, head)
+        s = lax.dot_general(q, k, (((1,), (1,)), ((), ())), preferred_element_type=jnp.float32)
+        w = jnp.exp(s * scale)
+        if masked:
+            row = lax.broadcasted_iota(jnp.int32, (heads * rows, 1), 0) & (rows - 1)
+            query_places = (qb * rows + row) * shards + own
+            lane = lax.broadcasted_iota(jnp.int32, (1, span), 1)
+            key_places = (kb * rows + (lane & (rows - 1))) * shards + lax.shift_right_logical(
+                lane, rows.bit_length() - 1
+            )
+            allowed = (key_places <= query_places) & (
+                key_places >= _segment_start(info_ref, query_places)
+            )
+            w = jnp.where(allowed, w, 0.0)
         tot_ref[...] += jnp.sum(w, -1, keepdims=True)
         acc_ref[...] += jnp.dot(w.astype(jnp.bfloat16), v, preferred_element_type=jnp.float32)
 
+    @pl.when(active & unmasked)
+    def _():
+        accumulate(False)
+
+    @pl.when(active & jnp.logical_not(unmasked))
+    def _():
+        accumulate(True)
+
     @pl.when(kb == pl.num_programs(1) - 1)
     def _():
         o_ref[...] = (acc_ref[...] / tot_ref[...]).astype(o_ref.dtype).reshape(o_ref.shape)
 
 
-def text_attention(q, kv, qpos, qseg, kpos, kseg, rows, scale):
+def text_attention(info, q, kv, rows, scale):
     heads, text_rows, head = q.shape
     shards = kv.shape[0]
     blocks = text_rows // rows
+    span = rows * shards
+
+    def kv_block(i, j, info_ref):
+        first_block = _segment_start(info_ref, i * span + info_ref[4]) // span
+        return (0, 0, jnp.maximum(jnp.minimum(i, j), first_block), 0)
+
     return pl.pallas_call(
         functools.partial(_text_kernel, scale=scale),
-        grid=(blocks, blocks),
-        in_specs=[
-            pl.BlockSpec((heads, rows, head), lambda i, j: (0, i, 0)),
-            pl.BlockSpec((shards, 2, rows, head), lambda i, j: (0, 0, jnp.minimum(i, j), 0)),
-            pl.BlockSpec((1, heads * rows, 1), lambda i, j: (i, 0, 0)),
-            pl.BlockSpec((1, heads * rows, 1), lambda i, j: (i, 0, 0)),
-            pl.BlockSpec((1, 1, shards * rows), lambda i, j: (jnp.minimum(i, j), 0, 0)),
-            pl.BlockSpec((1, 1, shards * rows), lambda i, j: (jnp.minimum(i, j), 0, 0)),
-        ],
-        out_specs=pl.BlockSpec((heads, rows, head), lambda i, j: (0, i, 0)),
+        grid_spec=pltpu.PrefetchScalarGridSpec(
+            num_scalar_prefetch=1,
+            grid=(blocks, blocks),
+            in_specs=[
+                pl.BlockSpec((heads, rows, head), lambda i, j, info_ref: (0, i, 0)),
+                pl.BlockSpec((shards, 2, rows, head), kv_block),
+            ],
+            out_specs=pl.BlockSpec((heads, rows, head), lambda i, j, info_ref: (0, i, 0)),
+            scratch_shapes=[
+                pltpu.VMEM((heads * rows, head), jnp.float32),
+                pltpu.VMEM((heads * rows, 1), jnp.float32),
+            ],
+        ),
         out_shape=jax.ShapeDtypeStruct((heads, text_rows, head), jnp.bfloat16),
-        scratch_shapes=[pltpu.VMEM((heads * rows, head), jnp.float32), pltpu.VMEM((heads * rows, 1), jnp.float32)],
         compiler_params=pltpu.CompilerParams(dimension_semantics=("arbitrary", "arbitrary")),
-    )(q, kv, qpos, qseg, kpos, kseg)
+    )(info, q, kv)
 
 
 def swap(values):
@@ -200,33 +240,14 @@
     shared = jnp.stack([key_rows, value_rows], 0)[None]
     piece = lax.all_gather(shared, "seq", axis=0, tiled=True)
     rows = 32
-    blocks = text_rows // rows
-    query_places = jnp.arange(text_rows, dtype=jnp.int32) * seq_count + seq_index
-    query_segments = lax.dynamic_slice_in_dim(segment_ids, seq_index, 1, 1)[:, 0]
-
-    def per_query_row(values):
-        spread = jnp.broadcast_to(values.reshape(blocks, 1, rows), (blocks, local_heads, rows))
-        return spread.reshape(blocks, local_heads * rows, 1)
-
-    def per_key(values):
-        return jnp.transpose(values.reshape(seq_count, blocks, rows), (1, 0, 2)).reshape(
-            blocks, 1, seq_count * rows
-        )
-
-    key_places = (
-        jnp.arange(text_rows, dtype=jnp.int32)[None, :] * seq_count
-        + jnp.arange(seq_count, dtype=jnp.int32)[:, None]
-    )
-    head_major = text_attention(
-        jnp.transpose(text_queries, (1, 0, 2)),
-        piece,
-        per_query_row(query_places),
-        per_query_row(query_segments),
-        per_key(key_places),
-        per_key(jnp.transpose(segment_ids)),
-        rows,
-        scale,
-    )
+    doc_starts = jnp.sum(
+        (segment_ids[None] < jnp.arange(4, dtype=jnp.int32)[:, None, None]).astype(jnp.int32),
+        (1, 2),
+    )
+    info = jnp.concatenate(
+        [doc_starts, jnp.full((1,), seq_index, jnp.int32), jnp.zeros((3,), jnp.int32)]
+    )
+    head_major = text_attention(info, jnp.transpose(text_queries, (1, 0, 2)), piece, rows, scale)
     attended_text = jnp.transpose(head_major, (1, 0, 2)).reshape(text_rows, -1)
     all_heads = in_head_order(first, attended_text, swap(attended_text), 1)
     output_terms = jnp.dot(all_heads, decoder_out_full, preferred_element_type=jnp.float32)

time: 228 us -> 212 us (0.930)
  Pallas kernels: 56 us -> 40.5 us
  local copies, waits for them, and re-layouts: 30.9 us -> 25.4 us
  waiting for transfers between devices: 66.7 us -> 72.2 us
    pallas_call x1, Pallas kernels: 56 us -> 40.5 us  [text_attention(): pl.pallas_call(functools.partial(_text_kernel, scale=scale), grid_spec=pl...]
    all_gather x1, waiting for transfers between devices: 54.7 us -> 60.2 us  [body(): piece = lax.all_gather(shared, 'seq', axis=0, tiled=True)]
    reshape x3 -> x0, local copies, waits for them, and re-layouts: 4.94 us -> none  [the longest x2 4.14 us: per_query_row(): return spread.reshape(blocks, local_heads * rows, 1)]
  transfers between devices with their start and end apart: 7 -> 7, of which waited for: 3 -> 3; matrix products, arithmetic and copies ran while one was open for 21% -> 20% of each run, Pallas kernels for 25% -> 19%
where the time goes in v4:
time: 212 us; the launch traced here: 211 us
  waiting for transfers between devices  72.2 us (34%)
  Pallas kernels  40.5 us (19%)
  matrix products  29.6 us (14%)
  local copies, waits for them, and re-layouts  25.4 us (12%)
  starting transfers between devices  16.8 us (8%)
  between operations  15.7 us (7%)
  other arithmetic  11 us (5%)
    all_gather x1, waiting for transfers between devices, body(): piece = lax.all_gather(shared, 'seq', axis=0, tiled=True)  60.2 us
    pallas_call x1, Pallas kernels, text_attention(): pl.pallas_call(functools.partial(_text_kernel, scale=scale), grid_spec=pl...  40.5 us
    all_to_all x1, starting transfers between devices, body(): lax.all_to_all(jnp.roll(image_rows.reshape(per_peer, seq_count, image_row...  11.2 us
    all_to_all x1, waiting for transfers between devices, body(): lax.all_to_all(jnp.roll(image_rows.reshape(per_peer, seq_count, image_row...  10.6 us
    all_gather x1, local copies, waits for them, and re-layouts, body(): piece = lax.all_gather(shared, 'seq', axis=0, tiled=True)  9.83 us
    dot_general x1, matrix products, body(): jnp.dot(normed, vision_qkv.reshape(D, -1), preferred_element_type=jnp.flo...  5.99 us
    dot_general x1, matrix products, body(): jnp.dot(all_heads, decoder_out_full, preferred_element_type=jnp.float32)  5.62 us
    ppermute x5, starting transfers between devices, swap(): return lax.ppermute(values, 'section', [(0, 1), (1, 0)])  5.57 us
  transfers between devices with their start and end apart: 7, of which 3 were waited for; matrix products, arithmetic and copies ran while one was open for 20% of the time, Pallas kernels for 19%

profile of v4, /device:TPU:1, one launch (start us, length us, event | category | flops | bytes accessed | tf_op | source)
XLA Modules:
  0.0 211.0 jit_solution(8280279998393701365)
XLA Ops:
  6.5 1.4 collective-permute-start.1
  8.0 0.7 slice_bitcast_fusion.2
  8.6 0.8 fusion.72
  9.6 0.1 broadcast_add_fusion.1
  9.7 1.6 convert_reduce_fusion
  11.4 0.5 fusion.20
  11.9 6.0 %fusion.37 = f32[512,3,8,88]{0,3,2,1:T(8,128)S(1)} fusion(bf16[3,8,88,1408]{3,2,1,0:T(8,128)(2,1)} %bitcast.124, bf16[512,1408]{1,0:T(8,128)(2,1)S(1)} %copy-done.1, f32[512]{0:T(512)S(1)} %add_rsqrt_fusion.3, f32[512]{0:T(512)S(1)} %broadcast_multiply_fusion), kind=kOutput, calls=%fused_computation.40 | convolution fusion | flops 3047948288 | bytes 11718656 | tf_op jit(solution)/shard_map/dot_general | solution.py:173
  17.9 2.0 copy-done.3
  19.9 0.4 multiply_reduce_fusion.1
  20.3 0.2 broadcast_compare_fusion
  20.6 0.1 copy.48
  20.7 0.1 reshape.537
  20.8 0.1 copy.51
  20.9 0.1 reshape.540
  21.1 4.1 %fusion = (f32[8,512]{1,0:T(8,128)S(1)}, f32[8,512,512]{1,2,0:T(8,128)S(1)}) fusion(pred[512,512]{0,1:T(8,128)(4,1)S(1)} %broadcast_compare_fusion, f32[512,3,8,88]{0,3,2,1:T(8,128)} %copy-done.3, f32[512,8]{0,1:T(8,128)S(1)} %get-tuple-element.25, f32[512,8]{0,1:T(8,128)S(1)} %get-tuple-element.26), kind=kOutput, calls=%fused_computation.5 | convolution fusion | flops 376827904 | bytes 11583488 | tf_op jit(solution)/shard_map/qhd,khd->hqk/dot_general | solution.py:183
  25.2 3.1 %divide_convert_fusion = bf16[512,8,88]{0,2,1:T(8,128)(2,1)S(1)} fusion(f32[8,512,512]{1,2,0:T(8,128)S(1)} %get-tuple-element.22, pred[512,512]{0,1:T(8,128)(4,1)S(1)} %broadcast_compare_fusion, f32[512,3,8,88]{0,3,2,1:T(8,128)} %copy-done.3, f32[512,8]{0,1:T(8,128)S(1)} %bitcast.125), kind=kOutput, calls=%fused_computation.44 | convolution fusion | flops 376111104 | bytes 10108928 | tf_op jit(solution)/shard_map/hqk,khd->qhd/dot_general | solution.py:187
  28.3 0.3 copy.50
  28.7 1.2 gather_fusion.2
  29.8 0.4 collective-permute-start
  30.3 1.9 gather_fusion.1
  32.2 3.5 %gather_fusion = bf16[256,1408]{1,0:T(8,128)(2,1)S(1)} fusion(bf16[512,1408]{1,0:T(8,128)(2,1)} %param.12, s32[1024]{0:T(1024)S(1)} %pad_clamp_fusion.1), kind=kCustom, calls=%fused_computation | custom fusion | bytes 1442816 | tf_op jit(solution)/shard_map/gather | solution.py:202
  35.7 3.8 %fusion.26 = bf16[256,1408]{1,0:T(8,128)(2,1)S(1)} fusion(bf16[704,1408]{1,0:T(8,128)(2,1)} %collective-permute-done.1, bf16[704,1408]{1,0:T(8,128)(2,1)} %param.19, bf16[256,1408]{1,0:T(8,128)(2,1)S(1)} %gather_fusion, bf16[256,704]{1,0:T(8,128)(2,1)} %collective-permute-done, bf16[256,704]{1,0:T(8,128)(2,1)} %gather_fusion.1), kind=kOutput, calls=%fused_computation.31 | convolution fusion | flops 1025474560 | bytes 6127616 | tf_op jit(solution)/shard_map/dot_general | solution.py:203
  39.5 0.2 reshape.541
  39.8 4.5 %fusion.79 = f32[128,1408]{1,0:T(8,128)S(1)} fusion(bf16[128,2816]{1,0:T(8,128)(2,1)S(1)} %reshape.541, bf16[2816,1408]{1,0:T(8,128)(2,1)} %bitcast.111), kind=kOutput, calls=%fused_computation.154 | convolution fusion | flops 1015021568 | bytes 9371648 | tf_op jit(solution)/shard_map/dot_general | solution.py:205
  44.3 0.4 collective-permute-start.2
  44.9 0.5 constant_dynamic-slice_fusion
  47.4 1.2 add_convert_fusion
  48.6 0.4 copy.53
  48.9 1.7 fusion.61
  50.6 11.2 %all-to-all-start = ((bf16[2,64,1408]{2,0,1:T(2,128)(2,1)}), bf16[2,64,1408]{2,0,1:T(2,128)(2,1)S(1)}, u32[]{:S(2)}, u32[]{:S(2)}) async-start(bf16[2,64,1408]{2,0,1:T(2,128)(2,1)} %fusion.61), calls=%async_computation | async-start | bytes 720896 | tf_op jit(solution)/shard_map/all_to_all | solution.py:215
  62.1 10.6 %all-to-all-done = bf16[2,64,1408]{2,0,1:T(2,128)(2,1)S(1)} async-done(((bf16[2,64,1408]{2,0,1:T(2,128)(2,1)}), bf16[2,64,1408]{2,0,1:T(2,128)(2,1)S(1)}, u32[]{:S(2)}, u32[]{:S(2)}) %all-to-all-start) | async-done | bytes 360480 | tf_op jit(solution)/shard_map/all_to_all | solution.py:215
  72.7 1.6 scatter_fusion
  74.3 0.2 fusion.34
  74.6 1.5 fusion.54
  76.1 0.7 pad_maximum_fusion
  76.8 2.0 collective-permute-start.4
  78.8 0.2 convert_reduce_fusion.1
  79.0 0.6 pad_add_fusion.1.info_ref
  79.6 0.8 fusion.63
  80.4 1.3 copy.56
  81.8 2.4 %fusion.59.q_ref = bf16[8,256,88]{2,1,0:T(8,128)(2,1)} fusion(f32[256,8,88]{2,0,1:T(8,128)} %copy.56, f32[256,8]{0,1:T(8,128)S(1)} %add_rsqrt_fusion.2), kind=kLoop, calls=%fused_computation.72 | loop fusion | flops 360448 | bytes 1089536 | tf_op jit(solution)/shard_map/transpose | solution.py:250
  84.2 60.2 %all-gather.3.cloned.1.call-done = bf16[128,256,88]{1,2,0:T(8,128)(2,1)} async-done(((bf16[2,256,88]{1,2,0:T(8,128)(2,1)}), bf16[128,256,88]{1,2,0:T(8,128)(2,1)}) %all-gather.3.cloned.1.call-update) | async-done | bytes 5767184 | tf_op jit(solution)/shard_map/all_gather | solution.py:241
  144.4 9.8 %copy.57 = bf16[128,256,88]{2,1,0:T(8,128)(2,1)} copy(bf16[128,256,88]{1,2,0:T(8,128)(2,1)} %all-gather.3.cloned.1.call-done) | data formatting | bytes 11534336 | tf_op jit(solution)/shard_map/all_gather | solution.py:241
  154.3 40.5 %shard_map.118 = bf16[8,256,88]{2,1,0:T(8,128)(2,1)} custom-call(s32[8]{0:T(128)} %pad_add_fusion.1.info_ref, bf16[8,256,88]{2,1,0:T(8,128)(2,1)} %fusion.59.q_ref, bf16[64,2,256,88]{3,2,1,0:T(8,128)(2,1)} %bitcast.110), custom_call_target="tpu_custom_call" | custom-call | tf_op jit(solution)/shard_map/pallas_call | solution.py:116
  194.7 1.2 copy.58
  196.0 1.3 collective-permute-start.3
  197.3 1.3 collective-permute-done.3
  198.6 5.6 %fusion.30 = bf16[256,1,1408]{2,0,1:T(8,128)(2,1)} fusion(bf16[704,1408]{1,0:T(8,128)(2,1)} %collective-permute-done.4, bf16[704,1408]{1,0:T(8,128)(2,1)} %param.23, pred[]{:T(512)S(6)} %eq.52, bf16[256,1408]{1,0:T(8,128)(2,1)S(1)} %scatter_fusion, bf16[256,704]{0,1:T(8,128)(2,1)S(1)} %collective-permute-done.3, bf16[256,704]{0,1:T(8,128)(2,1)S(1)} %bitcast.120), kind=kOutput, calls=%fused_computation.33 | convolution fusion | flops 1037189120 | bytes 6127617 | tf_op jit(solution)/shard_map/dot_general | solution.py:253
  (43 shorter events, 0.8 us)
Async XLA Ops:
  6.5 73.1 %copy-start = (bf16[1408,704]{0,1:T(8,128)(2,1)S(1)}, bf16[1408,704]{0,1:T(8,128)(2,1)}, u32[]{:S(2)}) copy-start(bf16[1408,704]{0,1:T(8,128)(2,1)} %param.21) | copy-start | bytes 5947396
  6.5 4.8 %copy-start.1 = (bf16[512,1408]{1,0:T(8,128)(2,1)S(1)}, bf16[512,1408]{1,0:T(8,128)(2,1)}, u32[]{:S(2)}) copy-start(bf16[512,1408]{1,0:T(8,128)(2,1)} %param.12) | copy-start | bytes 4325380
  6.5 29.1 %collective-permute-start.1 = (bf16[704,1408]{1,0:T(8,128)(2,1)}, bf16[704,1408]{1,0:T(8,128)(2,1)}, u32[]{:S(2)}, u32[]{:S(2)}) collective-permute-start(bf16[704,1408]{1,0:T(8,128)(2,1)} %param.19), channel_id=1, source_target_pairs={{0,64},{64,0},{1,65},{65,1},{2,66},{66,2},{3,67},{67,3},{4,68},{68... | collective-permute-start | bytes 5947400 | tf_op jit(solution)/shard_map/ppermute | solution.py:137
  17.9 2.0 copy-start.3
  29.8 5.8 %collective-permute-start = (bf16[256,704]{1,0:T(8,128)(2,1)S(1)}, bf16[256,704]{1,0:T(8,128)(2,1)}, u32[]{:S(2)}, u32[]{:S(2)}) collective-permute-start(bf16[256,704]{1,0:T(8,128)(2,1)S(1)} %gather_fusion.2), channel_id=1, source_target_pairs={{0,64},{64,0},{1,65},{65,1},{2,66},{66,2},{3,67},{67,3},{4,68},{68... | collective-permute-start | bytes 1081352 | tf_op jit(solution)/shard_map/ppermute | solution.py:137
  39.8 5.0 %copy-start.5 = (s32[8192]{0:T(1024)S(1)}, s32[8192]{0:T(1024)}, u32[]{:S(2)}) copy-start(s32[8192]{0:T(1024)} %param.15) | copy-start | bytes 98308
  44.3 28.4 %copy-start.2 = (bf16[256,1,1408]{2,0,1:T(8,128)(2,1)S(1)}, bf16[256,1,1408]{2,0,1:T(8,128)(2,1)}, u32[]{:S(2)}) copy-start(bf16[256,1,1408]{2,0,1:T(8,128)(2,1)} %param.16) | copy-start | bytes 2162692
  44.3 3.0 %collective-permute-start.2 = (f32[128,1408]{1,0:T(8,128)S(1)}, f32[128,1408]{1,0:T(8,128)}, u32[]{:S(2)}, u32[]{:S(2)}) collective-permute-start(f32[128,1408]{1,0:T(8,128)S(1)} %fusion.79), channel_id=1, source_target_pairs={{0,64},{64,0},{1,65},{65,1},{2,66},{66,2},{3,67},{67,3},{4,68},{68... | collective-permute-start | bytes 2162696 | tf_op jit(solution)/shard_map/ppermute | solution.py:137
  50.6 22.1 %all-to-all-start = ((bf16[2,64,1408]{2,0,1:T(2,128)(2,1)}), bf16[2,64,1408]{2,0,1:T(2,128)(2,1)S(1)}, u32[]{:S(2)}, u32[]{:S(2)}) async-start(bf16[2,64,1408]{2,0,1:T(2,128)(2,1)} %fusion.61), calls=%async_computation | async-start | bytes 720896 | tf_op jit(solution)/shard_map/all_to_all | solution.py:215
  61.8 82.6 %all-gather.3.cloned.1.call-start = ((), (), s32[]{:S(2)}) async-start(), calls=%async_computation.1 | async-start | bytes 5857280 | tf_op jit(solution)/shard_map/all_gather | solution.py:241
  74.3 4.5 %copy-start.4 = (s32[256,64]{0,1:T(8,128)S(1)}, s32[256,64]{0,1:T(8,128)}, u32[]{:S(2)}) copy-start(s32[256,64]{0,1:T(8,128)} %param.17) | copy-start | bytes 196612
  76.8 120.5 %collective-permute-start.4 = (bf16[704,1408]{1,0:T(8,128)(2,1)}, bf16[704,1408]{1,0:T(8,128)(2,1)}, u32[]{:S(2)}, u32[]{:S(2)}) collective-permute-start(bf16[704,1408]{1,0:T(8,128)(2,1)} %param.23), channel_id=1, source_target_pairs={{0,64},{64,0},{1,65},{65,1},{2,66},{66,2},{3,67},{67,3},{4,68},{68... | collective-permute-start | bytes 5947400 | tf_op jit(solution)/shard_map/ppermute | solution.py:137
  196.0 2.6 %collective-permute-start.3 = (bf16[256,704]{0,1:T(8,128)(2,1)S(1)}, bf16[256,704]{0,1:T(8,128)(2,1)S(1)}, u32[]{:S(2)}, u32[]{:S(2)}) collective-permute-start(bf16[256,704]{0,1:T(8,128)(2,1)S(1)} %bitcast.119), channel_id=1, source_target_pairs={{0,64},{64,0},{1,65},{65,1},{2,66},{66,2},{3,67},{67,3},{4,68},{68... | collective-permute-start | bytes 1081352 | tf_op jit(solution)/shard_map/ppermute | solution.py:137
Sparse Core Ops, SparseCore 0:
  76.9 67.4 all-gather.2

commit v5 on v4

--- a/solution.py
+++ b/solution.py
@@ -195,11 +195,19 @@
     picks = merge_rows(image_grid, offsets, merged_count)
     own_picks = lax.dynamic_slice_in_dim(picks, 2 * section_index, 2, 1).reshape(-1)
     other_picks = lax.dynamic_slice_in_dim(picks, 2 - 2 * section_index, 2, 1).reshape(-1)
-    received_heads = swap(attended[other_picks])
-    own_rows = jnp.concatenate([attended[own_picks], received_heads], 1)
+    patch_ids = jnp.arange(patch_count, dtype=jnp.int32)[None, :]
+    own_select = (own_picks[:, None] == patch_ids).astype(jnp.bfloat16)
+    other_select = (other_picks[:, None] == patch_ids).astype(jnp.bfloat16)
+    received_heads = swap(
+        jnp.dot(other_select, attended, preferred_element_type=jnp.float32).astype(jnp.bfloat16)
+    )
+    own_heads = jnp.dot(own_select, attended, preferred_element_type=jnp.float32).astype(
+        jnp.bfloat16
+    )
+    own_rows = jnp.concatenate([own_heads, received_heads], 1)
     full_out = jnp.concatenate([vision_out, vision_out_other], 0)
     kept = (
-        patches[own_picks].astype(jnp.float32)
+        jnp.dot(own_select, patches, preferred_element_type=jnp.float32)
         + jnp.dot(own_rows, full_out, preferred_element_type=jnp.float32)
     ).astype(jnp.bfloat16)
     merge_terms = jnp.dot(
@@ -226,9 +234,12 @@
     text_rows = text_embeds.shape[0]
     prompt = text_embeds.reshape(text_rows, D).at[landing.reshape(-1)].set(received.reshape(-1, D))
     text_normed = root_norm(prompt).astype(jnp.bfloat16)
-    text_queries = root_norm(
-        jnp.dot(text_normed, decoder_q, preferred_element_type=jnp.float32).reshape(
-            text_rows, local_heads, HEAD
+    head_queries = root_norm(
+        jnp.einsum(
+            "td,dhe->hte",
+            text_normed,
+            decoder_q.reshape(D, local_heads, HEAD),
+            preferred_element_type=jnp.float32,
         )
     ).astype(jnp.bfloat16)
     paired = jnp.dot(
@@ -247,7 +258,7 @@
     info = jnp.concatenate(
         [doc_starts, jnp.full((1,), seq_index, jnp.int32), jnp.zeros((3,), jnp.int32)]
     )
-    head_major = text_attention(info, jnp.transpose(text_queries, (1, 0, 2)), piece, rows, scale)
+    head_major = text_attention(info, head_queries, piece, rows, scale)
     attended_text = jnp.transpose(head_major, (1, 0, 2)).reshape(text_rows, -1)
     all_heads = in_head_order(first, attended_text, swap(attended_text), 1)
     output_terms = jnp.dot(all_heads, decoder_out_full, preferred_element_type=jnp.float32)

time: 212 us -> 202 us (0.953); the launches traced: 211 us -> 204 us
  local copies, waits for them, and re-layouts: 25.4 us -> 16.6 us
  Pallas kernels: 40.5 us -> 43.4 us
    gather x3 -> x0, local copies, waits for them, and re-layouts: 6.57 us -> none  [the longest x1 3.45 us: body(): patches[own_picks].astype(jnp.float32)]
    pallas_call x1, Pallas kernels: 40.5 us -> 43.4 us  [text_attention(): pl.pallas_call(functools.partial(_text_kernel, scale=scale), grid_spec=pl...]
    dot_general x1 -> x3, matrix products: 0.83 us -> 3.53 us  [the longest x1 1.72 us: body(): jnp.dot(own_select, attended, preferred_element_type=jnp.float32)]
    convert_element_type x0 -> x1, other arithmetic: none -> 2.38 us  [body(): head_queries = root_norm(jnp.einsum('td,dhe->hte', text_normed, decoder_q...]
    transpose x1 -> x0, other arithmetic: 2.36 us -> none  [body(): jnp.transpose(text_queries, (1, 0, 2))]
  transfers between devices with their start and end apart: 7 -> 7, of which waited for: 3 -> 3; matrix products, arithmetic and copies ran while one was open for 20% -> 18% of each run, Pallas kernels for 19% -> 21%
where the time goes in v5:
time: 202 us; the launch traced here: 204 us
  waiting for transfers between devices  70.9 us (35%)
  Pallas kernels  43.4 us (21%)
  matrix products  29.4 us (15%)
  local copies, waits for them, and re-layouts  16.6 us (8%)
  starting transfers between devices  16.5 us (8%)
  between operations  15.7 us (8%)
  other arithmetic  11.2 us (6%)
    all_gather x1, waiting for transfers between devices, body(): piece = lax.all_gather(shared, 'seq', axis=0, tiled=True)  58.9 us
    pallas_call x1, Pallas kernels, text_attention(): pl.pallas_call(functools.partial(_text_kernel, scale=scale), grid_spec=pl...  43.4 us
    all_to_all x1, starting transfers between devices, body(): lax.all_to_all(jnp.roll(image_rows.reshape(per_peer, seq_count, image_row...  11.2 us
    all_to_all x1, waiting for transfers between devices, body(): lax.all_to_all(jnp.roll(image_rows.reshape(per_peer, seq_count, image_row...  10.6 us
    all_gather x1, local copies, waits for them, and re-layouts, body(): piece = lax.all_gather(shared, 'seq', axis=0, tiled=True)  9.83 us
    dot_general x1, matrix products, body(): jnp.dot(normed, vision_qkv.reshape(D, -1), preferred_element_type=jnp.flo...  5.99 us
    dot_general x1, matrix products, body(): jnp.dot(all_heads, decoder_out_full, preferred_element_type=jnp.float32)  5.62 us
    ppermute x5, starting transfers between devices, swap(): return lax.ppermute(values, 'section', [(0, 1), (1, 0)])  5.28 us
  transfers between devices with their start and end apart: 7, of which 3 were waited for; matrix products, arithmetic and copies ran while one was open for 18% of the time, Pallas kernels for 21%

profile of v5, /device:TPU:1, one launch (start us, length us, event | category | flops | bytes accessed | tf_op | source)
XLA Modules:
  0.0 203.7 jit_solution(13125870860386719047)
XLA Ops:
  6.5 1.4 collective-permute-start.1
  8.0 0.7 slice_bitcast_fusion.2
  8.6 0.8 fusion.77
  9.6 0.1 broadcast_add_fusion.1
  9.8 0.1 copy.43
  9.9 0.1 eq.86
  10.0 0.3 convert_reduce_fusion
  10.3 0.5 fusion.20
  10.8 6.0 %fusion.37 = f32[512,3,8,88]{0,3,2,1:T(8,128)S(1)} fusion(bf16[3,8,88,1408]{3,2,1,0:T(8,128)(2,1)} %bitcast.129, bf16[512,1408]{1,0:T(8,128)(2,1)S(1)} %copy-done.2, f32[512]{0:T(512)S(1)} %add_rsqrt_fusion.3, f32[512]{0:T(512)S(1)} %broadcast_multiply_fusion), kind=kOutput, calls=%fused_computation.37 | convolution fusion | flops 3047948288 | bytes 11718656 | tf_op jit(solution)/shard_map/dot_general | solution.py:173
  16.8 0.4 multiply_reduce_fusion.1
  17.3 0.2 broadcast_compare_fusion
  17.5 2.6 %fusion = (f32[8,512]{1,0:T(8,128)S(1)}, f32[8,512,512]{1,2,0:T(8,128)S(1)}) fusion(pred[512,512]{0,1:T(8,128)(4,1)S(1)} %broadcast_compare_fusion, f32[512,3,8,88]{0,3,2,1:T(8,128)S(1)} %fusion.37, f32[512,8]{0,1:T(8,128)S(1)} %get-tuple-element.23, f32[512,8]{0,1:T(8,128)S(1)} %get-tuple-element.24), kind=kOutput, calls=%fused_computation.2 | convolution fusion | flops 376827904 | bytes 11583488 | tf_op jit(solution)/shard_map/qhd,khd->hqk/dot_general | solution.py:183
  20.1 1.8 divide_convert_fusion
  21.8 1.2 convolution_convert_fusion
  23.0 0.2 collective-permute-start
  23.2 0.1 copy.41
  23.3 0.1 eq.79
  23.5 1.7 convolution_convert_fusion.1
  25.2 0.6 fusion.61
  25.8 3.1 %fusion.26 = bf16[256,1408]{1,0:T(8,128)(2,1)S(1)} fusion(f32[256,1408]{1,0:T(8,128)S(1)} %fusion.61, bf16[704,1408]{1,0:T(8,128)(2,1)} %collective-permute-done.1, bf16[704,1408]{1,0:T(8,128)(2,1)S(1)} %copy-done.5, bf16[256,704]{0,1:T(8,128)(2,1)} %collective-permute-done, bf16[256,704]{0,1:T(8,128)(2,1)S(1)} %convolution_convert_fusion.1), kind=kOutput, calls=%fused_computation.28 | convolution fusion | flops 1025114112 | bytes 6848512 | tf_op jit(solution)/shard_map/dot_general | solution.py:211
  28.9 0.2 reshape.479
  29.2 4.5 %fusion.84 = f32[128,1408]{1,0:T(8,128)S(1)} fusion(bf16[128,2816]{1,0:T(8,128)(2,1)S(1)} %reshape.479, bf16[2816,1408]{1,0:T(8,128)(2,1)} %bitcast.120), kind=kOutput, calls=%fused_computation.156 | convolution fusion | flops 1015021568 | bytes 9371648 | tf_op jit(solution)/shard_map/dot_general | solution.py:213
  33.7 0.6 collective-permute-start.2
  34.4 0.1 fusion.83
  34.5 0.5 constant_dynamic-slice_fusion
  37.0 1.2 add_convert_fusion
  38.2 0.4 copy.44
  38.6 1.7 fusion.63
  40.3 11.2 %all-to-all-start = ((bf16[2,64,1408]{2,0,1:T(2,128)(2,1)}), bf16[2,64,1408]{2,0,1:T(2,128)(2,1)S(1)}, u32[]{:S(2)}, u32[]{:S(2)}) async-start(bf16[2,64,1408]{2,0,1:T(2,128)(2,1)} %fusion.63), calls=%async_computation | async-start | bytes 720896 | tf_op jit(solution)/shard_map/all_to_all | solution.py:223
  51.7 10.6 %all-to-all-done = bf16[2,64,1408]{2,0,1:T(2,128)(2,1)S(1)} async-done(((bf16[2,64,1408]{2,0,1:T(2,128)(2,1)}), bf16[2,64,1408]{2,0,1:T(2,128)(2,1)S(1)}, u32[]{:S(2)}, u32[]{:S(2)}) %all-to-all-start) | async-done | bytes 360480 | tf_op jit(solution)/shard_map/all_to_all | solution.py:223
  62.4 1.6 scatter_fusion
  64.0 0.2 fusion.34
  64.2 1.5 fusion.56
  65.8 0.7 pad_maximum_fusion
  66.5 1.8 collective-permute-start.4
  68.3 0.2 convert_reduce_fusion.1
  68.4 0.6 pad_add_fusion.1.info_ref
  69.0 0.8 fusion.65
  69.9 1.3 copy.47
  71.2 1.6 fusion.41
  72.8 2.4 %fusion.42.q_ref = bf16[8,256,88]{2,1,0:T(8,128)(2,1)} fusion(f32[256,8,88]{2,0,1:T(8,128)} %copy.47, f32[8,256]{1,0:T(8,128)S(1)} %add_rsqrt_fusion.2), kind=kLoop, calls=%fused_computation.53 | loop fusion | flops 360448 | bytes 1089536 | tf_op jit(solution)/shard_map/convert_element_type | solution.py:244
  75.2 58.9 %all-gather.3.cloned.1.call-done = bf16[128,256,88]{1,2,0:T(8,128)(2,1)} async-done(((bf16[2,256,88]{1,2,0:T(8,128)(2,1)}), bf16[128,256,88]{1,2,0:T(8,128)(2,1)}) %all-gather.3.cloned.1.call-update) | async-done | bytes 5767184 | tf_op jit(solution)/shard_map/all_gather | solution.py:252
  134.1 9.8 %copy.48 = bf16[128,256,88]{2,1,0:T(8,128)(2,1)} copy(bf16[128,256,88]{1,2,0:T(8,128)(2,1)} %all-gather.3.cloned.1.call-done) | data formatting | bytes 11534336 | tf_op jit(solution)/shard_map/all_gather | solution.py:252
  143.9 43.4 %shard_map.118 = bf16[8,256,88]{2,1,0:T(8,128)(2,1)} custom-call(s32[8]{0:T(128)} %pad_add_fusion.1.info_ref, bf16[8,256,88]{2,1,0:T(8,128)(2,1)} %fusion.42.q_ref, bf16[64,2,256,88]{3,2,1,0:T(8,128)(2,1)} %bitcast.119), custom_call_target="tpu_custom_call" | custom-call | tf_op jit(solution)/shard_map/pallas_call | solution.py:116
  187.4 1.2 copy.49
  188.6 1.3 collective-permute-start.3
  189.9 1.3 collective-permute-done.3
  191.2 5.6 %fusion.30 = bf16[256,1,1408]{2,0,1:T(8,128)(2,1)} fusion(bf16[704,1408]{1,0:T(8,128)(2,1)} %collective-permute-done.4, bf16[704,1408]{1,0:T(8,128)(2,1)} %param.23, pred[]{:T(512)S(6)} %eq.90, bf16[256,1408]{1,0:T(8,128)(2,1)S(1)} %scatter_fusion, bf16[256,704]{0,1:T(8,128)(2,1)S(1)} %collective-permute-done.3, bf16[256,704]{0,1:T(8,128)(2,1)S(1)} %bitcast.127), kind=kOutput, calls=%fused_computation.30 | convolution fusion | flops 1037189120 | bytes 6127617 | tf_op jit(solution)/shard_map/dot_general | solution.py:264
  (41 shorter events, 0.6 us)
Async XLA Ops:
  6.5 62.5 %copy-start = (bf16[1408,704]{0,1:T(8,128)(2,1)S(1)}, bf16[1408,704]{0,1:T(8,128)(2,1)}, u32[]{:S(2)}) copy-start(bf16[1408,704]{0,1:T(8,128)(2,1)} %param.21) | copy-start | bytes 5947396
  6.5 3.5 %copy-start.2 = (bf16[512,1408]{1,0:T(8,128)(2,1)S(1)}, bf16[512,1408]{1,0:T(8,128)(2,1)}, u32[]{:S(2)}) copy-start(bf16[512,1408]{1,0:T(8,128)(2,1)} %param.12) | copy-start | bytes 4325380
  6.5 19.3 %collective-permute-start.1 = (bf16[704,1408]{1,0:T(8,128)(2,1)}, bf16[704,1408]{1,0:T(8,128)(2,1)}, u32[]{:S(2)}, u32[]{:S(2)}) collective-permute-start(bf16[704,1408]{1,0:T(8,128)(2,1)} %param.19), channel_id=1, source_target_pairs={{0,64},{64,0},{1,65},{65,1},{2,66},{66,2},{3,67},{67,3},{4,68},{68... | collective-permute-start | bytes 5947400 | tf_op jit(solution)/shard_map/ppermute | solution.py:137
  21.8 1.4 copy-start.6
  23.0 2.8 %collective-permute-start = (bf16[256,704]{0,1:T(8,128)(2,1)}, bf16[256,704]{0,1:T(8,128)(2,1)}, u32[]{:S(2)}, u32[]{:S(2)}) collective-permute-start(bf16[256,704]{0,1:T(8,128)(2,1)} %convolution_convert_fusion), channel_id=1, source_target_pairs={{0,64},{64,0},{1,65},{65,1},{2,66},{66,2},{3,67},{67,3},{4,68},{68... | collective-permute-start | bytes 1081352 | tf_op jit(solution)/shard_map/ppermute | solution.py:137
  23.4 2.4 %copy-start.5 = (bf16[704,1408]{1,0:T(8,128)(2,1)S(1)}, bf16[704,1408]{1,0:T(8,128)(2,1)}, u32[]{:S(2)}) copy-start(bf16[704,1408]{1,0:T(8,128)(2,1)} %param.19) | copy-start | bytes 5947396
  29.2 5.2 %copy-start.4 = (s32[8192]{0:T(1024)S(1)}, s32[8192]{0:T(1024)}, u32[]{:S(2)}) copy-start(s32[8192]{0:T(1024)} %param.15) | copy-start | bytes 98308
  33.7 3.3 %collective-permute-start.2 = (f32[128,1408]{1,0:T(8,128)S(1)}, f32[128,1408]{1,0:T(8,128)}, u32[]{:S(2)}, u32[]{:S(2)}) collective-permute-start(f32[128,1408]{1,0:T(8,128)S(1)} %fusion.84), channel_id=1, source_target_pairs={{0,64},{64,0},{1,65},{65,1},{2,66},{66,2},{3,67},{67,3},{4,68},{68... | collective-permute-start | bytes 2162696 | tf_op jit(solution)/shard_map/ppermute | solution.py:137
  37.0 25.4 %copy-start.1 = (bf16[256,1,1408]{2,0,1:T(8,128)(2,1)S(1)}, bf16[256,1,1408]{2,0,1:T(8,128)(2,1)}, u32[]{:S(2)}) copy-start(bf16[256,1,1408]{2,0,1:T(8,128)(2,1)} %param.16) | copy-start | bytes 2162692
  40.3 22.1 %all-to-all-start = ((bf16[2,64,1408]{2,0,1:T(2,128)(2,1)}), bf16[2,64,1408]{2,0,1:T(2,128)(2,1)S(1)}, u32[]{:S(2)}, u32[]{:S(2)}) async-start(bf16[2,64,1408]{2,0,1:T(2,128)(2,1)} %fusion.63), calls=%async_computation | async-start | bytes 720896 | tf_op jit(solution)/shard_map/all_to_all | solution.py:223
  51.5 82.6 %all-gather.3.cloned.1.call-start = ((), (), s32[]{:S(2)}) async-start(), calls=%async_computation.1 | async-start | bytes 5857280 | tf_op jit(solution)/shard_map/all_gather | solution.py:252
  64.0 4.3 %copy-start.3 = (s32[256,64]{0,1:T(8,128)S(1)}, s32[256,64]{0,1:T(8,128)}, u32[]{:S(2)}) copy-start(s32[256,64]{0,1:T(8,128)} %param.17) | copy-start | bytes 196612
  66.5 123.5 %collective-permute-start.4 = (bf16[704,1408]{1,0:T(8,128)(2,1)}, bf16[704,1408]{1,0:T(8,128)(2,1)}, u32[]{:S(2)}, u32[]{:S(2)}) collective-permute-start(bf16[704,1408]{1,0:T(8,128)(2,1)} %param.23), channel_id=1, source_target_pairs={{0,64},{64,0},{1,65},{65,1},{2,66},{66,2},{3,67},{67,3},{4,68},{68... | collective-permute-start | bytes 5947400 | tf_op jit(solution)/shard_map/ppermute | solution.py:137
  188.6 2.6 %collective-permute-start.3 = (bf16[256,704]{0,1:T(8,128)(2,1)S(1)}, bf16[256,704]{0,1:T(8,128)(2,1)S(1)}, u32[]{:S(2)}, u32[]{:S(2)}) collective-permute-start(bf16[256,704]{0,1:T(8,128)(2,1)S(1)} %bitcast.126), channel_id=1, source_target_pairs={{0,64},{64,0},{1,65},{65,1},{2,66},{66,2},{3,67},{67,3},{4,68},{68... | collective-permute-start | bytes 1081352 | tf_op jit(solution)/shard_map/ppermute | solution.py:137
Sparse Core Ops, SparseCore 0:
  66.6 67.4 all-gather.2

commit v6 on v5

--- a/solution.py
+++ b/solution.py
@@ -52,17 +52,20 @@
     return start
 
 
-def _text_kernel(info_ref, q_ref, kv_ref, o_ref, acc_ref, tot_ref, *, scale):
-    qb = pl.program_id(0)
-    kb = pl.program_id(1)
+def _first_block(info_ref, qb, span):
+    return _segment_start(info_ref, qb * span + info_ref[4]) // span
+
+
+def _text_kernel(query_block_ref, key_block_ref, info_ref, q_ref, kv_ref, o_ref, acc_ref, tot_ref, *, scale):
+    step = pl.program_id(0)
+    qb = query_block_ref[step]
+    kb = key_block_ref[step]
     heads, rows, head = q_ref.shape
     shards = kv_ref.shape[0]
     span = rows * shards
     own = info_ref[4]
-    first_query = qb * span + own
-    last_query = first_query + (rows - 1) * shards
-    first_block = _segment_start(info_ref, first_query) // span
-    active = (kb >= first_block) & (kb <= qb)
+    last_query = qb * span + own + (rows - 1) * shards
+    active = kb >= _first_block(info_ref, qb, span)
     unmasked = (kb < qb) & (kb * span >= _segment_start(info_ref, last_query))
 
     @pl.when(kb == 0)
@@ -98,7 +101,7 @@
     def _():
         accumulate(True)
 
-    @pl.when(kb == pl.num_programs(1) - 1)
+    @pl.when(kb == qb)
     def _():
         o_ref[...] = (acc_ref[...] / tot_ref[...]).astype(o_ref.dtype).reshape(o_ref.shape)
 
@@ -108,29 +111,35 @@
     shards = kv.shape[0]
     blocks = text_rows // rows
     span = rows * shards
-
-    def kv_block(i, j, info_ref):
-        first_block = _segment_start(info_ref, i * span + info_ref[4]) // span
-        return (0, 0, jnp.maximum(jnp.minimum(i, j), first_block), 0)
+    pairs = [(i, j) for i in range(blocks) for j in range(i + 1)]
+    query_block = jnp.array([i for i, _ in pairs], jnp.int32)
+    key_block = jnp.array([j for _, j in pairs], jnp.int32)
+
+    def q_block(t, qb_ref, kb_ref, info_ref):
+        return (0, qb_ref[t], 0)
+
+    def kv_block(t, qb_ref, kb_ref, info_ref):
+        qb = qb_ref[t]
+        return (0, 0, jnp.maximum(kb_ref[t], _first_block(info_ref, qb, span)), 0)
 
     return pl.pallas_call(
         functools.partial(_text_kernel, scale=scale),
         grid_spec=pltpu.PrefetchScalarGridSpec(
-            num_scalar_prefetch=1,
-            grid=(blocks, blocks),
+            num_scalar_prefetch=3,
+            grid=(len(pairs),),
             in_specs=[
-                pl.BlockSpec((heads, rows, head), lambda i, j, info_ref: (0, i, 0)),
+                pl.BlockSpec((heads, rows, head), q_block),
                 pl.BlockSpec((shards, 2, rows, head), kv_block),
             ],
-            out_specs=pl.BlockSpec((heads, rows, head), lambda i, j, info_ref: (0, i, 0)),
+            out_specs=pl.BlockSpec((heads, rows, head), q_block),
             scratch_shapes=[
                 pltpu.VMEM((heads * rows, head), jnp.float32),
                 pltpu.VMEM((heads * rows, 1), jnp.float32),
             ],
         ),
         out_shape=jax.ShapeDtypeStruct((heads, text_rows, head), jnp.bfloat16),
-        compiler_params=pltpu.CompilerParams(dimension_semantics=("arbitrary", "arbitrary")),
-    )(info, q, kv)
+        compiler_params=pltpu.CompilerParams(dimension_semantics=("arbitrary",)),
+    )(query_block, key_block, info, q, kv)
 
 
 def swap(values):
@@ -167,7 +176,7 @@
     merged_count = patch_count // 4
 
     vision_out_other = swap(vision_out)
-    decoder_out_full = in_head_order(first, decoder_out, swap(decoder_out), 0)
+    decoder_out_other = swap(decoder_out)
 
     normed = layer_norm(patches).astype(jnp.bfloat16)
     mixed = jnp.dot(normed, vision_qkv.reshape(D, -1), preferred_element_type=jnp.float32).reshape(
@@ -203,6 +212,9 @@
     )
     own_heads = jnp.dot(own_select, attended, preferred_element_type=jnp.float32).astype(
         jnp.bfloat16
+    )
+    decoder_out_full, received_heads = lax.optimization_barrier(
+        (in_head_order(first, decoder_out, decoder_out_other, 0), received_heads)
     )
     own_rows = jnp.concatenate([own_heads, received_heads], 1)
     full_out = jnp.concatenate([vision_out, vision_out_other], 0)

time: 202 us -> 206 us (1.020)
  Pallas kernels: 43.4 us -> 30.6 us
  other arithmetic: 11.2 us -> 20.1 us
  matrix products: 29.4 us -> 33 us
  local copies, waits for them, and re-layouts: 16.6 us -> 19 us
    pallas_call x1, Pallas kernels: 43.4 us -> 30.6 us  [text_attention(): pl.pallas_call(functools.partial(_text_kernel, scale=scale), grid_spec=pl...]
    select_n x0 -> x1, other arithmetic: none -> 8.39 us  [in_head_order(): jnp.where(first, jnp.concatenate([own, other], axis), jnp.concatenate([ot...]
    unnamed x14 -> x20, local copies, waits for them, and re-layouts: 0.04 us -> 2.28 us
    dot_general x1, matrix products: 1.77 us -> 3.87 us  [body(): jnp.einsum('hqk,khd->qhd', weights.astype(jnp.bfloat16), values, preferre...]
  transfers between devices with their start and end apart: 7 -> 7, of which waited for: 3 -> 3; matrix products, arithmetic and copies ran while one was open for 18% -> 19% of each run, Pallas kernels for 21% -> 0%
where the time goes in v6:
time: 206 us
  waiting for transfers between devices  72.7 us (35%)
  matrix products  33 us (16%)
  Pallas kernels  30.6 us (15%)
  other arithmetic  20.1 us (10%)
  local copies, waits for them, and re-layouts  19 us (9%)
  between operations  15.7 us (8%)
  starting transfers between devices  14.7 us (7%)
    all_gather x1, waiting for transfers between devices, body(): piece = lax.all_gather(shared, 'seq', axis=0, tiled=True)  60.9 us
    pallas_call x1, Pallas kernels, text_attention(): pl.pallas_call(functools.partial(_text_kernel, scale=scale), grid_spec=pl...  30.6 us
    all_to_all x1, starting transfers between devices, body(): lax.all_to_all(jnp.roll(image_rows.reshape(per_peer, seq_count, image_row...  11.2 us
    all_to_all x1, waiting for transfers between devices, body(): lax.all_to_all(jnp.roll(image_rows.reshape(per_peer, seq_count, image_row...  10.4 us
    all_gather x1, local copies, waits for them, and re-layouts, body(): piece = lax.all_gather(shared, 'seq', axis=0, tiled=True)  9.83 us
    select_n x1, other arithmetic, in_head_order(): jnp.where(first, jnp.concatenate([own, other], axis), jnp.concatenate([ot...  8.39 us
    dot_general x1, matrix products, body(): jnp.dot(normed, vision_qkv.reshape(D, -1), preferred_element_type=jnp.flo...  5.99 us
    dot_general x1, matrix products, body(): jnp.dot(kept.reshape(merged_count, 2 * D), projector.reshape(2 * D, D), p...  4.54 us
  transfers between devices with their start and end apart: 7, of which 3 were waited for; matrix products, arithmetic and copies ran while one was open for 19% of the time, Pallas kernels for 0%

profile of v6, /device:TPU:1, one launch (start us, length us, event | category | flops | bytes accessed | tf_op | source)
XLA Modules:
  0.0 205.8 jit_solution(3437402447665762296)
XLA Ops:
  6.5 1.4 collective-permute-start
  8.0 0.7 slice_bitcast_fusion.2
  8.6 1.6 convert_reduce_fusion
  10.3 0.5 fusion.13
  10.8 6.0 %fusion.29 = f32[512,3,8,88]{0,3,2,1:T(8,128)S(1)} fusion(bf16[3,8,88,1408]{3,2,1,0:T(8,128)(2,1)} %bitcast.130, bf16[512,1408]{1,0:T(8,128)(2,1)S(1)} %copy-done.2, f32[512]{0:T(512)S(1)} %add_rsqrt_fusion.3, f32[512]{0:T(512)S(1)} %broadcast_multiply_fusion), kind=kOutput, calls=%fused_computation.30 | convolution fusion | flops 3047948288 | bytes 11718656 | tf_op jit(solution)/shard_map/dot_general | solution.py:182
  16.8 2.0 copy-done.4
  18.8 0.4 multiply_reduce_fusion.1
  19.2 0.3 copy-done.7
  19.6 0.2 broadcast_compare_fusion
  19.9 0.1 broadcast_add_fusion.1
  20.1 4.1 %fusion = (f32[8,512]{1,0:T(8,128)S(1)}, f32[8,512,512]{1,2,0:T(8,128)S(1)}) fusion(pred[512,512]{0,1:T(8,128)(4,1)S(1)} %broadcast_compare_fusion, f32[512,3,8,88]{0,3,2,1:T(8,128)} %copy-done.4, f32[512,8]{0,1:T(8,128)S(1)} %get-tuple-element.27, f32[512,8]{0,1:T(8,128)S(1)} %get-tuple-element.28), kind=kOutput, calls=%fused_computation.2 | convolution fusion | flops 376827904 | bytes 11583488 | tf_op jit(solution)/shard_map/qhd,khd->hqk/dot_general | solution.py:192
  24.2 3.9 %divide_convert_fusion = bf16[512,8,88]{0,2,1:T(8,128)(2,1)} fusion(f32[8,512,512]{1,2,0:T(8,128)S(1)} %get-tuple-element.26, pred[512,512]{0,1:T(8,128)(4,1)S(1)} %broadcast_compare_fusion, f32[512,3,8,88]{0,3,2,1:T(8,128)} %copy-done.4, f32[512,8]{0,1:T(8,128)S(1)} %bitcast.133), kind=kOutput, calls=%fused_computation.34 | convolution fusion | flops 376111104 | bytes 10108928 | tf_op jit(solution)/shard_map/hqk,khd->qhd/dot_general | solution.py:196
  28.1 0.1 copy.45
  28.2 0.1 eq.87
  28.3 2.3 %convolution_convert_fusion = bf16[256,704]{0,1:T(8,128)(2,1)} fusion(bf16[512,704]{0,1:T(8,128)(2,1)} %bitcast.131, s32[256]{0:T(256)S(1)} %eq.87), kind=kOutput, calls=%fused_computation.41 | convolution fusion | flops 184860672 | bytes 1082368 | tf_op jit(solution)/shard_map/dot_general | solution.py:211
  30.6 0.6 collective-permute-start.1
  31.3 0.1 copy.43
  31.4 0.1 eq.79
  31.5 1.7 convolution_convert_fusion.1
  33.3 0.6 fusion.53
  33.9 8.4 %maximum_select_fusion = bf16[1408,1408]{1,0:T(8,128)(2,1)} fusion(bf16[704,1408]{1,0:T(8,128)(2,1)} %collective-permute-done, bf16[704,1408]{1,0:T(8,128)(2,1)S(1)} %copy-done.3, pred[]{:T(512)S(6)} %eq.86), kind=kLoop, calls=%fused_computation.8 | loop fusion | flops 17842176 | bytes 7929857 | tf_op jit(solution)/shard_map/jit(_where)/select_n | solution.py:150
  42.3 3.1 %fusion.19 = bf16[256,1408]{1,0:T(8,128)(2,1)S(1)} fusion(f32[256,1408]{1,0:T(8,128)S(1)} %fusion.53, bf16[704,1408]{1,0:T(8,128)(2,1)} %collective-permute-done.2, bf16[704,1408]{1,0:T(8,128)(2,1)S(1)} %copy-done.9, bf16[256,704]{0,1:T(8,128)(2,1)} %collective-permute-done.1, bf16[256,704]{0,1:T(8,128)(2,1)S(1)} %convolution_convert_fusion.1), kind=kOutput, calls=%fused_computation.22 | convolution fusion | flops 1025114112 | bytes 6848512 | tf_op jit(solution)/shard_map/dot_general | solution.py:223
  45.4 0.2 reshape.479
  45.7 4.5 %fusion.76 = f32[128,1408]{1,0:T(8,128)S(1)} fusion(bf16[128,2816]{1,0:T(8,128)(2,1)S(1)} %reshape.479, bf16[2816,1408]{1,0:T(8,128)(2,1)} %bitcast.121), kind=kOutput, calls=%fused_computation.149 | convolution fusion | flops 1015021568 | bytes 9371648 | tf_op jit(solution)/shard_map/dot_general | solution.py:225
  50.4 0.1 fusion.75
  50.5 0.5 constant_dynamic-slice_fusion
  53.0 1.2 add_convert_fusion
  54.2 0.4 copy.46
  54.5 1.7 fusion.55
  56.2 11.2 %all-to-all-start = ((bf16[2,64,1408]{2,0,1:T(2,128)(2,1)}), bf16[2,64,1408]{2,0,1:T(2,128)(2,1)S(1)}, u32[]{:S(2)}, u32[]{:S(2)}) async-start(bf16[2,64,1408]{2,0,1:T(2,128)(2,1)} %fusion.55), calls=%async_computation | async-start | bytes 720896 | tf_op jit(solution)/shard_map/all_to_all | solution.py:235
  67.7 10.4 %all-to-all-done = bf16[2,64,1408]{2,0,1:T(2,128)(2,1)S(1)} async-done(((bf16[2,64,1408]{2,0,1:T(2,128)(2,1)}), bf16[2,64,1408]{2,0,1:T(2,128)(2,1)S(1)}, u32[]{:S(2)}, u32[]{:S(2)}) %all-to-all-start) | async-done | bytes 360480 | tf_op jit(solution)/shard_map/all_to_all | solution.py:235
  78.2 1.8 scatter_fusion
  80.0 0.2 fusion.26
  80.2 1.5 fusion.48
  81.8 0.7 pad_maximum_fusion
  82.5 0.2 convert_reduce_fusion.1
  82.7 0.6 pad_add_fusion.1.info_ref
  83.2 0.8 fusion.57
  84.1 1.3 copy.49
  85.4 1.6 fusion.33
  87.0 2.4 %fusion.34.q_ref = bf16[8,256,88]{2,1,0:T(8,128)(2,1)} fusion(f32[256,8,88]{2,0,1:T(8,128)} %copy.49, f32[8,256]{1,0:T(8,128)S(1)} %add_rsqrt_fusion.2), kind=kLoop, calls=%fused_computation.46 | loop fusion | flops 360448 | bytes 1089536 | tf_op jit(solution)/shard_map/convert_element_type | solution.py:256
  89.3 60.9 %all-gather.3.cloned.1.call-done = bf16[128,256,88]{1,2,0:T(8,128)(2,1)} async-done(((bf16[2,256,88]{1,2,0:T(8,128)(2,1)}), bf16[128,256,88]{1,2,0:T(8,128)(2,1)}) %all-gather.3.cloned.1.call-update) | async-done | bytes 5767184 | tf_op jit(solution)/shard_map/all_gather | solution.py:264
  150.2 9.8 %copy.50 = bf16[128,256,88]{2,1,0:T(8,128)(2,1)} copy(bf16[128,256,88]{1,2,0:T(8,128)(2,1)} %all-gather.3.cloned.1.call-done) | data formatting | bytes 11534336 | tf_op jit(solution)/shard_map/all_gather | solution.py:264
  160.1 30.6 %shard_map.136 = bf16[8,256,88]{2,1,0:T(8,128)(2,1)} custom-call(s32[36]{0:T(128)} %constant.137.clone.query_block_ref, s32[36]{0:T(128)} %constant.138.clone.key_block_ref, s32[8]{0:T(128)} %pad_add_fusion.1.info_ref, bf16[8,256,88]{2,1,0:T(8,128)(2,1)} %fusion.34.q_ref, bf16[64,2,256,88]{3,2,1,0:T(8,128)(2,1)} %bitcast.120), custom_call_target="tpu_custom_call" | custom-call | tf_op jit(solution)/shard_map/pallas_call | solution.py:125
  190.7 1.2 copy.51
  191.9 1.3 collective-permute-start.4
  193.3 1.3 collective-permute-done.4
  194.6 4.4 %fusion.22 = bf16[256,1,1408]{2,0,1:T(8,128)(2,1)} fusion(bf16[1408,1408]{1,0:T(8,128)(2,1)} %maximum_select_fusion, bf16[256,1408]{1,0:T(8,128)(2,1)S(1)} %scatter_fusion, bf16[256,704]{0,1:T(8,128)(2,1)S(1)} %collective-permute-done.4, bf16[256,704]{0,1:T(8,128)(2,1)S(1)} %bitcast.128, pred[]{:T(512)S(6)} %eq.86), kind=kOutput, calls=%fused_computation.23 | convolution fusion | flops 1019346944 | bytes 6127617 | tf_op jit(solution)/shard_map/dot_general | solution.py:276
  (48 shorter events, 0.7 us)
Async XLA Ops:
  6.5 76.7 %copy-start = (bf16[1408,704]{0,1:T(8,128)(2,1)S(1)}, bf16[1408,704]{0,1:T(8,128)(2,1)}, u32[]{:S(2)}) copy-start(bf16[1408,704]{0,1:T(8,128)(2,1)} %param.23) | copy-start | bytes 5947396
  6.5 3.7 %copy-start.2 = (bf16[512,1408]{1,0:T(8,128)(2,1)S(1)}, bf16[512,1408]{1,0:T(8,128)(2,1)}, u32[]{:S(2)}) copy-start(bf16[512,1408]{1,0:T(8,128)(2,1)} %param.14) | copy-start | bytes 4325380
  6.5 27.4 %collective-permute-start = (bf16[704,1408]{1,0:T(8,128)(2,1)}, bf16[704,1408]{1,0:T(8,128)(2,1)}, u32[]{:S(2)}, u32[]{:S(2)}) collective-permute-start(bf16[704,1408]{1,0:T(8,128)(2,1)} %param.25), channel_id=1, source_target_pairs={{0,64},{64,0},{1,65},{65,1},{2,66},{66,2},{3,67},{67,3},{4,68},{68... | collective-permute-start | bytes 5947400 | tf_op jit(solution)/shard_map/ppermute | solution.py:146
  8.0 34.4 %collective-permute-start.2 = (bf16[704,1408]{1,0:T(8,128)(2,1)}, bf16[704,1408]{1,0:T(8,128)(2,1)}, u32[]{:S(2)}, u32[]{:S(2)}) collective-permute-start(bf16[704,1408]{1,0:T(8,128)(2,1)} %param.21), channel_id=1, source_target_pairs={{0,64},{64,0},{1,65},{65,1},{2,66},{66,2},{3,67},{67,3},{4,68},{68... | collective-permute-start | bytes 5947400 | tf_op jit(solution)/shard_map/ppermute | solution.py:146
  16.8 2.0 copy-start.4
  18.8 0.7 copy-start.7
  18.8 0.7 copy-start.8
  30.6 11.7 %collective-permute-start.1 = (bf16[256,704]{0,1:T(8,128)(2,1)}, bf16[256,704]{0,1:T(8,128)(2,1)}, u32[]{:S(2)}, u32[]{:S(2)}) collective-permute-start(bf16[256,704]{0,1:T(8,128)(2,1)} %convolution_convert_fusion), channel_id=1, source_target_pairs={{0,64},{64,0},{1,65},{65,1},{2,66},{66,2},{3,67},{67,3},{4,68},{68... | collective-permute-start | bytes 1081352 | tf_op jit(solution)/shard_map/ppermute | solution.py:146
  31.5 2.4 %copy-start.3 = (bf16[704,1408]{1,0:T(8,128)(2,1)S(1)}, bf16[704,1408]{1,0:T(8,128)(2,1)}, u32[]{:S(2)}) copy-start(bf16[704,1408]{1,0:T(8,128)(2,1)} %param.25) | copy-start | bytes 5947396
  33.9 8.4 %copy-start.9 = (bf16[704,1408]{1,0:T(8,128)(2,1)S(1)}, bf16[704,1408]{1,0:T(8,128)(2,1)}, u32[]{:S(2)}) copy-start(bf16[704,1408]{1,0:T(8,128)(2,1)} %param.21) | copy-start | bytes 5947396
  45.7 4.7 %copy-start.6 = (s32[8192]{0:T(1024)S(1)}, s32[8192]{0:T(1024)}, u32[]{:S(2)}) copy-start(s32[8192]{0:T(1024)} %param.17) | copy-start | bytes 98308
  50.2 27.9 %copy-start.1 = (bf16[256,1,1408]{2,0,1:T(8,128)(2,1)S(1)}, bf16[256,1,1408]{2,0,1:T(8,128)(2,1)}, u32[]{:S(2)}) copy-start(bf16[256,1,1408]{2,0,1:T(8,128)(2,1)} %param.18) | copy-start | bytes 2162692
  50.2 2.7 %collective-permute-start.3 = (f32[128,1408]{1,0:T(8,128)S(1)}, f32[128,1408]{1,0:T(8,128)}, u32[]{:S(2)}, u32[]{:S(2)}) collective-permute-start(f32[128,1408]{1,0:T(8,128)S(1)} %fusion.76), channel_id=1, source_target_pairs={{0,64},{64,0},{1,65},{65,1},{2,66},{66,2},{3,67},{67,3},{4,68},{68... | collective-permute-start | bytes 2162696 | tf_op jit(solution)/shard_map/ppermute | solution.py:146
  56.2 21.9 %all-to-all-start = ((bf16[2,64,1408]{2,0,1:T(2,128)(2,1)}), bf16[2,64,1408]{2,0,1:T(2,128)(2,1)S(1)}, u32[]{:S(2)}, u32[]{:S(2)}) async-start(bf16[2,64,1408]{2,0,1:T(2,128)(2,1)} %fusion.55), calls=%async_computation | async-start | bytes 720896 | tf_op jit(solution)/shard_map/all_to_all | solution.py:235
  67.4 82.8 %all-gather.3.cloned.1.call-start = ((), (), s32[]{:S(2)}) async-start(), calls=%async_computation.1 | async-start | bytes 5857280 | tf_op jit(solution)/shard_map/all_gather | solution.py:264
  79.9 2.5 %copy-start.5 = (s32[256,64]{0,1:T(8,128)S(1)}, s32[256,64]{0,1:T(8,128)}, u32[]{:S(2)}) copy-start(s32[256,64]{0,1:T(8,128)} %param.19) | copy-start | bytes 196612
  191.9 2.6 %collective-permute-start.4 = (bf16[256,704]{0,1:T(8,128)(2,1)S(1)}, bf16[256,704]{0,1:T(8,128)(2,1)S(1)}, u32[]{:S(2)}, u32[]{:S(2)}) collective-permute-start(bf16[256,704]{0,1:T(8,128)(2,1)S(1)} %bitcast.127), channel_id=1, source_target_pairs={{0,64},{64,0},{1,65},{65,1},{2,66},{66,2},{3,67},{67,3},{4,68},{68... | collective-permute-start | bytes 1081352 | tf_op jit(solution)/shard_map/ppermute | solution.py:146
Sparse Core Ops, SparseCore 0:
  82.6 67.6 all-gather.2

commit v7 on v6

--- a/solution.py
+++ b/solution.py
@@ -213,9 +213,6 @@
     own_heads = jnp.dot(own_select, attended, preferred_element_type=jnp.float32).astype(
         jnp.bfloat16
     )
-    decoder_out_full, received_heads = lax.optimization_barrier(
-        (in_head_order(first, decoder_out, decoder_out_other, 0), received_heads)
-    )
     own_rows = jnp.concatenate([own_heads, received_heads], 1)
     full_out = jnp.concatenate([vision_out, vision_out_other], 0)
     kept = (
@@ -270,6 +267,9 @@
     info = jnp.concatenate(
         [doc_starts, jnp.full((1,), seq_index, jnp.int32), jnp.zeros((3,), jnp.int32)]
     )
+    decoder_out_full, head_queries = lax.optimization_barrier(
+        (in_head_order(first, decoder_out, decoder_out_other, 0), head_queries)
+    )
     head_major = text_attention(info, head_queries, piece, rows, scale)
     attended_text = jnp.transpose(head_major, (1, 0, 2)).reshape(text_rows, -1)
     all_heads = in_head_order(first, attended_text, swap(attended_text), 1)

time: 206 us -> 193 us (0.937)
  waiting for transfers between devices: 72.7 us -> 64.7 us
  matrix products: 33 us -> 28.2 us
  local copies, waits for them, and re-layouts: 19 us -> 16.6 us
    all_gather x1, waiting for transfers between devices: 60.9 us -> 49.5 us  [body(): piece = lax.all_gather(shared, 'seq', axis=0, tiled=True)]
    ppermute x5, waiting for transfers between devices: 1.31 us -> 4.52 us  [swap(): return lax.ppermute(values, 'section', [(0, 1), (1, 0)])]
    unnamed x20 -> x14, local copies, waits for them, and re-layouts: 2.28 us -> 0.04 us
    select_n x1, other arithmetic: 8.39 us -> 6.23 us  [in_head_order(): jnp.where(first, jnp.concatenate([own, other], axis), jnp.concatenate([ot...]
    dot_general x1, matrix products: 3.87 us -> 1.76 us  [body(): jnp.einsum('hqk,khd->qhd', weights.astype(jnp.bfloat16), values, preferre...]
  transfers between devices with their start and end apart: 7 -> 7, of which waited for: 3 -> 4; matrix products, arithmetic and copies ran while one was open for 19% -> 17% of each run, Pallas kernels for 0% -> 0%
where the time goes in v7:
time: 193 us; the launch traced here: 192 us
  waiting for transfers between devices  64.7 us (34%)
  Pallas kernels  31.6 us (16%)
  matrix products  28.2 us (15%)
  other arithmetic  18.7 us (10%)
  local copies, waits for them, and re-layouts  16.6 us (9%)
  starting transfers between devices  16.6 us (9%)
  between operations  15.7 us (8%)
    all_gather x1, waiting for transfers between devices, body(): piece = lax.all_gather(shared, 'seq', axis=0, tiled=True)  49.5 us
    pallas_call x1, Pallas kernels, text_attention(): pl.pallas_call(functools.partial(_text_kernel, scale=scale), grid_spec=pl...  31.6 us
    all_to_all x1, starting transfers between devices, body(): lax.all_to_all(jnp.roll(image_rows.reshape(per_peer, seq_count, image_row...  11.2 us
    all_to_all x1, waiting for transfers between devices, body(): lax.all_to_all(jnp.roll(image_rows.reshape(per_peer, seq_count, image_row...  10.6 us
    all_gather x1, local copies, waits for them, and re-layouts, body(): piece = lax.all_gather(shared, 'seq', axis=0, tiled=True)  9.83 us
    select_n x1, other arithmetic, in_head_order(): jnp.where(first, jnp.concatenate([own, other], axis), jnp.concatenate([ot...  6.23 us
    dot_general x1, matrix products, body(): jnp.dot(normed, vision_qkv.reshape(D, -1), preferred_element_type=jnp.flo...  5.99 us
    ppermute x5, starting transfers between devices, swap(): return lax.ppermute(values, 'section', [(0, 1), (1, 0)])  5.28 us
  transfers between devices with their start and end apart: 7, of which 4 were waited for; matrix products, arithmetic and copies ran while one was open for 17% of the time, Pallas kernels for 0%

profile of v7, /device:TPU:1, one launch (start us, length us, event | category | flops | bytes accessed | tf_op | source)
XLA Modules:
  0.0 192.0 jit_solution(5507231437707126965)
XLA Ops:
  6.5 1.4 collective-permute-start.1
  8.0 0.7 slice_bitcast_fusion.2
  8.6 0.8 fusion.69
  9.6 0.1 broadcast_add_fusion.1
  9.8 0.1 copy.45
  9.9 0.1 eq.86
  10.0 1.6 convert_reduce_fusion
  11.7 0.5 fusion.13
  12.2 6.0 %fusion.29 = f32[512,3,8,88]{0,3,2,1:T(8,128)S(1)} fusion(bf16[3,8,88,1408]{3,2,1,0:T(8,128)(2,1)} %bitcast.130, bf16[512,1408]{1,0:T(8,128)(2,1)S(1)} %copy-done.2, f32[512]{0:T(512)S(1)} %add_rsqrt_fusion.3, f32[512]{0:T(512)S(1)} %broadcast_multiply_fusion), kind=kOutput, calls=%fused_computation.30 | convolution fusion | flops 3047948288 | bytes 11718656 | tf_op jit(solution)/shard_map/dot_general | solution.py:182
  18.2 0.4 multiply_reduce_fusion.1
  18.6 0.2 broadcast_compare_fusion
  18.9 2.5 %fusion = (f32[8,512]{1,0:T(8,128)S(1)}, f32[8,512,512]{1,2,0:T(8,128)S(1)}) fusion(pred[512,512]{0,1:T(8,128)(4,1)S(1)} %broadcast_compare_fusion, f32[512,3,8,88]{0,3,2,1:T(8,128)S(1)} %fusion.29, f32[512,8]{0,1:T(8,128)S(1)} %get-tuple-element.27, f32[512,8]{0,1:T(8,128)S(1)} %get-tuple-element.28), kind=kOutput, calls=%fused_computation.2 | convolution fusion | flops 376827904 | bytes 11583488 | tf_op jit(solution)/shard_map/qhd,khd->hqk/dot_general | solution.py:192
  21.4 1.8 divide_convert_fusion
  23.2 1.2 convolution_convert_fusion
  24.4 0.2 collective-permute-start
  24.7 0.1 eq.79
  24.8 1.7 convolution_convert_fusion.1
  26.6 0.6 fusion.53
  27.2 3.1 %fusion.19 = bf16[256,1408]{1,0:T(8,128)(2,1)S(1)} fusion(f32[256,1408]{1,0:T(8,128)S(1)} %fusion.53, bf16[704,1408]{1,0:T(8,128)(2,1)} %collective-permute-done.1, bf16[704,1408]{1,0:T(8,128)(2,1)S(1)} %copy-done.5, bf16[256,704]{0,1:T(8,128)(2,1)} %collective-permute-done, bf16[256,704]{0,1:T(8,128)(2,1)S(1)} %convolution_convert_fusion.1), kind=kOutput, calls=%fused_computation.22 | convolution fusion | flops 1025114112 | bytes 6848512 | tf_op jit(solution)/shard_map/dot_general | solution.py:220
  30.3 0.2 reshape.479
  30.6 4.5 %fusion.76 = f32[128,1408]{1,0:T(8,128)S(1)} fusion(bf16[128,2816]{1,0:T(8,128)(2,1)S(1)} %reshape.479, bf16[2816,1408]{1,0:T(8,128)(2,1)} %bitcast.121), kind=kOutput, calls=%fused_computation.149 | convolution fusion | flops 1015021568 | bytes 9371648 | tf_op jit(solution)/shard_map/dot_general | solution.py:222
  35.1 0.6 collective-permute-start.2
  35.8 0.5 constant_dynamic-slice_fusion
  38.3 1.2 add_convert_fusion
  39.5 0.4 copy.46
  39.9 1.7 fusion.55
  41.6 11.2 %all-to-all-start = ((bf16[2,64,1408]{2,0,1:T(2,128)(2,1)}), bf16[2,64,1408]{2,0,1:T(2,128)(2,1)S(1)}, u32[]{:S(2)}, u32[]{:S(2)}) async-start(bf16[2,64,1408]{2,0,1:T(2,128)(2,1)} %fusion.55), calls=%async_computation | async-start | bytes 720896 | tf_op jit(solution)/shard_map/all_to_all | solution.py:232
  53.0 10.6 %all-to-all-done = bf16[2,64,1408]{2,0,1:T(2,128)(2,1)S(1)} async-done(((bf16[2,64,1408]{2,0,1:T(2,128)(2,1)}), bf16[2,64,1408]{2,0,1:T(2,128)(2,1)S(1)}, u32[]{:S(2)}, u32[]{:S(2)}) %all-to-all-start) | async-done | bytes 360480 | tf_op jit(solution)/shard_map/all_to_all | solution.py:232
  63.7 1.6 scatter_fusion
  65.3 0.2 fusion.26
  65.5 1.5 fusion.48
  67.1 0.7 pad_maximum_fusion
  67.8 1.8 collective-permute-start.3
  69.6 0.2 convert_reduce_fusion.1
  69.7 0.6 pad_add_fusion.1.info_ref
  70.3 3.2 %collective-permute-done.3 = bf16[704,1408]{1,0:T(8,128)(2,1)} collective-permute-done((bf16[704,1408]{1,0:T(8,128)(2,1)}, bf16[704,1408]{1,0:T(8,128)(2,1)}, u32[]{:S(2)}, u32[]{:S(2)}) %collective-permute-start.3) | collective-permute-done | bytes 1982496 | tf_op jit(solution)/shard_map/ppermute | solution.py:146
  73.5 6.2 %maximum_select_fusion = bf16[1408,1408]{1,0:T(8,128)(2,1)} fusion(bf16[704,1408]{1,0:T(8,128)(2,1)} %collective-permute-done.3, bf16[704,1408]{1,0:T(8,128)(2,1)} %param.25, pred[]{:T(512)S(6)} %eq.90), kind=kLoop, calls=%fused_computation.12 | loop fusion | flops 17842176 | bytes 7929857 | tf_op jit(solution)/shard_map/jit(_where)/select_n | solution.py:150
  79.8 0.8 fusion.57
  80.6 1.3 copy.49
  81.9 1.6 fusion.33
  83.5 2.4 %fusion.34.q_ref = bf16[8,256,88]{2,1,0:T(8,128)(2,1)} fusion(f32[256,8,88]{2,0,1:T(8,128)} %copy.49, f32[8,256]{1,0:T(8,128)S(1)} %add_rsqrt_fusion.2), kind=kLoop, calls=%fused_computation.46 | loop fusion | flops 360448 | bytes 1089536 | tf_op jit(solution)/shard_map/convert_element_type | solution.py:253
  85.9 49.5 %all-gather.3.cloned.1.call-done = bf16[128,256,88]{1,2,0:T(8,128)(2,1)} async-done(((bf16[2,256,88]{1,2,0:T(8,128)(2,1)}), bf16[128,256,88]{1,2,0:T(8,128)(2,1)}) %all-gather.3.cloned.1.call-update) | async-done | bytes 5767184 | tf_op jit(solution)/shard_map/all_gather | solution.py:261
  135.4 9.8 %copy.50 = bf16[128,256,88]{2,1,0:T(8,128)(2,1)} copy(bf16[128,256,88]{1,2,0:T(8,128)(2,1)} %all-gather.3.cloned.1.call-done) | data formatting | bytes 11534336 | tf_op jit(solution)/shard_map/all_gather | solution.py:261
  145.2 31.6 %shard_map.136 = bf16[8,256,88]{2,1,0:T(8,128)(2,1)} custom-call(s32[36]{0:T(128)} %constant.137.clone.query_block_ref, s32[36]{0:T(128)} %constant.138.clone.key_block_ref, s32[8]{0:T(128)} %pad_add_fusion.1.info_ref, bf16[8,256,88]{2,1,0:T(8,128)(2,1)} %fusion.34.q_ref, bf16[64,2,256,88]{3,2,1,0:T(8,128)(2,1)} %bitcast.120), custom_call_target="tpu_custom_call" | custom-call | tf_op jit(solution)/shard_map/pallas_call | solution.py:125
  176.9 1.2 copy.51
  178.1 1.3 collective-permute-start.4
  179.4 1.3 collective-permute-done.4
  180.7 4.4 %fusion.22 = bf16[256,1,1408]{2,0,1:T(8,128)(2,1)} fusion(bf16[1408,1408]{1,0:T(8,128)(2,1)} %maximum_select_fusion, bf16[256,1408]{1,0:T(8,128)(2,1)S(1)} %scatter_fusion, bf16[256,704]{0,1:T(8,128)(2,1)S(1)} %collective-permute-done.4, bf16[256,704]{0,1:T(8,128)(2,1)S(1)} %bitcast.128, pred[]{:T(512)S(6)} %eq.90), kind=kOutput, calls=%fused_computation.23 | convolution fusion | flops 1019346944 | bytes 6127617 | tf_op jit(solution)/shard_map/dot_general | solution.py:276
  (42 shorter events, 0.8 us)
Async XLA Ops:
  6.5 73.2 %copy-start = (bf16[1408,704]{0,1:T(8,128)(2,1)S(1)}, bf16[1408,704]{0,1:T(8,128)(2,1)}, u32[]{:S(2)}) copy-start(bf16[1408,704]{0,1:T(8,128)(2,1)} %param.23) | copy-start | bytes 5947396
  6.5 5.1 %copy-start.2 = (bf16[512,1408]{1,0:T(8,128)(2,1)S(1)}, bf16[512,1408]{1,0:T(8,128)(2,1)}, u32[]{:S(2)}) copy-start(bf16[512,1408]{1,0:T(8,128)(2,1)} %param.14) | copy-start | bytes 4325380
  6.5 20.7 %collective-permute-start.1 = (bf16[704,1408]{1,0:T(8,128)(2,1)}, bf16[704,1408]{1,0:T(8,128)(2,1)}, u32[]{:S(2)}, u32[]{:S(2)}) collective-permute-start(bf16[704,1408]{1,0:T(8,128)(2,1)} %param.21), channel_id=1, source_target_pairs={{0,64},{64,0},{1,65},{65,1},{2,66},{66,2},{3,67},{67,3},{4,68},{68... | collective-permute-start | bytes 5947400 | tf_op jit(solution)/shard_map/ppermute | solution.py:146
  23.2 1.4 copy-start.6
  24.4 2.8 %collective-permute-start = (bf16[256,704]{0,1:T(8,128)(2,1)}, bf16[256,704]{0,1:T(8,128)(2,1)}, u32[]{:S(2)}, u32[]{:S(2)}) collective-permute-start(bf16[256,704]{0,1:T(8,128)(2,1)} %convolution_convert_fusion), channel_id=1, source_target_pairs={{0,64},{64,0},{1,65},{65,1},{2,66},{66,2},{3,67},{67,3},{4,68},{68... | collective-permute-start | bytes 1081352 | tf_op jit(solution)/shard_map/ppermute | solution.py:146
  24.8 2.4 %copy-start.5 = (bf16[704,1408]{1,0:T(8,128)(2,1)S(1)}, bf16[704,1408]{1,0:T(8,128)(2,1)}, u32[]{:S(2)}) copy-start(bf16[704,1408]{1,0:T(8,128)(2,1)} %param.21) | copy-start | bytes 5947396
  30.5 5.2 %copy-start.4 = (s32[8192]{0:T(1024)S(1)}, s32[8192]{0:T(1024)}, u32[]{:S(2)}) copy-start(s32[8192]{0:T(1024)} %param.17) | copy-start | bytes 98308
  35.1 28.6 %copy-start.1 = (bf16[256,1,1408]{2,0,1:T(8,128)(2,1)S(1)}, bf16[256,1,1408]{2,0,1:T(8,128)(2,1)}, u32[]{:S(2)}) copy-start(bf16[256,1,1408]{2,0,1:T(8,128)(2,1)} %param.18) | copy-start | bytes 2162692
  35.1 3.2 %collective-permute-start.2 = (f32[128,1408]{1,0:T(8,128)S(1)}, f32[128,1408]{1,0:T(8,128)}, u32[]{:S(2)}, u32[]{:S(2)}) collective-permute-start(f32[128,1408]{1,0:T(8,128)S(1)} %fusion.76), channel_id=1, source_target_pairs={{0,64},{64,0},{1,65},{65,1},{2,66},{66,2},{3,67},{67,3},{4,68},{68... | collective-permute-start | bytes 2162696 | tf_op jit(solution)/shard_map/ppermute | solution.py:146
  41.6 22.1 %all-to-all-start = ((bf16[2,64,1408]{2,0,1:T(2,128)(2,1)}), bf16[2,64,1408]{2,0,1:T(2,128)(2,1)S(1)}, u32[]{:S(2)}, u32[]{:S(2)}) async-start(bf16[2,64,1408]{2,0,1:T(2,128)(2,1)} %fusion.55), calls=%async_computation | async-start | bytes 720896 | tf_op jit(solution)/shard_map/all_to_all | solution.py:232
  52.8 82.6 %all-gather.3.cloned.1.call-start = ((), (), s32[]{:S(2)}) async-start(), calls=%async_computation.1 | async-start | bytes 5857280 | tf_op jit(solution)/shard_map/all_gather | solution.py:261
  65.3 4.3 %copy-start.3 = (s32[256,64]{0,1:T(8,128)S(1)}, s32[256,64]{0,1:T(8,128)}, u32[]{:S(2)}) copy-start(s32[256,64]{0,1:T(8,128)} %param.19) | copy-start | bytes 196612
  67.8 5.7 %collective-permute-start.3 = (bf16[704,1408]{1,0:T(8,128)(2,1)}, bf16[704,1408]{1,0:T(8,128)(2,1)}, u32[]{:S(2)}, u32[]{:S(2)}) collective-permute-start(bf16[704,1408]{1,0:T(8,128)(2,1)} %param.25), channel_id=1, source_target_pairs={{0,64},{64,0},{1,65},{65,1},{2,66},{66,2},{3,67},{67,3},{4,68},{68... | collective-permute-start | bytes 5947400 | tf_op jit(solution)/shard_map/ppermute | solution.py:146
  178.1 2.6 %collective-permute-start.4 = (bf16[256,704]{0,1:T(8,128)(2,1)S(1)}, bf16[256,704]{0,1:T(8,128)(2,1)S(1)}, u32[]{:S(2)}, u32[]{:S(2)}) collective-permute-start(bf16[256,704]{0,1:T(8,128)(2,1)S(1)} %bitcast.127), channel_id=1, source_target_pairs={{0,64},{64,0},{1,65},{65,1},{2,66},{66,2},{3,67},{67,3},{4,68},{68... | collective-permute-start | bytes 1081352 | tf_op jit(solution)/shard_map/ppermute | solution.py:146
Sparse Core Ops, SparseCore 0:
  67.9 67.4 all-gather.2

commit v8 on v7

--- a/solution.py
+++ b/solution.py
@@ -56,7 +56,7 @@
     return _segment_start(info_ref, qb * span + info_ref[4]) // span
 
 
-def _text_kernel(query_block_ref, key_block_ref, info_ref, q_ref, kv_ref, o_ref, acc_ref, tot_ref, *, scale):
+def _text_kernel(query_block_ref, key_block_ref, info_ref, q_ref, kv_ref, o_ref, acc_ref, ext_ref, *, scale):
     step = pl.program_id(0)
     qb = query_block_ref[step]
     kb = key_block_ref[step]
@@ -68,15 +68,19 @@
     active = kb >= _first_block(info_ref, qb, span)
     unmasked = (kb < qb) & (kb * span >= _segment_start(info_ref, last_query))
 
+    @pl.when(step == 0)
+    def _():
+        lane = lax.broadcasted_iota(jnp.int32, ext_ref.shape, 1)
+        ext_ref[...] = jnp.where(lane == head, 1.0, 0.0).astype(ext_ref.dtype)
+
     @pl.when(kb == 0)
     def _():
         acc_ref[...] = jnp.zeros_like(acc_ref)
-        tot_ref[...] = jnp.zeros_like(tot_ref)
 
     def accumulate(masked):
         q = q_ref[...].reshape(heads * rows, head)
         k = kv_ref[:, 0].reshape(span, head)
-        v = kv_ref[:, 1].reshape(span, head)
+        ext_ref[:, :head] = kv_ref[:, 1].reshape(span, head)
         s = lax.dot_general(q, k, (((1,), (1,)), ((), ())), preferred_element_type=jnp.float32)
         w = jnp.exp(s * scale)
         if masked:
@@ -90,8 +94,9 @@
                 key_places >= _segment_start(info_ref, query_places)
             )
             w = jnp.where(allowed, w, 0.0)
-        tot_ref[...] += jnp.sum(w, -1, keepdims=True)
-        acc_ref[...] += jnp.dot(w.astype(jnp.bfloat16), v, preferred_element_type=jnp.float32)
+        acc_ref[...] += jnp.dot(
+            w.astype(jnp.bfloat16), ext_ref[...], preferred_element_type=jnp.float32
+        )
 
     @pl.when(active & unmasked)
     def _():
@@ -103,7 +108,10 @@
 
     @pl.when(kb == qb)
     def _():
-        o_ref[...] = (acc_ref[...] / tot_ref[...]).astype(o_ref.dtype).reshape(o_ref.shape)
+        acc = acc_ref[...]
+        o_ref[...] = (acc[:, :head] / acc[:, head : head + 1]).astype(o_ref.dtype).reshape(
+            o_ref.shape
+        )
 
 
 def text_attention(info, q, kv, rows, scale):
@@ -133,8 +141,8 @@
             ],
             out_specs=pl.BlockSpec((heads, rows, head), q_block),
             scratch_shapes=[
-                pltpu.VMEM((heads * rows, head), jnp.float32),
-                pltpu.VMEM((heads * rows, 1), jnp.float32),
+                pltpu.VMEM((heads * rows, 128), jnp.float32),
+                pltpu.VMEM((span, 128), jnp.bfloat16),
             ],
         ),
         out_shape=jax.ShapeDtypeStruct((heads, text_rows, head), jnp.bfloat16),

time: 193 us -> 195 us (1.010)
  no operation moved by 1% of the time
where the time goes in v8:
time: 195 us; the launch traced here: 192 us
  waiting for transfers between devices  64.7 us (33%)
  Pallas kernels  32 us (16%)
  matrix products  28.2 us (14%)
  other arithmetic  18.7 us (10%)
  local copies, waits for them, and re-layouts  16.6 us (9%)
  starting transfers between devices  16.6 us (9%)
  between operations  15.7 us (8%)
    all_gather x1, waiting for transfers between devices, body(): piece = lax.all_gather(shared, 'seq', axis=0, tiled=True)  49.5 us
    pallas_call x1, Pallas kernels, text_attention(): pl.pallas_call(functools.partial(_text_kernel, scale=scale), grid_spec=pl...  32 us
    all_to_all x1, starting transfers between devices, body(): lax.all_to_all(jnp.roll(image_rows.reshape(per_peer, seq_count, image_row...  11.2 us
    all_to_all x1, waiting for transfers between devices, body(): lax.all_to_all(jnp.roll(image_rows.reshape(per_peer, seq_count, image_row...  10.6 us
    all_gather x1, local copies, waits for them, and re-layouts, body(): piece = lax.all_gather(shared, 'seq', axis=0, tiled=True)  9.83 us
    select_n x1, other arithmetic, in_head_order(): jnp.where(first, jnp.concatenate([own, other], axis), jnp.concatenate([ot...  6.23 us
    dot_general x1, matrix products, body(): jnp.dot(normed, vision_qkv.reshape(D, -1), preferred_element_type=jnp.flo...  5.99 us
    ppermute x5, starting transfers between devices, swap(): return lax.ppermute(values, 'section', [(0, 1), (1, 0)])  5.29 us
  transfers between devices with their start and end apart: 7, of which 4 were waited for; matrix products, arithmetic and copies ran while one was open for 17% of the time, Pallas kernels for 0%

profile of v8, /device:TPU:1, one launch (start us, length us, event | category | flops | bytes accessed | tf_op | source)
XLA Modules:
  0.0 192.3 jit_solution(10485986380540386003)
XLA Ops:
  6.5 1.4 collective-permute-start.1
  8.0 0.7 slice_bitcast_fusion.2
  8.6 0.8 fusion.69
  9.6 0.1 broadcast_add_fusion.1
  9.8 0.1 copy.45
  9.9 0.1 eq.86
  10.0 1.6 convert_reduce_fusion
  11.7 0.5 fusion.13
  12.2 6.0 %fusion.29 = f32[512,3,8,88]{0,3,2,1:T(8,128)S(1)} fusion(bf16[3,8,88,1408]{3,2,1,0:T(8,128)(2,1)} %bitcast.130, bf16[512,1408]{1,0:T(8,128)(2,1)S(1)} %copy-done.2, f32[512]{0:T(512)S(1)} %add_rsqrt_fusion.3, f32[512]{0:T(512)S(1)} %broadcast_multiply_fusion), kind=kOutput, calls=%fused_computation.30 | convolution fusion | flops 3047948288 | bytes 11718656 | tf_op jit(solution)/shard_map/dot_general | solution.py:190
  18.2 0.4 multiply_reduce_fusion.1
  18.6 0.2 broadcast_compare_fusion
  18.9 2.5 %fusion = (f32[8,512]{1,0:T(8,128)S(1)}, f32[8,512,512]{1,2,0:T(8,128)S(1)}) fusion(pred[512,512]{0,1:T(8,128)(4,1)S(1)} %broadcast_compare_fusion, f32[512,3,8,88]{0,3,2,1:T(8,128)S(1)} %fusion.29, f32[512,8]{0,1:T(8,128)S(1)} %get-tuple-element.27, f32[512,8]{0,1:T(8,128)S(1)} %get-tuple-element.28), kind=kOutput, calls=%fused_computation.2 | convolution fusion | flops 376827904 | bytes 11583488 | tf_op jit(solution)/shard_map/qhd,khd->hqk/dot_general | solution.py:200
  21.4 1.8 divide_convert_fusion
  23.2 1.2 convolution_convert_fusion
  24.4 0.2 collective-permute-start
  24.7 0.1 eq.79
  24.8 1.7 convolution_convert_fusion.1
  26.6 0.6 fusion.53
  27.2 3.1 %fusion.19 = bf16[256,1408]{1,0:T(8,128)(2,1)S(1)} fusion(f32[256,1408]{1,0:T(8,128)S(1)} %fusion.53, bf16[704,1408]{1,0:T(8,128)(2,1)} %collective-permute-done.1, bf16[704,1408]{1,0:T(8,128)(2,1)S(1)} %copy-done.5, bf16[256,704]{0,1:T(8,128)(2,1)} %collective-permute-done, bf16[256,704]{0,1:T(8,128)(2,1)S(1)} %convolution_convert_fusion.1), kind=kOutput, calls=%fused_computation.22 | convolution fusion | flops 1025114112 | bytes 6848512 | tf_op jit(solution)/shard_map/dot_general | solution.py:228
  30.3 0.2 reshape.479
  30.6 4.5 %fusion.76 = f32[128,1408]{1,0:T(8,128)S(1)} fusion(bf16[128,2816]{1,0:T(8,128)(2,1)S(1)} %reshape.479, bf16[2816,1408]{1,0:T(8,128)(2,1)} %bitcast.121), kind=kOutput, calls=%fused_computation.149 | convolution fusion | flops 1015021568 | bytes 9371648 | tf_op jit(solution)/shard_map/dot_general | solution.py:230
  35.1 0.6 collective-permute-start.2
  35.8 0.5 constant_dynamic-slice_fusion
  38.3 1.2 add_convert_fusion
  39.5 0.4 copy.46
  39.9 1.7 fusion.55
  41.6 11.2 %all-to-all-start = ((bf16[2,64,1408]{2,0,1:T(2,128)(2,1)}), bf16[2,64,1408]{2,0,1:T(2,128)(2,1)S(1)}, u32[]{:S(2)}, u32[]{:S(2)}) async-start(bf16[2,64,1408]{2,0,1:T(2,128)(2,1)} %fusion.55), calls=%async_computation | async-start | bytes 720896 | tf_op jit(solution)/shard_map/all_to_all | solution.py:240
  53.0 10.6 %all-to-all-done = bf16[2,64,1408]{2,0,1:T(2,128)(2,1)S(1)} async-done(((bf16[2,64,1408]{2,0,1:T(2,128)(2,1)}), bf16[2,64,1408]{2,0,1:T(2,128)(2,1)S(1)}, u32[]{:S(2)}, u32[]{:S(2)}) %all-to-all-start) | async-done | bytes 360480 | tf_op jit(solution)/shard_map/all_to_all | solution.py:240
  63.7 1.6 scatter_fusion
  65.3 0.2 fusion.26
  65.5 1.5 fusion.48
  67.1 0.7 pad_maximum_fusion
  67.8 1.8 collective-permute-start.3
  69.6 0.2 convert_reduce_fusion.1
  69.7 0.6 pad_add_fusion.1.info_ref
  70.3 3.2 %collective-permute-done.3 = bf16[704,1408]{1,0:T(8,128)(2,1)} collective-permute-done((bf16[704,1408]{1,0:T(8,128)(2,1)}, bf16[704,1408]{1,0:T(8,128)(2,1)}, u32[]{:S(2)}, u32[]{:S(2)}) %collective-permute-start.3) | collective-permute-done | bytes 1982496 | tf_op jit(solution)/shard_map/ppermute | solution.py:154
  73.5 6.2 %maximum_select_fusion = bf16[1408,1408]{1,0:T(8,128)(2,1)} fusion(bf16[704,1408]{1,0:T(8,128)(2,1)} %collective-permute-done.3, bf16[704,1408]{1,0:T(8,128)(2,1)} %param.25, pred[]{:T(512)S(6)} %eq.90), kind=kLoop, calls=%fused_computation.12 | loop fusion | flops 17842176 | bytes 7929857 | tf_op jit(solution)/shard_map/jit(_where)/select_n | solution.py:158
  79.8 0.8 fusion.57
  80.6 1.3 copy.49
  81.9 1.6 fusion.33
  83.5 2.4 %fusion.34.q_ref = bf16[8,256,88]{2,1,0:T(8,128)(2,1)} fusion(f32[256,8,88]{2,0,1:T(8,128)} %copy.49, f32[8,256]{1,0:T(8,128)S(1)} %add_rsqrt_fusion.2), kind=kLoop, calls=%fused_computation.46 | loop fusion | flops 360448 | bytes 1089536 | tf_op jit(solution)/shard_map/convert_element_type | solution.py:261
  85.9 49.5 %all-gather.3.cloned.1.call-done = bf16[128,256,88]{1,2,0:T(8,128)(2,1)} async-done(((bf16[2,256,88]{1,2,0:T(8,128)(2,1)}), bf16[128,256,88]{1,2,0:T(8,128)(2,1)}) %all-gather.3.cloned.1.call-update) | async-done | bytes 5767184 | tf_op jit(solution)/shard_map/all_gather | solution.py:269
  135.4 9.8 %copy.50 = bf16[128,256,88]{2,1,0:T(8,128)(2,1)} copy(bf16[128,256,88]{1,2,0:T(8,128)(2,1)} %all-gather.3.cloned.1.call-done) | data formatting | bytes 11534336 | tf_op jit(solution)/shard_map/all_gather | solution.py:269
  145.2 32.0 %shard_map.136 = bf16[8,256,88]{2,1,0:T(8,128)(2,1)} custom-call(s32[36]{0:T(128)} %constant.137.clone.query_block_ref, s32[36]{0:T(128)} %constant.138.clone.key_block_ref, s32[8]{0:T(128)} %pad_add_fusion.1.info_ref, bf16[8,256,88]{2,1,0:T(8,128)(2,1)} %fusion.34.q_ref, bf16[64,2,256,88]{3,2,1,0:T(8,128)(2,1)} %bitcast.120), custom_call_target="tpu_custom_call" | custom-call | tf_op jit(solution)/shard_map/pallas_call | solution.py:133
  177.2 1.2 copy.51
  178.4 1.3 collective-permute-start.4
  179.8 1.3 collective-permute-done.4
  181.1 4.4 %fusion.22 = bf16[256,1,1408]{2,0,1:T(8,128)(2,1)} fusion(bf16[1408,1408]{1,0:T(8,128)(2,1)} %maximum_select_fusion, bf16[256,1408]{1,0:T(8,128)(2,1)S(1)} %scatter_fusion, bf16[256,704]{0,1:T(8,128)(2,1)S(1)} %collective-permute-done.4, bf16[256,704]{0,1:T(8,128)(2,1)S(1)} %bitcast.128, pred[]{:T(512)S(6)} %eq.90), kind=kOutput, calls=%fused_computation.23 | convolution fusion | flops 1019346944 | bytes 6127617 | tf_op jit(solution)/shard_map/dot_general | solution.py:284
  (42 shorter events, 0.8 us)
Async XLA Ops:
  6.5 73.2 %copy-start = (bf16[1408,704]{0,1:T(8,128)(2,1)S(1)}, bf16[1408,704]{0,1:T(8,128)(2,1)}, u32[]{:S(2)}) copy-start(bf16[1408,704]{0,1:T(8,128)(2,1)} %param.23) | copy-start | bytes 5947396
  6.5 5.1 %copy-start.2 = (bf16[512,1408]{1,0:T(8,128)(2,1)S(1)}, bf16[512,1408]{1,0:T(8,128)(2,1)}, u32[]{:S(2)}) copy-start(bf16[512,1408]{1,0:T(8,128)(2,1)} %param.14) | copy-start | bytes 4325380
  6.5 20.7 %collective-permute-start.1 = (bf16[704,1408]{1,0:T(8,128)(2,1)}, bf16[704,1408]{1,0:T(8,128)(2,1)}, u32[]{:S(2)}, u32[]{:S(2)}) collective-permute-start(bf16[704,1408]{1,0:T(8,128)(2,1)} %param.21), channel_id=1, source_target_pairs={{0,64},{64,0},{1,65},{65,1},{2,66},{66,2},{3,67},{67,3},{4,68},{68... | collective-permute-start | bytes 5947400 | tf_op jit(solution)/shard_map/ppermute | solution.py:154
  23.2 1.4 copy-start.6
  24.4 2.8 %collective-permute-start = (bf16[256,704]{0,1:T(8,128)(2,1)}, bf16[256,704]{0,1:T(8,128)(2,1)}, u32[]{:S(2)}, u32[]{:S(2)}) collective-permute-start(bf16[256,704]{0,1:T(8,128)(2,1)} %convolution_convert_fusion), channel_id=1, source_target_pairs={{0,64},{64,0},{1,65},{65,1},{2,66},{66,2},{3,67},{67,3},{4,68},{68... | collective-permute-start | bytes 1081352 | tf_op jit(solution)/shard_map/ppermute | solution.py:154
  24.8 2.4 %copy-start.5 = (bf16[704,1408]{1,0:T(8,128)(2,1)S(1)}, bf16[704,1408]{1,0:T(8,128)(2,1)}, u32[]{:S(2)}) copy-start(bf16[704,1408]{1,0:T(8,128)(2,1)} %param.21) | copy-start | bytes 5947396
  30.5 5.2 %copy-start.4 = (s32[8192]{0:T(1024)S(1)}, s32[8192]{0:T(1024)}, u32[]{:S(2)}) copy-start(s32[8192]{0:T(1024)} %param.17) | copy-start | bytes 98308
  35.1 28.6 %copy-start.1 = (bf16[256,1,1408]{2,0,1:T(8,128)(2,1)S(1)}, bf16[256,1,1408]{2,0,1:T(8,128)(2,1)}, u32[]{:S(2)}) copy-start(bf16[256,1,1408]{2,0,1:T(8,128)(2,1)} %param.18) | copy-start | bytes 2162692
  35.1 3.2 %collective-permute-start.2 = (f32[128,1408]{1,0:T(8,128)S(1)}, f32[128,1408]{1,0:T(8,128)}, u32[]{:S(2)}, u32[]{:S(2)}) collective-permute-start(f32[128,1408]{1,0:T(8,128)S(1)} %fusion.76), channel_id=1, source_target_pairs={{0,64},{64,0},{1,65},{65,1},{2,66},{66,2},{3,67},{67,3},{4,68},{68... | collective-permute-start | bytes 2162696 | tf_op jit(solution)/shard_map/ppermute | solution.py:154
  41.6 22.1 %all-to-all-start = ((bf16[2,64,1408]{2,0,1:T(2,128)(2,1)}), bf16[2,64,1408]{2,0,1:T(2,128)(2,1)S(1)}, u32[]{:S(2)}, u32[]{:S(2)}) async-start(bf16[2,64,1408]{2,0,1:T(2,128)(2,1)} %fusion.55), calls=%async_computation | async-start | bytes 720896 | tf_op jit(solution)/shard_map/all_to_all | solution.py:240
  52.8 82.6 %all-gather.3.cloned.1.call-start = ((), (), s32[]{:S(2)}) async-start(), calls=%async_computation.1 | async-start | bytes 5857280 | tf_op jit(solution)/shard_map/all_gather | solution.py:269
  65.3 4.3 %copy-start.3 = (s32[256,64]{0,1:T(8,128)S(1)}, s32[256,64]{0,1:T(8,128)}, u32[]{:S(2)}) copy-start(s32[256,64]{0,1:T(8,128)} %param.19) | copy-start | bytes 196612
  67.8 5.7 %collective-permute-start.3 = (bf16[704,1408]{1,0:T(8,128)(2,1)}, bf16[704,1408]{1,0:T(8,128)(2,1)}, u32[]{:S(2)}, u32[]{:S(2)}) collective-permute-start(bf16[704,1408]{1,0:T(8,128)(2,1)} %param.25), channel_id=1, source_target_pairs={{0,64},{64,0},{1,65},{65,1},{2,66},{66,2},{3,67},{67,3},{4,68},{68... | collective-permute-start | bytes 5947400 | tf_op jit(solution)/shard_map/ppermute | solution.py:154
  178.4 2.6 %collective-permute-start.4 = (bf16[256,704]{0,1:T(8,128)(2,1)S(1)}, bf16[256,704]{0,1:T(8,128)(2,1)S(1)}, u32[]{:S(2)}, u32[]{:S(2)}) collective-permute-start(bf16[256,704]{0,1:T(8,128)(2,1)S(1)} %bitcast.127), channel_id=1, source_target_pairs={{0,64},{64,0},{1,65},{65,1},{2,66},{66,2},{3,67},{67,3},{4,68},{68... | collective-permute-start | bytes 1081352 | tf_op jit(solution)/shard_map/ppermute | solution.py:154
Sparse Core Ops, SparseCore 0:
  67.9 67.4 all-gather.2

commit v9 on v8

--- a/solution.py
+++ b/solution.py
@@ -52,23 +52,16 @@
     return start
 
 
-def _first_block(info_ref, qb, span):
-    return _segment_start(info_ref, qb * span + info_ref[4]) // span
-
-
-def _text_kernel(query_block_ref, key_block_ref, info_ref, q_ref, kv_ref, o_ref, acc_ref, ext_ref, *, scale):
-    step = pl.program_id(0)
-    qb = query_block_ref[step]
-    kb = key_block_ref[step]
+def _text_kernel(plan_ref, fetch_ref, info_ref, q_ref, kv_ref, kpos_ref, o_ref, acc_ref, ext_ref, *, scale, blocks):
+    qb = pl.program_id(0)
+    kb = pl.program_id(1)
     heads, rows, head = q_ref.shape
     shards = kv_ref.shape[0]
     span = rows * shards
     own = info_ref[4]
-    last_query = qb * span + own + (rows - 1) * shards
-    active = kb >= _first_block(info_ref, qb, span)
-    unmasked = (kb < qb) & (kb * span >= _segment_start(info_ref, last_query))
-
-    @pl.when(step == 0)
+    mode = plan_ref[qb * blocks + kb]
+
+    @pl.when((qb == 0) & (kb == 0))
     def _():
         lane = lax.broadcasted_iota(jnp.int32, ext_ref.shape, 1)
         ext_ref[...] = jnp.where(lane == head, 1.0, 0.0).astype(ext_ref.dtype)
@@ -86,10 +79,7 @@
         if masked:
             row = lax.broadcasted_iota(jnp.int32, (heads * rows, 1), 0) & (rows - 1)
             query_places = (qb * rows + row) * shards + own
-            lane = lax.broadcasted_iota(jnp.int32, (1, span), 1)
-            key_places = (kb * rows + (lane & (rows - 1))) * shards + lax.shift_right_logical(
-                lane, rows.bit_length() - 1
-            )
+            key_places = kpos_ref[0]
             allowed = (key_places <= query_places) & (
                 key_places >= _segment_start(info_ref, query_places)
             )
@@ -98,15 +88,15 @@
             w.astype(jnp.bfloat16), ext_ref[...], preferred_element_type=jnp.float32
         )
 
-    @pl.when(active & unmasked)
+    @pl.when(mode == 1)
     def _():
         accumulate(False)
 
-    @pl.when(active & jnp.logical_not(unmasked))
+    @pl.when(mode == 2)
     def _():
         accumulate(True)
 
-    @pl.when(kb == qb)
+    @pl.when(kb == blocks - 1)
     def _():
         acc = acc_ref[...]
         o_ref[...] = (acc[:, :head] / acc[:, head : head + 1]).astype(o_ref.dtype).reshape(
@@ -114,30 +104,55 @@
         )
 
 
-def text_attention(info, q, kv, rows, scale):
+def text_attention(info, q, kv, key_places, rows, scale):
     heads, text_rows, head = q.shape
     shards = kv.shape[0]
     blocks = text_rows // rows
     span = rows * shards
-    pairs = [(i, j) for i in range(blocks) for j in range(i + 1)]
-    query_block = jnp.array([i for i, _ in pairs], jnp.int32)
-    key_block = jnp.array([j for _, j in pairs], jnp.int32)
-
-    def q_block(t, qb_ref, kb_ref, info_ref):
-        return (0, qb_ref[t], 0)
-
-    def kv_block(t, qb_ref, kb_ref, info_ref):
-        qb = qb_ref[t]
-        return (0, 0, jnp.maximum(kb_ref[t], _first_block(info_ref, qb, span)), 0)
+    block_places = jnp.transpose(key_places.reshape(shards, blocks, rows), (1, 0, 2)).reshape(
+        blocks, 1, span
+    )
+    lowest = jnp.min(block_places, (1, 2))
+    highest = jnp.max(block_places, (1, 2))
+    first_query = jnp.arange(blocks, dtype=jnp.int32) * span + info[4]
+    last_query = first_query + (rows - 1) * shards
+
+    def segment_start(places):
+        start = jnp.zeros_like(places) + info[0]
+        for doc in range(1, 4):
+            start = jnp.where(places >= info[doc], info[doc], start)
+        return start
+
+    active = (lowest[None, :] <= last_query[:, None]) & (
+        highest[None, :] >= segment_start(first_query)[:, None]
+    )
+    clear = (highest[None, :] <= first_query[:, None]) & (
+        lowest[None, :] >= segment_start(last_query)[:, None]
+    )
+    plan = jnp.where(active, jnp.where(clear, 1, 2), 0).astype(jnp.int32)
+    key_ids = jnp.broadcast_to(jnp.arange(blocks, dtype=jnp.int32)[None, :], (blocks, blocks))
+    seen = lax.cummax(jnp.where(active, key_ids, -1), axis=1)
+    first_active = jnp.argmax(active, axis=1).astype(jnp.int32)
+    fetch = jnp.where(seen < 0, first_active[:, None], seen).astype(jnp.int32)
+
+    def q_block(i, j, plan_ref, fetch_ref, info_ref):
+        return (0, i, 0)
+
+    def kv_block(i, j, plan_ref, fetch_ref, info_ref):
+        return (0, 0, fetch_ref[i * blocks + j], 0)
+
+    def kpos_block(i, j, plan_ref, fetch_ref, info_ref):
+        return (fetch_ref[i * blocks + j], 0, 0)
 
     return pl.pallas_call(
-        functools.partial(_text_kernel, scale=scale),
+        functools.partial(_text_kernel, scale=scale, blocks=blocks),
         grid_spec=pltpu.PrefetchScalarGridSpec(
             num_scalar_prefetch=3,
-            grid=(len(pairs),),
+            grid=(blocks, blocks),
             in_specs=[
                 pl.BlockSpec((heads, rows, head), q_block),
                 pl.BlockSpec((shards, 2, rows, head), kv_block),
+                pl.BlockSpec((1, 1, span), kpos_block),
             ],
             out_specs=pl.BlockSpec((heads, rows, head), q_block),
             scratch_shapes=[
@@ -146,8 +161,8 @@
             ],
         ),
         out_shape=jax.ShapeDtypeStruct((heads, text_rows, head), jnp.bfloat16),
-        compiler_params=pltpu.CompilerParams(dimension_semantics=("arbitrary",)),
-    )(query_block, key_block, info, q, kv)
+        compiler_params=pltpu.CompilerParams(dimension_semantics=("arbitrary", "arbitrary")),
+    )(plan.reshape(-1), fetch.reshape(-1), info, q, kv, block_places)
 
 
 def swap(values):
@@ -234,8 +249,47 @@
     )
     image_rows = (merge_terms + swap(merge_terms)).astype(jnp.bfloat16)
 
+    def key_value(rows_in):
+        normed_rows = root_norm(rows_in).astype(jnp.bfloat16)
+        paired = jnp.dot(
+            normed_rows, decoder_kv.reshape(D, -1), preferred_element_type=jnp.float32
+        ).reshape(rows_in.shape[0], 2, HEAD)
+        return jnp.stack(
+            [root_norm(paired[:, 0]).astype(jnp.bfloat16), paired[:, 1].astype(jnp.bfloat16)], 0
+        )
+
+    text_rows = text_embeds.shape[0]
+    run_starts = dest_positions.reshape(seq_count, merged_count)[:, 0]
+    places = (
+        jnp.arange(text_rows, dtype=jnp.int32)[:, None] * seq_count
+        + jnp.arange(seq_count, dtype=jnp.int32)[None, :]
+    )
+    is_text = jnp.logical_not(
+        jnp.any(
+            (places[..., None] >= run_starts) & (places[..., None] < run_starts + merged_count), -1
+        )
+    )
+    text_rank = jnp.cumsum(is_text.astype(jnp.int32), 0) - 1
+    slots = jnp.arange(merged_count, dtype=jnp.int32)
+    text_pick = (text_rank[None] == slots[:, None, None]) & is_text[None]
+    text_places = jnp.sum(jnp.where(text_pick, places[None], 0), 1).T
+    own_pick = lax.dynamic_slice_in_dim(text_pick, seq_index, 1, 2)[:, :, 0]
+    text_kv = jnp.einsum(
+        "ci,kid->kcd",
+        own_pick.astype(jnp.bfloat16),
+        key_value(text_embeds.reshape(text_rows, D)),
+        preferred_element_type=jnp.float32,
+    ).astype(jnp.bfloat16)
+    contribution = jnp.concatenate([text_kv, key_value(image_rows)], 1)[None]
+    piece = lax.all_gather(contribution, "seq", axis=0, tiled=True)
+    order = jnp.argsort(run_starts)
+    sorted_starts = run_starts[order]
+    all_kv = jnp.concatenate(
+        [piece[:, :, :merged_count], jnp.take(piece[:, :, merged_count:], order, axis=0)], 2
+    )
+    all_places = jnp.concatenate([text_places, sorted_starts[:, None] + slots[None, :]], 1)
+
     per_peer = merged_count // seq_count
-    run_starts = dest_positions.reshape(seq_count, merged_count)[:, 0]
     own_start = run_starts[seq_index]
     received = lax.all_to_all(
         jnp.roll(image_rows.reshape(per_peer, seq_count, image_rows.shape[1]), own_start, axis=1),
@@ -248,7 +302,6 @@
     landing = (
         run_starts[None, :] + slot_base + (seq_index - run_starts[None, :]) % seq_count
     ) // seq_count
-    text_rows = text_embeds.shape[0]
     prompt = text_embeds.reshape(text_rows, D).at[landing.reshape(-1)].set(received.reshape(-1, D))
     text_normed = root_norm(prompt).astype(jnp.bfloat16)
     head_queries = root_norm(
@@ -259,14 +312,6 @@
             preferred_element_type=jnp.float32,
         )
     ).astype(jnp.bfloat16)
-    paired = jnp.dot(
-        text_normed, decoder_kv.reshape(D, -1), preferred_element_type=jnp.float32
-    ).reshape(text_rows, 2, HEAD)
-    key_rows = root_norm(paired[:, 0]).astype(jnp.bfloat16)
-    value_rows = paired[:, 1].astype(jnp.bfloat16)
-
-    shared = jnp.stack([key_rows, value_rows], 0)[None]
-    piece = lax.all_gather(shared, "seq", axis=0, tiled=True)
     rows = 32
     doc_starts = jnp.sum(
         (segment_ids[None] < jnp.arange(4, dtype=jnp.int32)[:, None, None]).astype(jnp.int32),
@@ -278,7 +323,7 @@
     decoder_out_full, head_queries = lax.optimization_barrier(
         (in_head_order(first, decoder_out, decoder_out_other, 0), head_queries)
     )
-    head_major = text_attention(info, head_queries, piece, rows, scale)
+    head_major = text_attention(info, head_queries, all_kv, all_places, rows, scale)
     attended_text = jnp.transpose(head_major, (1, 0, 2)).reshape(text_rows, -1)
     all_heads = in_head_order(first, attended_text, swap(attended_text), 1)
     output_terms = jnp.dot(all_heads, decoder_out_full, preferred_element_type=jnp.float32)

time: 195 us -> 249 us (1.28)
  Pallas kernels: 32 us -> 66.3 us
  waiting for transfers between devices: 64.7 us -> 31.7 us
  other arithmetic: 18.7 us -> 50.3 us
  local copies, waits for them, and re-layouts: 16.6 us -> 35.8 us
  matrix products: 28.2 us -> 33.6 us
    pallas_call x1, Pallas kernels: 32 us -> 66.3 us  [text_attention(): pl.pallas_call(functools.partial(_text_kernel, scale=scale, blocks=blocks...]
    all_gather x1, waiting for transfers between devices: 49.5 us -> 25.8 us  [body(): piece = lax.all_gather(contribution, 'seq', axis=0, tiled=True)]
    concatenate x0 -> x2, other arithmetic: none -> 10.8 us  [the longest x1 10.2 us: body(): jnp.concatenate([piece[:, :, :merged_count], jnp.take(piece[:, :, merged_...]
    select_n x1 -> x4, other arithmetic: 0.01 us -> 7.75 us  [the longest x1 4.55 us: body(): jnp.take(piece[:, :, merged_count:], order, axis=0)]
    slice x0 -> x3, local copies, waits for them, and re-layouts: none -> 6.83 us  [the longest x1 6.04 us: body(): piece[:, :, :merged_count]]
    all_to_all x1, waiting for transfers between devices: 10.6 us -> 4.56 us  [body(): lax.all_to_all(jnp.roll(image_rows.reshape(per_peer, seq_count, image_row...]
    gather x0 -> x2, local copies, waits for them, and re-layouts: none -> 5.97 us  [the longest x1 5.19 us: body(): jnp.take(piece[:, :, merged_count:], order, axis=0)]
    ppermute x5, waiting for transfers between devices: 4.52 us -> 1.31 us  [swap(): return lax.ppermute(values, 'section', [(0, 1), (1, 0)])]
  transfers between devices with their start and end apart: 7 -> 7, of which waited for: 4 -> 3; matrix products, arithmetic and copies ran while one was open for 17% -> 17% of each run, Pallas kernels for 0% -> 0%
where the time goes in v9:
time: 249 us
  Pallas kernels  66.3 us (27%)
  other arithmetic  50.3 us (20%)
  local copies, waits for them, and re-layouts  35.8 us (14%)
  matrix products  33.6 us (13%)
  waiting for transfers between devices  31.7 us (13%)
  between operations  15.8 us (6%)
  starting transfers between devices  14.9 us (6%)
    pallas_call x1, Pallas kernels, text_attention(): pl.pallas_call(functools.partial(_text_kernel, scale=scale, blocks=blocks...  66.3 us
    all_gather x1, waiting for transfers between devices, body(): piece = lax.all_gather(contribution, 'seq', axis=0, tiled=True)  25.8 us
    all_to_all x1, starting transfers between devices, body(): lax.all_to_all(jnp.roll(image_rows.reshape(per_peer, seq_count, image_row...  11.2 us
    concatenate x1, other arithmetic, body(): jnp.concatenate([piece[:, :, :merged_count], jnp.take(piece[:, :, merged_...  10.2 us
    all_gather x1, local copies, waits for them, and re-layouts, body(): piece = lax.all_gather(contribution, 'seq', axis=0, tiled=True)  9.83 us
    dot_general x1, matrix products, body(): jnp.dot(normed, vision_qkv.reshape(D, -1), preferred_element_type=jnp.flo...  6.42 us
    select_n x1, other arithmetic, in_head_order(): jnp.where(first, jnp.concatenate([own, other], axis), jnp.concatenate([ot...  6.09 us
    slice x1, local copies, waits for them, and re-layouts, body(): piece[:, :, :merged_count]  6.04 us
  transfers between devices with their start and end apart: 7, of which 3 were waited for; matrix products, arithmetic and copies ran while one was open for 17% of the time, Pallas kernels for 0%

profile of v9, /device:TPU:1, one launch (start us, length us, event | category | flops | bytes accessed | tf_op | source)
XLA Modules:
  0.0 248.5 jit_solution(13099015979007539447)
XLA Ops:
  6.5 1.3 copy.83
  7.8 0.7 slice_bitcast_fusion.2
  8.5 0.8 fusion.87
  10.1 1.6 convert_reduce_fusion
  11.7 1.9 fusion.14
  13.6 6.4 %fusion.30 = f32[512,3,8,88]{0,3,2,1:T(8,128)S(1)} fusion(bf16[3,8,88,1408]{3,2,1,0:T(8,128)(2,1)} %bitcast.170, bf16[512,1408]{1,0:T(8,128)(2,1)} %param.12, f32[512]{0:T(512)S(1)} %add_rsqrt_fusion.3, f32[512]{0:T(512)S(1)} %broadcast_multiply_fusion), kind=kOutput, calls=%fused_computation.38 | convolution fusion | flops 3047948288 | bytes 11718656 | tf_op jit(solution)/shard_map/dot_general | solution.py:205
  20.5 2.6 %fusion.1 = (f32[8,512]{1,0:T(8,128)S(1)}, f32[8,512,512]{1,2,0:T(8,128)S(1)}) fusion(pred[512,512]{0,1:T(8,128)(4,1)S(1)} %broadcast_compare_fusion, f32[512,3,8,88]{0,3,2,1:T(8,128)S(1)} %fusion.30, f32[512,8]{0,1:T(8,128)S(1)} %get-tuple-element.53, f32[512,8]{0,1:T(8,128)S(1)} %get-tuple-element.54), kind=kOutput, calls=%fused_computation.8 | convolution fusion | flops 376827904 | bytes 11583488 | tf_op jit(solution)/shard_map/qhd,khd->hqk/dot_general | solution.py:215
  23.1 1.8 divide_convert_fusion
  24.8 1.2 convolution_convert_fusion
  26.1 1.4 collective-permute-start
  27.5 0.7 fusion.97
  28.2 2.0 sort.17
  31.4 2.1 and_reduce_fusion
  35.8 1.6 convolution_convert_fusion.1
  37.6 2.0 fusion.62
  39.7 4.5 %fusion.20 = bf16[256,1408]{1,0:T(8,128)(2,1)} fusion(f32[256,1408]{1,0:T(8,128)S(1)} %fusion.62, bf16[704,1408]{1,0:T(8,128)(2,1)} %collective-permute-done.1, bf16[704,1408]{1,0:T(8,128)(2,1)} %param.19, bf16[256,704]{0,1:T(8,128)(2,1)} %collective-permute-done, bf16[256,704]{0,1:T(8,128)(2,1)S(1)} %convolution_convert_fusion.1), kind=kOutput, calls=%fused_computation.30 | convolution fusion | flops 1025114112 | bytes 6848512 | tf_op jit(solution)/shard_map/dot_general | solution.py:243
  44.2 1.3 reshape.689
  45.5 5.4 %fusion.99 = f32[128,1408]{1,0:T(8,128)} fusion(bf16[128,2816]{1,0:T(8,128)(2,1)S(1)} %reshape.689, bf16[2816,1408]{1,0:T(8,128)(2,1)} %bitcast.159), kind=kOutput, calls=%fused_computation.215 | convolution fusion | flops 1015021568 | bytes 9371648 | tf_op jit(solution)/shard_map/dot_general | solution.py:245
  51.7 2.2 fusion
  53.8 1.0 fusion.34
  54.8 1.5 fusion.39
  56.3 1.4 fusion.63
  58.8 1.2 constant_dynamic-slice_fusion
  62.2 0.8 gather_fusion
  63.0 1.8 select_reduce_fusion
  66.0 2.5 %compare_select_fusion.8 = (s32[8]{0:T(128)S(1)}, s32[8]{0:T(128)S(1)}) fusion(s32[]{:T(128)} %bitcast.29, s32[]{:T(128)} %bitcast.28, s32[]{:T(128)} %bitcast.27, s32[]{:T(128)} %bitcast.26, s32[]{:T(128)} %axis_index.22), kind=kLoop, calls=%fused_computation.150 | loop fusion | flops 120 | bytes 84 | tf_op jit(solution)/shard_map/jit(_where)/select_n | solution.py:123
  68.9 0.7 iota_reduce_fusion
  70.6 0.8 reshape.735.kpos_ref
  73.6 1.7 fusion.66
  75.3 11.2 %all-to-all-start = ((bf16[2,64,1408]{2,0,1:T(2,128)(2,1)}), bf16[2,64,1408]{2,0,1:T(2,128)(2,1)S(1)}, u32[]{:S(2)}, u32[]{:S(2)}) async-start(bf16[2,64,1408]{2,0,1:T(2,128)(2,1)} %fusion.66), calls=%async_computation | async-start | bytes 720896 | tf_op jit(solution)/shard_map/all_to_all | solution.py:294
  86.5 6.1 %maximum_select_fusion = bf16[1408,1408]{1,0:T(8,128)(2,1)} fusion(bf16[704,1408]{1,0:T(8,128)(2,1)} %collective-permute-done.3, bf16[704,1408]{1,0:T(8,128)(2,1)} %param.23, pred[]{:T(512)S(6)} %eq.105), kind=kLoop, calls=%fused_computation.20 | loop fusion | flops 17842176 | bytes 7929857 | tf_op jit(solution)/shard_map/jit(_where)/select_n | solution.py:173
  92.6 4.6 %all-to-all-done = bf16[2,64,1408]{2,0,1:T(2,128)(2,1)S(1)} async-done(((bf16[2,64,1408]{2,0,1:T(2,128)(2,1)}), bf16[2,64,1408]{2,0,1:T(2,128)(2,1)S(1)}, u32[]{:S(2)}, u32[]{:S(2)}) %all-to-all-start) | async-done | bytes 360480 | tf_op jit(solution)/shard_map/all_to_all | solution.py:294
  97.2 1.8 scatter_fusion
  99.3 0.8 fusion.47
  100.1 1.3 copy.66
  101.4 1.6 fusion.35
  103.1 2.4 fusion.36.q_ref
  105.4 25.8 %all-gather.3.cloned.1.call-done = bf16[128,256,88]{1,2,0:T(8,128)(2,1)} async-done(((bf16[2,256,88]{1,2,0:T(8,128)(2,1)}), bf16[128,256,88]{1,2,0:T(8,128)(2,1)}) %all-gather.3.cloned.1.call-update) | async-done | bytes 5767184 | tf_op jit(solution)/shard_map/all_gather | solution.py:284
  131.2 9.8 %copy.67 = bf16[128,256,88]{2,1,0:T(8,128)(2,1)} copy(bf16[128,256,88]{1,2,0:T(8,128)(2,1)} %all-gather.3.cloned.1.call-done) | data formatting | bytes 11534336 | tf_op jit(solution)/shard_map/all_gather | solution.py:284
  141.1 6.0 %fusion.96 = (bf16[64,2,128,88]{3,2,1,0:T(8,128)(2,1)}, bf16[64,2,128,88]{3,2,1,0:T(8,128)(2,1)}) fusion(bf16[64,2,256,88]{3,2,1,0:T(8,128)(2,1)} %bitcast.158), kind=kLoop, calls=%fused_computation.212 | loop fusion | bytes 11534336 | tf_op jit(solution)/shard_map/slice | solution.py:288
  147.1 5.2 %gather_fusion.1 = bf16[64,2,128,88]{3,2,1,0:T(8,128)(2,1)} fusion(bf16[64,2,128,88]{3,2,1,0:T(8,128)(2,1)} %get-tuple-element.30, s32[1024]{0:T(1024)S(1)} %pad_clamp_fusion), kind=kCustom, calls=%fused_computation.1 | custom fusion | bytes 5767424 | tf_op jit(solution)/shard_map/jit(_take)/gather | solution.py:288
  152.3 4.5 %broadcast_select_fusion = bf16[64,2,128,88]{3,2,1,0:T(8,128)(2,1)} fusion(bf16[64,2,128,88]{3,2,1,0:T(8,128)(2,1)} %gather_fusion.1, pred[64]{0:T(512)(128)(4,1)S(1)} %compare_and_fusion.1), kind=kLoop, calls=%fused_computation.13 | loop fusion | flops 1441792 | bytes 5767232 | tf_op jit(solution)/shard_map/jit(_take)/select_n | solution.py:288
  156.9 10.2 %pad_maximum_fusion.kv_ref = bf16[64,2,256,88]{3,2,1,0:T(8,128)(2,1)} fusion(bf16[64,2,128,88]{3,2,1,0:T(8,128)(2,1)} %broadcast_select_fusion, bf16[64,2,128,88]{3,2,1,0:T(8,128)(2,1)} %get-tuple-element.29), kind=kLoop, calls=%fused_computation.3 | loop fusion | flops 11534336 | bytes 11534336 | tf_op jit(solution)/shard_map/concatenate | solution.py:287
  167.0 66.3 %shard_map.118 = bf16[8,256,88]{2,1,0:T(8,128)(2,1)} custom-call(s32[64]{0:T(128)} %select_n.288.plan_ref, s32[64]{0:T(128)} %compare_select_fusion.fetch_ref, s32[8]{0:T(128)} %pad_add_fusion.2.info_ref, bf16[8,256,88]{2,1,0:T(8,128)(2,1)} %fusion.36.q_ref, bf16[64,2,256,88]{3,2,1,0:T(8,128)(2,1)} %pad_maximum_fusion.kv_ref, s32[8,1,2048]{2,1,0:T(1,128)} %reshape.735.kpos_ref), custom_call_target="tpu_custom_call" | custom-call | tf_op jit(solution)/shard_map/pallas_call | solution.py:147
  233.4 1.2 copy.71
  234.6 1.3 collective-permute-start.4
  235.9 1.3 collective-permute-done.4
  237.3 4.4 %fusion.23 = bf16[256,1,1408]{2,0,1:T(8,128)(2,1)} fusion(bf16[1408,1408]{1,0:T(8,128)(2,1)} %maximum_select_fusion, bf16[256,1408]{1,0:T(8,128)(2,1)S(1)} %scatter_fusion, bf16[256,704]{0,1:T(8,128)(2,1)S(1)} %collective-permute-done.4, bf16[256,704]{0,1:T(8,128)(2,1)S(1)} %bitcast.166, pred[]{:T(512)S(6)} %eq.105), kind=kOutput, calls=%fused_computation.31 | convolution fusion | flops 1019346944 | bytes 6127617 | tf_op jit(solution)/shard_map/dot_general | solution.py:329
  (102 shorter events, 11.9 us)
Async XLA Ops:
  6.5 92.7 %copy-start = (bf16[1408,704]{0,1:T(8,128)(2,1)S(1)}, bf16[1408,704]{0,1:T(8,128)(2,1)}, u32[]{:S(2)}) copy-start(bf16[1408,704]{0,1:T(8,128)(2,1)} %param.21) | copy-start | bytes 5947396
  6.5 124.7 %all-gather.3.cloned.1.call-start = ((), (), s32[]{:S(2)}) async-start(), calls=%async_computation.1 | async-start | bytes 5857280 | tf_op jit(solution)/shard_map/all_gather | solution.py:284
  23.0 4.5 %copy-start.5 = (s32[8192]{0:T(1024)S(1)}, s32[8192]{0:T(1024)}, u32[]{:S(2)}) copy-start(s32[8192]{0:T(1024)} %param.15) | copy-start | bytes 98308
  23.0 11.6 %copy-start.3 = (bf16[1408,2,88]{0,2,1:T(8,128)(2,1)S(1)}, bf16[1408,2,88]{0,2,1:T(8,128)(2,1)}, u32[]{:S(2)}) copy-start(bf16[1408,2,88]{0,2,1:T(8,128)(2,1)} %param.22) | copy-start | bytes 1486852
  24.8 3.4 %copy-start.10 = (bf16[512,8,88]{0,2,1:T(8,128)(2,1)}, bf16[512,8,88]{0,2,1:T(8,128)(2,1)S(1)}, u32[]{:S(2)}) copy-start(bf16[512,8,88]{0,2,1:T(8,128)(2,1)S(1)} %divide_convert_fusion) | copy-start | bytes 2162692
  26.1 13.6 %collective-permute-start = (bf16[256,704]{0,1:T(8,128)(2,1)}, bf16[256,704]{0,1:T(8,128)(2,1)}, u32[]{:S(2)}, u32[]{:S(2)}) collective-permute-start(bf16[256,704]{0,1:T(8,128)(2,1)} %convolution_convert_fusion), channel_id=1, source_target_pairs={{0,64},{64,0},{1,65},{65,1},{2,66},{66,2},{3,67},{67,3},{4,68},{68... | collective-permute-start | bytes 1081352 | tf_op jit(solution)/shard_map/ppermute | solution.py:169
  27.5 12.2 %collective-permute-start.1 = (bf16[704,1408]{1,0:T(8,128)(2,1)}, bf16[704,1408]{1,0:T(8,128)(2,1)}, u32[]{:S(2)}, u32[]{:S(2)}) collective-permute-start(bf16[704,1408]{1,0:T(8,128)(2,1)} %param.19), channel_id=1, source_target_pairs={{0,64},{64,0},{1,65},{65,1},{2,66},{66,2},{3,67},{67,3},{4,68},{68... | collective-permute-start | bytes 5947400 | tf_op jit(solution)/shard_map/ppermute | solution.py:169
  30.2 3.5 %copy-start.9 = (s32[64]{0:T(128)}, s32[64]{0:T(128)S(1)}, u32[]{:S(2)}) copy-start(s32[64]{0:T(128)S(1)} %get-tuple-element.9) | copy-start | bytes 772
  30.8 0.6 copy-start.1
  37.6 2.0 copy-start.6
  45.5 6.0 %slice-start = ((s32[64,3]{0,1:T(4,128)}), s32[64,2]{0,1:T(2,128)S(1)}, s32[]{:S(2)}) async-start(s32[64,3]{0,1:T(4,128)} %copy-done.6), calls=%async_computation.2 | async-start | bytes 2048 | tf_op jit(solution)/shard_map/slice.1
  51.0 11.0 %copy-start.8 = (s32[64]{0:T(128)S(1)}, s32[64]{0:T(128)}, u32[]{:S(2)}) copy-start(s32[64]{0:T(128)} %get-tuple-element.45) | copy-start | bytes 772
  51.0 11.2 %copy-start.7 = (s32[64]{0:T(128)S(1)}, s32[64]{0:T(128)}, u32[]{:S(2)}) copy-start(s32[64]{0:T(128)} %get-tuple-element.48) | copy-start | bytes 772
  51.0 12.1 %copy-start.2 = (s32[256,64]{0,1:T(8,128)S(1)}, s32[256,64]{0,1:T(8,128)}, u32[]{:S(2)}) copy-start(s32[256,64]{0,1:T(8,128)} %copy-done.1) | copy-start | bytes 196612
  51.0 14.2 %copy-start.4 = (s32[256,64]{0,1:T(8,128)S(1)}, s32[256,64]{0,1:T(8,128)}, u32[]{:S(2)}) copy-start(s32[256,64]{0,1:T(8,128)} %param.17) | copy-start | bytes 196612
  51.0 3.8 %collective-permute-start.2 = (f32[128,1408]{1,0:T(8,128)}, f32[128,1408]{1,0:T(8,128)}, u32[]{:S(2)}, u32[]{:S(2)}) collective-permute-start(f32[128,1408]{1,0:T(8,128)} %fusion.99), channel_id=1, source_target_pairs={{0,64},{64,0},{1,65},{65,1},{2,66},{66,2},{3,67},{67,3},{4,68},{68... | collective-permute-start | bytes 2162696 | tf_op jit(solution)/shard_map/ppermute | solution.py:169
  58.5 28.0 %collective-permute-start.3 = (bf16[704,1408]{1,0:T(8,128)(2,1)}, bf16[704,1408]{1,0:T(8,128)(2,1)}, u32[]{:S(2)}, u32[]{:S(2)}) collective-permute-start(bf16[704,1408]{1,0:T(8,128)(2,1)} %param.23), channel_id=1, source_target_pairs={{0,64},{64,0},{1,65},{65,1},{2,66},{66,2},{3,67},{67,3},{4,68},{68... | collective-permute-start | bytes 5947400 | tf_op jit(solution)/shard_map/ppermute | solution.py:169
  75.3 21.9 %all-to-all-start = ((bf16[2,64,1408]{2,0,1:T(2,128)(2,1)}), bf16[2,64,1408]{2,0,1:T(2,128)(2,1)S(1)}, u32[]{:S(2)}, u32[]{:S(2)}) async-start(bf16[2,64,1408]{2,0,1:T(2,128)(2,1)} %fusion.66), calls=%async_computation | async-start | bytes 720896 | tf_op jit(solution)/shard_map/all_to_all | solution.py:294
  234.6 2.6 %collective-permute-start.4 = (bf16[256,704]{0,1:T(8,128)(2,1)S(1)}, bf16[256,704]{0,1:T(8,128)(2,1)S(1)}, u32[]{:S(2)}, u32[]{:S(2)}) collective-permute-start(bf16[256,704]{0,1:T(8,128)(2,1)S(1)} %bitcast.165), channel_id=1, source_target_pairs={{0,64},{64,0},{1,65},{65,1},{2,66},{66,2},{3,67},{67,3},{4,68},{68... | collective-permute-start | bytes 1081352 | tf_op jit(solution)/shard_map/ppermute | solution.py:169
Sparse Core Ops, SparseCore 0:
  58.6 72.5 all-gather.2
